TPU v7x, 256 devices: a whole 4x4x8 slice. The times are simulated.
256 devices in a mesh: prow: 8 (over x, core), pcol: 32 (over y, z).
Axes of the slice: x: 4, y: 4, z: 8, core: 2. Of those that a mesh axis runs over, the one named last changes fastest.
Arguments:
- factor: bfloat16 [16, 8, 4, 32, 256, 256], P(None, 'prow', None, 'pcol')
- right_side: bfloat16 [4, 32, 256, 256], P(None, 'pcol'), may hold values from -6 to 6
- node_blocks: int32 [15], replicated, may hold values from 1 to 32, as said below
- front_mask: int32 [15, 128], replicated, may hold values from 0 to 1, as said below
Outputs:
- solution: bfloat16 [4, 32, 256, 256], P(None, 'pcol')
Inputs may be any that keep to these rules, and one draw needn't show every extreme that they name: node_blocks[s] counts the blocks of node s of a complete binary elimination tree in heap order (the parent of s is (s - 1) // 2); the nodes of one depth together have 32 blocks. front_mask[s, i] is 1 only where block i belongs to a strict ancestor of node s.
All inputs are finite; a program needn't handle non-finite values.
Results may differ from a plain program's by a relative error of at most 0.024.
Values may be sent and summed in bfloat16 or wider, within the bound.
No kernel may reach another device: no remote copies, remote signals or barrier semaphores. Data moves between devices by JAX's collectives and lax.ppermute only.
A program may use at most 128 MiB of HBM per device.

v0:
```python
import jax
import jax.numpy as jnp
from jax import lax
from jax.sharding import PartitionSpec as P

LEVELS = 4


def node_order():
    ordering = []
    for depth_now in range(LEVELS - 1, -1, -1):
        ordering.extend(range(2**depth_now - 1, 2 ** (depth_now + 1) - 1))
    return ordering


def node_table(node_blocks, total_blocks):
    node_count = node_blocks.shape[0]
    ordered = jnp.array(node_order(), dtype=jnp.int32)
    node_ids = jnp.arange(node_count, dtype=jnp.int32)
    pick_sizes = (ordered[:, None] == node_ids[None, :]).astype(jnp.int32)
    level_sizes = jnp.sum(pick_sizes * node_blocks[None, :], axis=1)
    block_ends = jnp.cumsum(level_sizes)
    block_ids = jnp.arange(total_blocks, dtype=jnp.int32)
    positions = jnp.sum((block_ids[:, None] >= block_ends[None, :]).astype(jnp.int32), axis=1)
    return jnp.sum(
        (positions[:, None] == node_ids[None, :]).astype(jnp.int32) * ordered[None, :], axis=1
    )


def lookup(values_table, indices):
    positions_all = jnp.arange(values_table.shape[0], dtype=jnp.int32)
    return jnp.sum(
        (indices[:, None] == positions_all[None, :]).astype(jnp.int32) * values_table[None, :],
        axis=1,
    )


def panel_products(tile_stack, live_bits, vector):
    products = jnp.einsum("nxy,yw->nxw", tile_stack, vector, preferred_element_type=jnp.float32)
    return products * live_bits.astype(jnp.float32)[:, None, None]


def local(factor, right_side, node_blocks, front_mask):
    rows_local = factor.shape[0]
    cols_local = factor.shape[2]
    block_size = factor.shape[4]
    prow_count = lax.axis_size("prow")
    pcol_count = lax.axis_size("pcol")
    prow_index = lax.axis_index("prow")
    pcol_index = lax.axis_index("pcol")
    total_blocks = rows_local * prow_count
    level_rows = pcol_count // prow_count
    piece_rows = block_size // pcol_count
    tile_grid = factor.reshape(rows_local, cols_local, block_size, block_size)
    columns_in = right_side.reshape(cols_local, block_size, right_side.shape[3])
    block_node = node_table(node_blocks, total_blocks)
    row_ids = jnp.arange(rows_local, dtype=jnp.int32) * prow_count + prow_index
    col_ids = jnp.arange(cols_local, dtype=jnp.int32) * pcol_count + pcol_index
    row_nodes = lookup(block_node, row_ids)
    col_nodes = lookup(block_node, col_ids)
    node_ids = jnp.arange(node_blocks.shape[0], dtype=jnp.int32)
    pick_node = (col_nodes[:, None] == node_ids[None, :]).astype(jnp.int32)
    front_rows = jnp.sum(pick_node[:, :, None] * front_mask[None, :, :], axis=1)
    block_all = jnp.arange(total_blocks, dtype=jnp.int32)
    pick_row = (row_ids[:, None] == block_all[None, :]).astype(jnp.int32)
    front_bits = jnp.sum(pick_row[:, None, :] * front_rows[None, :, :], axis=2)
    diag_bits = (
        (row_nodes[:, None] == col_nodes[None, :]) & (row_ids[:, None] >= col_ids[None, :])
    ).astype(jnp.int32)

    def row_pieces(level_terms):
        rhs_width = level_terms.shape[2]
        split_rows = level_terms.reshape(level_rows, pcol_count, piece_rows, rhs_width)
        return jnp.transpose(split_rows, (1, 0, 2, 3))

    rhs_width = columns_in.shape[2]
    partial_value = jnp.zeros((rows_local, block_size, rhs_width), jnp.float32)
    solved_list = []
    for section_now in range(LEVELS):
        first_row = section_now * level_rows
        after_row = first_row + level_rows
        if section_now == 0:
            rhs_column = columns_in[0]
        else:
            mine = lax.psum_scatter(
                row_pieces(partial_value[first_row:after_row]).astype(jnp.bfloat16),
                "pcol",
                scatter_dimension=0,
                tiled=True,
            ).astype(jnp.float32)
            stacked = lax.all_gather(
                mine.reshape(level_rows, 1, piece_rows, rhs_width).astype(jnp.bfloat16),
                "prow",
                axis=1,
                tiled=True,
            ).astype(jnp.float32)
            arrived = lax.all_to_all(
                stacked.reshape(pcol_count, 1, piece_rows, rhs_width).astype(jnp.bfloat16),
                "pcol",
                split_axis=0,
                concat_axis=1,
                tiled=True,
            ).astype(jnp.float32)
            update = arrived.reshape(block_size, rhs_width)
            rhs_column = (columns_in[section_now].astype(jnp.float32) - update).astype(jnp.bfloat16)
        diag_terms = panel_products(
            tile_grid[first_row:after_row, section_now],
            diag_bits[first_row:after_row, section_now],
            rhs_column,
        )
        mine_solved = lax.psum_scatter(
            row_pieces(diag_terms).astype(jnp.bfloat16), "pcol", scatter_dimension=0, tiled=True
        )
        stacked_solved = lax.all_gather(
            mine_solved.reshape(level_rows, 1, piece_rows, rhs_width), "prow", axis=1, tiled=True
        )
        arrived_solved = lax.all_to_all(
            stacked_solved.reshape(pcol_count, 1, piece_rows, rhs_width),
            "pcol",
            split_axis=0,
            concat_axis=1,
            tiled=True,
        )
        solved = arrived_solved.reshape(block_size, rhs_width)
        solved_list.append(solved)
        if section_now + 1 < LEVELS:
            update_terms = panel_products(
                tile_grid[after_row:, section_now], front_bits[after_row:, section_now], solved
            )
            partial_value = partial_value.at[after_row:].add(update_terms)
    solution = jnp.stack(solved_list)
    return solution.reshape(cols_local, 1, block_size, columns_in.shape[2])


def solution(mesh):
    in_specs = (P(None, "prow", None, "pcol", None, None), P(None, "pcol", None, None), P(), P())
    out_specs = P(None, "pcol", None, None)
    return jax.shard_map(local, mesh=mesh, in_specs=in_specs, out_specs=out_specs, check_vma=False)
```

profile of v0, /device:TPU:1, one launch (start us, length us, event | category | flops | bytes accessed | tf_op | source)
XLA Modules:
  0.0 1262.8 jit_solution(1602754912323718388)
XLA Ops:
  9.0 7.6 copy.38
  19.5 146.2 %all-reduce.15.cloned.1.call-done = bf16[32,4,8,256]{3,2,0,1:T(8,128)(2,1)} async-done(((bf16[32,4,8,256]{3,2,0,1:T(8,128)(2,1)}), bf16[32,4,8,256]{3,2,0,1:T(8,128)(2,1)}) %all-reduce.15.cloned.1.call-update) | async-done | bytes 524304
  167.0 19.3 %all-gather = bf16[1,4,64,256]{3,2,0,1:T(8,128)(2,1)} all-gather(bf16[1,4,8,256]{3,2,0,1:T(8,128)(2,1)S(1)} %constant_dynamic-slice_fusion.6), channel_id=2, replica_groups=mesh['prow'=8,'pcol'=32] {'prow'}, dimensions={2}, use_global_device_ids=true | all-gather | bytes 147456 | tf_op jit(solution)/shard_map/all_gather | solution.py:114
  186.2 5.2 all-to-all-start
  191.7 8.9 all-to-all-done
  203.5 139.1 %all-reduce.17.cloned.1.call-done = bf16[32,4,8,256]{3,2,0,1:T(8,128)(2,1)} async-done(((bf16[32,4,8,256]{3,2,0,1:T(8,128)(2,1)}), bf16[32,4,8,256]{3,2,0,1:T(8,128)(2,1)}) %all-reduce.17.cloned.1.call-update) | async-done | bytes 524304
  343.8 18.1 %all-gather.1 = bf16[1,4,64,256]{3,2,0,1:T(8,128)(2,1)S(1)} all-gather(bf16[1,4,8,256]{3,2,0,1:T(8,128)(2,1)S(1)} %constant_dynamic-slice_fusion.5), channel_id=3, replica_groups=mesh['prow'=8,'pcol'=32] {'prow'}, dimensions={2}, use_global_device_ids=true | all-gather | bytes 147456 | tf_op jit(solution)/shard_map/all_gather | solution.py:91
  361.9 14.2 %all_to_all.28 = bf16[32,1,8,256]{3,2,1,0:T(8,128)(2,1)S(1)} all-to-all(bf16[32,1,8,256]{3,2,1,0:T(8,128)(2,1)S(1)} %bitcast.191), channel_id=1, replica_groups=mesh['prow'=8,'pcol'=32] {'pcol'}, dimensions={0} | all-to-all | bytes 262144 | tf_op jit(solution)/shard_map/all_to_all | solution.py:97
  378.3 139.1 %all-reduce.19.cloned.1.call-done = bf16[32,4,8,256]{3,2,0,1:T(8,128)(2,1)} async-done(((bf16[32,4,8,256]{3,2,0,1:T(8,128)(2,1)}), bf16[32,4,8,256]{3,2,0,1:T(8,128)(2,1)}) %all-reduce.19.cloned.1.call-update) | async-done | bytes 524304
  518.7 19.3 %all-gather.2 = bf16[1,4,64,256]{3,2,0,1:T(8,128)(2,1)} all-gather(bf16[1,4,8,256]{3,2,0,1:T(8,128)(2,1)S(1)} %constant_dynamic-slice_fusion.4), channel_id=4, replica_groups=mesh['prow'=8,'pcol'=32] {'prow'}, dimensions={2}, use_global_device_ids=true | all-gather | bytes 147456 | tf_op jit(solution)/shard_map/all_gather | solution.py:114
  538.0 5.2 all-to-all-start.2
  543.3 9.0 all-to-all-done.2
  556.3 139.1 %all-reduce.21.cloned.1.call-done = bf16[32,4,8,256]{3,2,0,1:T(8,128)(2,1)} async-done(((bf16[32,4,8,256]{3,2,0,1:T(8,128)(2,1)}), bf16[32,4,8,256]{3,2,0,1:T(8,128)(2,1)}) %all-reduce.21.cloned.1.call-update) | async-done | bytes 524304
  696.7 18.1 %all-gather.3 = bf16[1,4,64,256]{3,2,0,1:T(8,128)(2,1)S(1)} all-gather(bf16[1,4,8,256]{3,2,0,1:T(8,128)(2,1)S(1)} %constant_dynamic-slice_fusion.3), channel_id=5, replica_groups=mesh['prow'=8,'pcol'=32] {'prow'}, dimensions={2}, use_global_device_ids=true | all-gather | bytes 147456 | tf_op jit(solution)/shard_map/all_gather | solution.py:91
  714.8 14.2 %all_to_all.29 = bf16[32,1,8,256]{3,2,1,0:T(8,128)(2,1)S(1)} all-to-all(bf16[32,1,8,256]{3,2,1,0:T(8,128)(2,1)S(1)} %bitcast.192), channel_id=1, replica_groups=mesh['prow'=8,'pcol'=32] {'pcol'}, dimensions={0} | all-to-all | bytes 262144 | tf_op jit(solution)/shard_map/all_to_all | solution.py:97
  731.2 139.1 %all-reduce.23.cloned.1.call-done = bf16[32,4,8,256]{3,2,0,1:T(8,128)(2,1)} async-done(((bf16[32,4,8,256]{3,2,0,1:T(8,128)(2,1)}), bf16[32,4,8,256]{3,2,0,1:T(8,128)(2,1)}) %all-reduce.23.cloned.1.call-update) | async-done | bytes 524304
  871.6 19.3 %all-gather.4 = bf16[1,4,64,256]{3,2,0,1:T(8,128)(2,1)} all-gather(bf16[1,4,8,256]{3,2,0,1:T(8,128)(2,1)S(1)} %constant_dynamic-slice_fusion.2), channel_id=6, replica_groups=mesh['prow'=8,'pcol'=32] {'prow'}, dimensions={2}, use_global_device_ids=true | all-gather | bytes 147456 | tf_op jit(solution)/shard_map/all_gather | solution.py:114
  896.2 9.0 all-to-all-done.4
  907.8 139.0 %all-reduce.25.cloned.1.call-done = bf16[32,4,8,256]{3,2,0,1:T(8,128)(2,1)} async-done(((bf16[32,4,8,256]{3,2,0,1:T(8,128)(2,1)}), bf16[32,4,8,256]{3,2,0,1:T(8,128)(2,1)}) %all-reduce.25.cloned.1.call-update) | async-done | bytes 524304
  1048.0 18.1 %all-gather.5 = bf16[1,4,64,256]{3,2,0,1:T(8,128)(2,1)S(1)} all-gather(bf16[1,4,8,256]{3,2,0,1:T(8,128)(2,1)S(1)} %constant_dynamic-slice_fusion.1), channel_id=7, replica_groups=mesh['prow'=8,'pcol'=32] {'prow'}, dimensions={2}, use_global_device_ids=true | all-gather | bytes 147456 | tf_op jit(solution)/shard_map/all_gather | solution.py:91
  1066.2 14.2 %all_to_all.30 = bf16[32,1,8,256]{3,2,1,0:T(8,128)(2,1)S(1)} all-to-all(bf16[32,1,8,256]{3,2,1,0:T(8,128)(2,1)S(1)} %bitcast.193), channel_id=1, replica_groups=mesh['prow'=8,'pcol'=32] {'pcol'}, dimensions={0} | all-to-all | bytes 262144 | tf_op jit(solution)/shard_map/all_to_all | solution.py:97
  1082.5 139.0 %all-reduce.27.cloned.1.call-done = bf16[32,4,8,256]{3,2,0,1:T(8,128)(2,1)} async-done(((bf16[32,4,8,256]{3,2,0,1:T(8,128)(2,1)}), bf16[32,4,8,256]{3,2,0,1:T(8,128)(2,1)}) %all-reduce.27.cloned.1.call-update) | async-done | bytes 524304
  1222.9 18.1 %all-gather.6 = bf16[1,4,64,256]{3,2,0,1:T(8,128)(2,1)S(1)} all-gather(bf16[1,4,8,256]{3,2,0,1:T(8,128)(2,1)S(1)} %constant_dynamic-slice_fusion), channel_id=8, replica_groups=mesh['prow'=8,'pcol'=32] {'prow'}, dimensions={2}, use_global_device_ids=true | all-gather | bytes 147456 | tf_op jit(solution)/shard_map/all_gather | solution.py:114
  1241.0 14.2 %all_to_all.31 = bf16[32,1,8,256]{3,2,1,0:T(8,128)(2,1)S(1)} all-to-all(bf16[32,1,8,256]{3,2,1,0:T(8,128)(2,1)S(1)} %bitcast.194), channel_id=1, replica_groups=mesh['prow'=8,'pcol'=32] {'pcol'}, dimensions={0} | all-to-all | bytes 262144 | tf_op jit(solution)/shard_map/all_to_all | solution.py:117
  (56 shorter events, 36.8 us)
Async XLA Ops:
  6.5 159.2 %all-reduce.15.cloned.1.call-start = ((), (), s32[]{:S(2)}) async-start(), calls=%async_computation.7 | async-start | bytes 1048576
  8.9 9.8 copy-start.2
  8.9 10.4 copy-start.1
  186.2 14.4 %all-to-all-start = ((bf16[32,1,8,256]{3,2,1,0:T(8,128)(2,1)}), bf16[32,1,8,256]{3,2,1,0:T(8,128)(2,1)S(1)}, u32[]{:S(2)}, u32[]{:S(2)}) async-start(bf16[32,1,8,256]{3,2,1,0:T(8,128)(2,1)} %bitcast.10), calls=%async_computation | async-start | bytes 262144 | tf_op jit(solution)/shard_map/all_to_all | solution.py:117
  191.5 151.1 %all-reduce.17.cloned.1.call-start = ((), (), s32[]{:S(2)}) async-start(), calls=%async_computation.8 | async-start | bytes 1048576
  203.5 314.0 %all-reduce.19.cloned.1.call-start = ((), (), s32[]{:S(2)}) async-start(), calls=%async_computation.9 | async-start | bytes 1048576
  538.0 14.4 %all-to-all-start.2 = ((bf16[32,1,8,256]{3,2,1,0:T(8,128)(2,1)}), bf16[32,1,8,256]{3,2,1,0:T(8,128)(2,1)S(1)}, u32[]{:S(2)}, u32[]{:S(2)}) async-start(bf16[32,1,8,256]{3,2,1,0:T(8,128)(2,1)} %bitcast.30), calls=%async_computation.2 | async-start | bytes 262144 | tf_op jit(solution)/shard_map/all_to_all | solution.py:117
  543.2 152.2 %all-reduce.21.cloned.1.call-start = ((), (), s32[]{:S(2)}) async-start(), calls=%async_computation.10 | async-start | bytes 1048576
  554.0 1.4 copy-start
  556.3 314.0 %all-reduce.23.cloned.1.call-start = ((), (), s32[]{:S(2)}) async-start(), calls=%async_computation.11 | async-start | bytes 1048576
  890.8 14.4 %all-to-all-start.4 = ((bf16[32,1,8,256]{3,2,1,0:T(8,128)(2,1)}), bf16[32,1,8,256]{3,2,1,0:T(8,128)(2,1)S(1)}, u32[]{:S(2)}, u32[]{:S(2)}) async-start(bf16[32,1,8,256]{3,2,1,0:T(8,128)(2,1)} %bitcast.50), calls=%async_computation.4 | async-start | bytes 262144 | tf_op jit(solution)/shard_map/all_to_all | solution.py:117
  896.0 150.7 %all-reduce.25.cloned.1.call-start = ((), (), s32[]{:S(2)}) async-start(), calls=%async_computation.12 | async-start | bytes 1048576
  907.7 313.9 %all-reduce.27.cloned.1.call-start = ((), (), s32[]{:S(2)}) async-start(), calls=%async_computation.13 | async-start | bytes 1048576
Sparse Core Ops, SparseCore 0:
  18.9 146.7 all-reduce.14
  203.6 138.9 all-reduce.16
  378.5 138.9 all-reduce.18
  556.4 138.9 all-reduce.20
  731.3 138.9 all-reduce.22
  907.8 138.9 all-reduce.24
  1082.7 138.8 all-reduce.26
where the time goes:
time: 1260 us
  waiting for transfers between devices  1010 us (80%)
  blocking collectives  187 us (15%)
  local copies, waits for them, and re-layouts  20.1 us (2%)
  starting transfers between devices  15.9 us (1%)
  matrix products  14.9 us (1%)
  between operations  13.6 us (1%)
    unnamed x14, waiting for transfers between devices  981 us
    all_gather x4, blocking collectives, local(): lax.all_gather(mine_solved.reshape(level_rows, 1, piece_rows, rhs_width),...  75.9 us
    all_gather x3, blocking collectives, local(): lax.all_gather(mine.reshape(level_rows, 1, piece_rows, rhs_width).astype(...  54.3 us
    all_to_all x3, blocking collectives, local(): lax.all_to_all(stacked.reshape(pcol_count, 1, piece_rows, rhs_width).asty...  42.5 us
    all_to_all x3, waiting for transfers between devices, local(): lax.all_to_all(stacked_solved.reshape(pcol_count, 1, piece_rows, rhs_widt...  26.9 us
  transfers between devices with their start and end apart: 10, of which 10 were waited for; matrix products, arithmetic and copies ran while one was open for 0% of the time, Pallas kernels for 0%

commit v1 on v0

--- a/solution.py
+++ b/solution.py
@@ -68,10 +68,17 @@
         (row_nodes[:, None] == col_nodes[None, :]) & (row_ids[:, None] >= col_ids[None, :])
     ).astype(jnp.int32)
 
-    def row_pieces(level_terms):
+    def reduce_route(level_terms):
         rhs_width = level_terms.shape[2]
-        split_rows = level_terms.reshape(level_rows, pcol_count, piece_rows, rhs_width)
-        return jnp.transpose(split_rows, (1, 0, 2, 3))
+        pieces = level_terms.astype(jnp.bfloat16).reshape(level_rows, pcol_count, piece_rows, rhs_width)
+        pieces = jnp.transpose(pieces, (1, 0, 2, 3))
+        got = lax.all_to_all(pieces, "pcol", 0, 0, tiled=True)
+        summed = jnp.sum(got.astype(jnp.float32), axis=0).astype(jnp.bfloat16)
+        spread = jnp.broadcast_to(summed[None], (prow_count,) + summed.shape)
+        gathered = lax.all_to_all(spread, "prow", 0, 0, tiled=True)
+        by_row = jnp.transpose(gathered, (1, 0, 2, 3)).reshape(pcol_count, piece_rows, rhs_width)
+        arrived = lax.all_to_all(by_row, "pcol", 0, 0, tiled=True)
+        return arrived.reshape(block_size, rhs_width)
 
     rhs_width = columns_in.shape[2]
     partial_value = jnp.zeros((rows_local, block_size, rhs_width), jnp.float32)
@@ -82,46 +89,14 @@
         if section_now == 0:
             rhs_column = columns_in[0]
         else:
-            mine = lax.psum_scatter(
-                row_pieces(partial_value[first_row:after_row]).astype(jnp.bfloat16),
-                "pcol",
-                scatter_dimension=0,
-                tiled=True,
-            ).astype(jnp.float32)
-            stacked = lax.all_gather(
-                mine.reshape(level_rows, 1, piece_rows, rhs_width).astype(jnp.bfloat16),
-                "prow",
-                axis=1,
-                tiled=True,
-            ).astype(jnp.float32)
-            arrived = lax.all_to_all(
-                stacked.reshape(pcol_count, 1, piece_rows, rhs_width).astype(jnp.bfloat16),
-                "pcol",
-                split_axis=0,
-                concat_axis=1,
-                tiled=True,
-            ).astype(jnp.float32)
-            update = arrived.reshape(block_size, rhs_width)
+            update = reduce_route(partial_value[first_row:after_row]).astype(jnp.float32)
             rhs_column = (columns_in[section_now].astype(jnp.float32) - update).astype(jnp.bfloat16)
         diag_terms = panel_products(
             tile_grid[first_row:after_row, section_now],
             diag_bits[first_row:after_row, section_now],
             rhs_column,
         )
-        mine_solved = lax.psum_scatter(
-            row_pieces(diag_terms).astype(jnp.bfloat16), "pcol", scatter_dimension=0, tiled=True
-        )
-        stacked_solved = lax.all_gather(
-            mine_solved.reshape(level_rows, 1, piece_rows, rhs_width), "prow", axis=1, tiled=True
-        )
-        arrived_solved = lax.all_to_all(
-            stacked_solved.reshape(pcol_count, 1, piece_rows, rhs_width),
-            "pcol",
-            split_axis=0,
-            concat_axis=1,
-            tiled=True,
-        )
-        solved = arrived_solved.reshape(block_size, rhs_width)
+        solved = reduce_route(diag_terms)
         solved_list.append(solved)
         if section_now + 1 < LEVELS:
             update_terms = panel_products(

time: 1260 us -> 346 us (0.27)
  waiting for transfers between devices: 1010 us -> 46.5 us
  blocking collectives: 187 us -> 232 us
  starting transfers between devices: 15.9 us -> 35.6 us
  between operations: 13.6 us -> 0.2 us
    unnamed x14 -> x0, waiting for transfers between devices: 981 us -> none
    all_to_all x4 -> x16, blocking collectives: 56.6 us -> 232 us  [the longest x6 98 us: reduce_route(): got = lax.all_to_all(pieces, 'pcol', 0, 0, tiled=True)]
    all_gather x7 -> x0, blocking collectives: 130 us -> none  [the longest x4 75.9 us: local(): lax.all_gather(mine_solved.reshape(level_rows, 1, piece_rows, rhs_width),...]
    all_to_all x3 -> x5, starting transfers between devices: 15.7 us -> 35.6 us  [the longest x3 15.8 us: reduce_route(): arrived = lax.all_to_all(by_row, 'pcol', 0, 0, tiled=True)]
    all_to_all x3 -> x5, waiting for transfers between devices: 26.9 us -> 46.5 us  [the longest x3 27.1 us: reduce_route(): arrived = lax.all_to_all(by_row, 'pcol', 0, 0, tiled=True)]
  transfers between devices with their start and end apart: 10 -> 5, of which waited for: 10 -> 5; matrix products, arithmetic and copies ran while one was open for 0% -> 0% of each run, Pallas kernels for 0% -> 0%
where the time goes in v1:
time: 346 us; the launch traced here: 344 us
  blocking collectives  232 us (67%)
  waiting for transfers between devices  46.5 us (13%)
  starting transfers between devices  35.6 us (10%)
  local copies, waits for them, and re-layouts  13 us (4%)
  matrix products  10.5 us (3%)
  other arithmetic  6.49 us (2%)
    all_to_all x6, blocking collectives, reduce_route(): got = lax.all_to_all(pieces, 'pcol', 0, 0, tiled=True)  98 us
    all_to_all x6, blocking collectives, reduce_route(): gathered = lax.all_to_all(spread, 'prow', 0, 0, tiled=True)  77.2 us
    all_to_all x4, blocking collectives, reduce_route(): arrived = lax.all_to_all(by_row, 'pcol', 0, 0, tiled=True)  56.8 us
    all_to_all x3, waiting for transfers between devices, reduce_route(): arrived = lax.all_to_all(by_row, 'pcol', 0, 0, tiled=True)  27.1 us
    all_to_all x3, starting transfers between devices, reduce_route(): arrived = lax.all_to_all(by_row, 'pcol', 0, 0, tiled=True)  15.8 us
    all_to_all x1, waiting for transfers between devices, reduce_route(): got = lax.all_to_all(pieces, 'pcol', 0, 0, tiled=True)  14.2 us
    all_to_all x1, starting transfers between devices, reduce_route(): got = lax.all_to_all(pieces, 'pcol', 0, 0, tiled=True)  12 us
    dot_general x7, matrix products, panel_products(): jnp.einsum('nxy,yw->nxw', tile_stack, vector, preferred_element_type=jnp....  10.5 us
  transfers between devices with their start and end apart: 5, of which 5 were waited for; matrix products, arithmetic and copies ran while one was open for 0% of the time, Pallas kernels for 0%

profile of v1, /device:TPU:1, one launch (start us, length us, event | category | flops | bytes accessed | tf_op | source)
XLA Modules:
  0.0 344.2 jit_solution(5557644550952876635)
XLA Ops:
  2.4 7.6 %copy.53 = bf16[16,1,4,1,256,256]{5,4,0,2,3,1:T(8,128)(2,1)} copy(bf16[16,1,4,1,256,256]{5,4,3,2,1,0:T(8,128)(2,1)} %param.11) | data formatting | bytes 16777216 | tf_op args[0]
  12.3 12.0 %all-to-all-start = ((bf16[32,4,8,256]{3,2,1,0:T(8,128)(2,1)}), bf16[32,4,8,256]{3,2,1,0:T(8,128)(2,1)S(1)}, u32[]{:S(2)}, u32[]{:S(2)}) async-start(bf16[32,4,8,256]{3,2,1,0:T(8,128)(2,1)} %bitcast.172), calls=%async_computation | async-start | bytes 1048576 | tf_op jit(solution)/shard_map/all_to_all | solution.py:75
  24.4 14.2 %all-to-all-done = bf16[32,4,8,256]{3,2,1,0:T(8,128)(2,1)S(1)} async-done(((bf16[32,4,8,256]{3,2,1,0:T(8,128)(2,1)}), bf16[32,4,8,256]{3,2,1,0:T(8,128)(2,1)S(1)}, u32[]{:S(2)}, u32[]{:S(2)}) %all-to-all-start) | async-done | bytes 524320 | tf_op jit(solution)/shard_map/all_to_all | solution.py:75
  39.3 7.8 %all-to-all-start.1 = ((bf16[8,4,8,256]{3,2,1,0:T(8,128)(2,1)}), bf16[8,4,8,256]{3,2,1,0:T(8,128)(2,1)S(1)}, u32[]{:S(2)}, u32[]{:S(2)}) async-start(bf16[8,4,8,256]{3,2,1,0:T(8,128)(2,1)} %broadcast_in_dim.14), calls=%async_computation.1 | async-start | bytes 262144 | tf_op jit(solution)/shard_map/all_to_all | solution.py:78
  53.1 5.3 %all-to-all-start.2 = ((bf16[32,8,256]{2,1,0:T(8,128)(2,1)}), bf16[32,8,256]{2,1,0:T(8,128)(2,1)S(1)}, u32[]{:S(2)}, u32[]{:S(2)}) async-start(bf16[32,8,256]{2,1,0:T(8,128)(2,1)} %bitcast.10), calls=%async_computation.2 | async-start | bytes 262144 | tf_op jit(solution)/shard_map/all_to_all | solution.py:80
  58.7 8.9 %all-to-all-done.2 = bf16[32,8,256]{2,1,0:T(8,128)(2,1)S(1)} async-done(((bf16[32,8,256]{2,1,0:T(8,128)(2,1)}), bf16[32,8,256]{2,1,0:T(8,128)(2,1)S(1)}, u32[]{:S(2)}, u32[]{:S(2)}) %all-to-all-start.2) | async-done | bytes 131104 | tf_op jit(solution)/shard_map/all_to_all | solution.py:80
  69.7 16.4 %all_to_all.105 = bf16[32,4,8,256]{3,2,1,0:T(8,128)(2,1)} all-to-all(bf16[32,4,8,256]{3,2,1,0:T(8,128)(2,1)S(1)} %copy_bitcast_fusion.6), channel_id=1, replica_groups=mesh['prow'=8,'pcol'=32] {'pcol'}, dimensions={0} | all-to-all | bytes 1048576 | tf_op jit(solution)/shard_map/all_to_all | solution.py:75
  87.2 12.9 %all_to_all.106 = bf16[8,4,8,256]{3,2,1,0:T(8,128)(2,1)S(1)} all-to-all(bf16[8,4,8,256]{3,2,1,0:T(8,128)(2,1)S(1)} %broadcast_in_dim.15), channel_id=1, replica_groups=mesh['prow'=8,'pcol'=32] {'prow'}, dimensions={0} | all-to-all | bytes 262144 | tf_op jit(solution)/shard_map/all_to_all | solution.py:78
  100.1 14.1 %all_to_all.107 = bf16[32,8,256]{2,1,0:T(8,128)(2,1)S(1)} all-to-all(bf16[32,8,256]{2,1,0:T(8,128)(2,1)S(1)} %bitcast.187), channel_id=1, replica_groups=mesh['prow'=8,'pcol'=32] {'pcol'}, dimensions={0} | all-to-all | bytes 262144 | tf_op jit(solution)/shard_map/all_to_all | solution.py:80
  115.7 16.4 %all_to_all.108 = bf16[32,4,8,256]{3,2,1,0:T(8,128)(2,1)} all-to-all(bf16[32,4,8,256]{3,2,1,0:T(8,128)(2,1)S(1)} %bitcast.180), channel_id=1, replica_groups=mesh['prow'=8,'pcol'=32] {'pcol'}, dimensions={0} | all-to-all | bytes 1048576 | tf_op jit(solution)/shard_map/all_to_all | solution.py:75
  133.3 12.9 %all_to_all.109 = bf16[8,4,8,256]{3,2,1,0:T(8,128)(2,1)S(1)} all-to-all(bf16[8,4,8,256]{3,2,1,0:T(8,128)(2,1)S(1)} %broadcast_in_dim.16), channel_id=1, replica_groups=mesh['prow'=8,'pcol'=32] {'prow'}, dimensions={0} | all-to-all | bytes 262144 | tf_op jit(solution)/shard_map/all_to_all | solution.py:78
  152.1 9.1 %all-to-all-done.8 = bf16[32,8,256]{2,1,0:T(8,128)(2,1)S(1)} async-done(((bf16[32,8,256]{2,1,0:T(8,128)(2,1)}), bf16[32,8,256]{2,1,0:T(8,128)(2,1)S(1)}, u32[]{:S(2)}, u32[]{:S(2)}) %all-to-all-start.8) | async-done | bytes 131104 | tf_op jit(solution)/shard_map/all_to_all | solution.py:80
  164.3 16.4 %all_to_all.110 = bf16[32,4,8,256]{3,2,1,0:T(8,128)(2,1)S(1)} all-to-all(bf16[32,4,8,256]{3,2,1,0:T(8,128)(2,1)S(1)} %copy_bitcast_fusion.4), channel_id=1, replica_groups=mesh['prow'=8,'pcol'=32] {'pcol'}, dimensions={0} | all-to-all | bytes 1048576 | tf_op jit(solution)/shard_map/all_to_all | solution.py:75
  180.8 13.0 %all_to_all.111 = bf16[8,4,8,256]{3,2,1,0:T(8,128)(2,1)S(1)} all-to-all(bf16[8,4,8,256]{3,2,1,0:T(8,128)(2,1)S(1)} %broadcast_in_dim.17), channel_id=1, replica_groups=mesh['prow'=8,'pcol'=32] {'prow'}, dimensions={0} | all-to-all | bytes 262144 | tf_op jit(solution)/shard_map/all_to_all | solution.py:78
  193.8 14.2 %all_to_all.112 = bf16[32,8,256]{2,1,0:T(8,128)(2,1)S(1)} all-to-all(bf16[32,8,256]{2,1,0:T(8,128)(2,1)S(1)} %bitcast.188), channel_id=1, replica_groups=mesh['prow'=8,'pcol'=32] {'pcol'}, dimensions={0} | all-to-all | bytes 262144 | tf_op jit(solution)/shard_map/all_to_all | solution.py:80
  209.4 16.3 %all_to_all.113 = bf16[32,4,8,256]{3,2,1,0:T(8,128)(2,1)S(1)} all-to-all(bf16[32,4,8,256]{3,2,1,0:T(8,128)(2,1)S(1)} %bitcast.181), channel_id=1, replica_groups=mesh['prow'=8,'pcol'=32] {'pcol'}, dimensions={0} | all-to-all | bytes 1048576 | tf_op jit(solution)/shard_map/all_to_all | solution.py:75
  225.8 12.8 %all_to_all.114 = bf16[8,4,8,256]{3,2,1,0:T(8,128)(2,1)S(1)} all-to-all(bf16[8,4,8,256]{3,2,1,0:T(8,128)(2,1)S(1)} %broadcast_in_dim.18), channel_id=1, replica_groups=mesh['prow'=8,'pcol'=32] {'prow'}, dimensions={0} | all-to-all | bytes 262144 | tf_op jit(solution)/shard_map/all_to_all | solution.py:78
  244.6 9.1 %all-to-all-done.14 = bf16[32,8,256]{2,1,0:T(8,128)(2,1)S(1)} async-done(((bf16[32,8,256]{2,1,0:T(8,128)(2,1)}), bf16[32,8,256]{2,1,0:T(8,128)(2,1)S(1)}, u32[]{:S(2)}, u32[]{:S(2)}) %all-to-all-start.14) | async-done | bytes 131104 | tf_op jit(solution)/shard_map/all_to_all | solution.py:80
  255.1 16.3 %all_to_all.115 = bf16[32,4,8,256]{3,2,1,0:T(8,128)(2,1)S(1)} all-to-all(bf16[32,4,8,256]{3,2,1,0:T(8,128)(2,1)S(1)} %bitcast.182), channel_id=1, replica_groups=mesh['prow'=8,'pcol'=32] {'pcol'}, dimensions={0} | all-to-all | bytes 1048576 | tf_op jit(solution)/shard_map/all_to_all | solution.py:75
  271.5 12.8 %all_to_all.116 = bf16[8,4,8,256]{3,2,1,0:T(8,128)(2,1)S(1)} all-to-all(bf16[8,4,8,256]{3,2,1,0:T(8,128)(2,1)S(1)} %broadcast_in_dim.19), channel_id=1, replica_groups=mesh['prow'=8,'pcol'=32] {'prow'}, dimensions={0} | all-to-all | bytes 262144 | tf_op jit(solution)/shard_map/all_to_all | solution.py:78
  284.3 14.2 %all_to_all.117 = bf16[32,8,256]{2,1,0:T(8,128)(2,1)S(1)} all-to-all(bf16[32,8,256]{2,1,0:T(8,128)(2,1)S(1)} %bitcast.189), channel_id=1, replica_groups=mesh['prow'=8,'pcol'=32] {'pcol'}, dimensions={0} | all-to-all | bytes 262144 | tf_op jit(solution)/shard_map/all_to_all | solution.py:80
  299.9 16.3 %all_to_all.118 = bf16[32,4,8,256]{3,2,1,0:T(8,128)(2,1)S(1)} all-to-all(bf16[32,4,8,256]{3,2,1,0:T(8,128)(2,1)S(1)} %bitcast.183), channel_id=1, replica_groups=mesh['prow'=8,'pcol'=32] {'pcol'}, dimensions={0} | all-to-all | bytes 1048576 | tf_op jit(solution)/shard_map/all_to_all | solution.py:75
  316.3 12.8 %all_to_all.119 = bf16[8,4,8,256]{3,2,1,0:T(8,128)(2,1)S(1)} all-to-all(bf16[8,4,8,256]{3,2,1,0:T(8,128)(2,1)S(1)} %broadcast_in_dim.20), channel_id=1, replica_groups=mesh['prow'=8,'pcol'=32] {'prow'}, dimensions={0} | all-to-all | bytes 262144 | tf_op jit(solution)/shard_map/all_to_all | solution.py:78
  329.1 14.2 %all_to_all.120 = bf16[32,8,256]{2,1,0:T(8,128)(2,1)S(1)} all-to-all(bf16[32,8,256]{2,1,0:T(8,128)(2,1)S(1)} %bitcast.190), channel_id=1, replica_groups=mesh['prow'=8,'pcol'=32] {'pcol'}, dimensions={0} | all-to-all | bytes 262144 | tf_op jit(solution)/shard_map/all_to_all | solution.py:80
  (64 shorter events, 37.9 us)
Async XLA Ops:
  10.0 37.2 %copy-start.3 = (s32[15,128]{1,0:T(8,128)S(1)}, s32[15,128]{1,0:T(8,128)}, u32[]{:S(2)}) copy-start(s32[15,128]{1,0:T(8,128)} %param.14) | copy-start | bytes 23044
  12.3 26.3 %all-to-all-start = ((bf16[32,4,8,256]{3,2,1,0:T(8,128)(2,1)}), bf16[32,4,8,256]{3,2,1,0:T(8,128)(2,1)S(1)}, u32[]{:S(2)}, u32[]{:S(2)}) async-start(bf16[32,4,8,256]{3,2,1,0:T(8,128)(2,1)} %bitcast.172), calls=%async_computation | async-start | bytes 1048576 | tf_op jit(solution)/shard_map/all_to_all | solution.py:75
  39.3 13.1 %all-to-all-start.1 = ((bf16[8,4,8,256]{3,2,1,0:T(8,128)(2,1)}), bf16[8,4,8,256]{3,2,1,0:T(8,128)(2,1)S(1)}, u32[]{:S(2)}, u32[]{:S(2)}) async-start(bf16[8,4,8,256]{3,2,1,0:T(8,128)(2,1)} %broadcast_in_dim.14), calls=%async_computation.1 | async-start | bytes 262144 | tf_op jit(solution)/shard_map/all_to_all | solution.py:78
  53.1 14.5 %all-to-all-start.2 = ((bf16[32,8,256]{2,1,0:T(8,128)(2,1)}), bf16[32,8,256]{2,1,0:T(8,128)(2,1)S(1)}, u32[]{:S(2)}, u32[]{:S(2)}) async-start(bf16[32,8,256]{2,1,0:T(8,128)(2,1)} %bitcast.10), calls=%async_computation.2 | async-start | bytes 262144 | tf_op jit(solution)/shard_map/all_to_all | solution.py:80
  146.8 14.3 %all-to-all-start.8 = ((bf16[32,8,256]{2,1,0:T(8,128)(2,1)}), bf16[32,8,256]{2,1,0:T(8,128)(2,1)S(1)}, u32[]{:S(2)}, u32[]{:S(2)}) async-start(bf16[32,8,256]{2,1,0:T(8,128)(2,1)} %bitcast.30), calls=%async_computation.8 | async-start | bytes 262144 | tf_op jit(solution)/shard_map/all_to_all | solution.py:80
  162.8 1.4 copy-start
  164.2 43.8 %copy-start.2 = (bf16[4,1,256,256]{3,2,1,0:T(8,128)(2,1)S(1)}, bf16[4,1,256,256]{3,2,1,0:T(8,128)(2,1)}, u32[]{:S(2)}) copy-start(bf16[4,1,256,256]{3,2,1,0:T(8,128)(2,1)} %param.12) | copy-start | bytes 1572868
  180.7 73.0 %copy-start.1 = (f32[8,256,256]{2,1,0:T(8,128)S(1)}, f32[8,256,256]{2,1,0:T(8,128)}, u32[]{:S(2)}) copy-start(f32[8,256,256]{2,1,0:T(8,128)} %copy-done) | copy-start | bytes 6291460
  239.3 14.4 %all-to-all-start.14 = ((bf16[32,8,256]{2,1,0:T(8,128)(2,1)}), bf16[32,8,256]{2,1,0:T(8,128)(2,1)S(1)}, u32[]{:S(2)}, u32[]{:S(2)}) async-start(bf16[32,8,256]{2,1,0:T(8,128)(2,1)} %bitcast.50), calls=%async_computation.14 | async-start | bytes 262144 | tf_op jit(solution)/shard_map/all_to_all | solution.py:80

commit v2 on v1

--- a/solution.py
+++ b/solution.py
@@ -51,8 +51,10 @@
     total_blocks = rows_local * prow_count
     level_rows = pcol_count // prow_count
     piece_rows = block_size // pcol_count
+    prow_piece = block_size // prow_count
     tile_grid = factor.reshape(rows_local, cols_local, block_size, block_size)
     columns_in = right_side.reshape(cols_local, block_size, right_side.shape[3])
+    rhs_width = columns_in.shape[2]
     block_node = node_table(node_blocks, total_blocks)
     row_ids = jnp.arange(rows_local, dtype=jnp.int32) * prow_count + prow_index
     col_ids = jnp.arange(cols_local, dtype=jnp.int32) * pcol_count + pcol_index
@@ -68,8 +70,43 @@
         (row_nodes[:, None] == col_nodes[None, :]) & (row_ids[:, None] >= col_ids[None, :])
     ).astype(jnp.int32)
 
+    level_groups = level_rows
+    group_of_col = pcol_index // prow_count
+    shifted = []
+    for shift in range(level_groups):
+        pick_k = (group_of_col + shift) % level_groups
+        sent = jnp.stack(
+            [
+                lax.dynamic_index_in_dim(tile_grid[:, level], level * level_groups + pick_k, 0, False)
+                for level in range(1, LEVELS)
+            ]
+        )
+        pairs = []
+        for p_src in range(prow_count):
+            for c_src in range(pcol_count):
+                k_dst = (c_src // prow_count + shift) % level_groups
+                dst = (c_src % prow_count) * pcol_count + k_dst * prow_count + p_src
+                pairs.append((p_src * pcol_count + c_src, dst))
+        shifted.append(lax.ppermute(sent, ("prow", "pcol"), pairs))
+    shifted = jnp.stack(shifted)
+    diag_tiles = jnp.stack(
+        [
+            lax.dynamic_index_in_dim(shifted, (group_of_col - m) % level_groups, 0, False)
+            for m in range(level_groups)
+        ],
+        axis=1,
+    )
+    own_row = jnp.arange(1, LEVELS, dtype=jnp.int32)[:, None] * pcol_count + pcol_index
+    group_cols = (
+        jnp.arange(1, LEVELS, dtype=jnp.int32)[:, None] * pcol_count
+        + prow_index
+        + prow_count * jnp.arange(level_groups, dtype=jnp.int32)[None, :]
+    )
+    own_node = lookup(block_node, own_row.reshape(-1)).reshape(own_row.shape)
+    group_node = lookup(block_node, group_cols.reshape(-1)).reshape(group_cols.shape)
+    group_bits = ((own_node == group_node) & (own_row >= group_cols)).astype(jnp.float32)
+
     def reduce_route(level_terms):
-        rhs_width = level_terms.shape[2]
         pieces = level_terms.astype(jnp.bfloat16).reshape(level_rows, pcol_count, piece_rows, rhs_width)
         pieces = jnp.transpose(pieces, (1, 0, 2, 3))
         got = lax.all_to_all(pieces, "pcol", 0, 0, tiled=True)
@@ -80,23 +117,47 @@
         arrived = lax.all_to_all(by_row, "pcol", 0, 0, tiled=True)
         return arrived.reshape(block_size, rhs_width)
 
-    rhs_width = columns_in.shape[2]
+    def reduce_gather_pcol(level_terms):
+        pieces = level_terms.astype(jnp.bfloat16).reshape(level_rows, pcol_count, piece_rows, rhs_width)
+        pieces = jnp.transpose(pieces, (1, 0, 2, 3))
+        got = lax.all_to_all(pieces, "pcol", 0, 0, tiled=True)
+        summed = (-jnp.sum(got.astype(jnp.float32), axis=0)).astype(jnp.bfloat16)
+        spread = jnp.broadcast_to(summed[None], (pcol_count,) + summed.shape)
+        gathered = lax.all_to_all(spread, "pcol", 0, 0, tiled=True)
+        return jnp.transpose(gathered, (1, 0, 2, 3)).reshape(level_rows, block_size, rhs_width)
+
+    def reduce_gather_prow(row_terms):
+        pieces = row_terms.astype(jnp.bfloat16).reshape(prow_count, prow_piece, rhs_width)
+        got = lax.all_to_all(pieces, "prow", 0, 0, tiled=True)
+        summed = jnp.sum(got.astype(jnp.float32), axis=0).astype(jnp.bfloat16)
+        spread = jnp.broadcast_to(summed[None], (prow_count,) + summed.shape)
+        gathered = lax.all_to_all(spread, "prow", 0, 0, tiled=True)
+        return gathered.reshape(block_size, rhs_width)
+
+    row_in_group = prow_index + prow_count * jnp.arange(level_rows, dtype=jnp.int32)
+    owns_row = (row_in_group == pcol_index).astype(jnp.float32)
+
     partial_value = jnp.zeros((rows_local, block_size, rhs_width), jnp.float32)
     solved_list = []
     for section_now in range(LEVELS):
         first_row = section_now * level_rows
         after_row = first_row + level_rows
         if section_now == 0:
-            rhs_column = columns_in[0]
+            diag_terms = panel_products(
+                tile_grid[first_row:after_row, 0], diag_bits[first_row:after_row, 0], columns_in[0]
+            )
+            solved = reduce_route(diag_terms)
         else:
-            update = reduce_route(partial_value[first_row:after_row]).astype(jnp.float32)
-            rhs_column = (columns_in[section_now].astype(jnp.float32) - update).astype(jnp.bfloat16)
-        diag_terms = panel_products(
-            tile_grid[first_row:after_row, section_now],
-            diag_bits[first_row:after_row, section_now],
-            rhs_column,
-        )
-        solved = reduce_route(diag_terms)
+            own_b = columns_in[section_now].astype(jnp.float32)
+            contrib = partial_value[first_row:after_row] - owns_row[:, None, None] * own_b[None]
+            rhs_group = reduce_gather_pcol(contrib)
+            tiles = diag_tiles[section_now - 1] * group_bits[section_now - 1][:, None, None].astype(
+                jnp.bfloat16
+            )
+            row_terms = jnp.einsum(
+                "mxy,myw->xw", tiles, rhs_group, preferred_element_type=jnp.float32
+            )
+            solved = reduce_gather_prow(row_terms)
         solved_list.append(solved)
         if section_now + 1 < LEVELS:
             update_terms = panel_products(

time: 346 us -> 357 us (1.032)
  blocking collectives: 232 us -> 127 us
  waiting for transfers between devices: 46.5 us -> 118 us
  starting transfers between devices: 35.6 us -> 66.1 us
  other arithmetic: 6.49 us -> 15.8 us
  local copies, waits for them, and re-layouts: 13 us -> 17.9 us
    all_to_all x16 -> x8, blocking collectives: 232 us -> 127 us  [the longest x2 42.3 us: reduce_gather_pcol(): gathered = lax.all_to_all(spread, 'pcol', 0, 0, tiled=True)]
    all_to_all x0 -> x4, waiting for transfers between devices: none -> 95.9 us  [the longest x1 85.5 us: reduce_gather_pcol(): gathered = lax.all_to_all(spread, 'pcol', 0, 0, tiled=True)]
    all_to_all x0 -> x4, starting transfers between devices: none -> 31 us  [the longest x1 18 us: reduce_gather_pcol(): gathered = lax.all_to_all(spread, 'pcol', 0, 0, tiled=True)]
    all_to_all x3 -> x1, waiting for transfers between devices: 27.1 us -> 8.27 us  [reduce_route(): arrived = lax.all_to_all(by_row, 'pcol', 0, 0, tiled=True)]
    all_to_all x3 -> x1, starting transfers between devices: 15.8 us -> 5.34 us  [reduce_route(): arrived = lax.all_to_all(by_row, 'pcol', 0, 0, tiled=True)]
    ppermute x0 -> x4, starting transfers between devices: none -> 9.93 us  [local(): shifted.append(lax.ppermute(sent, ('prow', 'pcol'), pairs))]
    another operation x1 -> x8, other arithmetic: 0.19 us -> 9.53 us  [the longest x4 6.37 us: local(): jnp.stack([lax.dynamic_index_in_dim(tile_grid[:, level], level * level_gr...]
    all_to_all x1, waiting for transfers between devices: 14.2 us -> 9.31 us  [reduce_route(): got = lax.all_to_all(pieces, 'pcol', 0, 0, tiled=True)]
  transfers between devices with their start and end apart: 5 -> 11, of which waited for: 5 -> 6; matrix products, arithmetic and copies ran while one was open for 0% -> 5% of each run, Pallas kernels for 0% -> 0%
where the time goes in v2:
time: 357 us; the launch traced here: 356 us
  blocking collectives  127 us (36%)
  waiting for transfers between devices  118 us (33%)
  starting transfers between devices  66.1 us (19%)
  local copies, waits for them, and re-layouts  17.9 us (5%)
  other arithmetic  15.8 us (4%)
  matrix products  10.9 us (3%)
    all_to_all x1, waiting for transfers between devices, reduce_gather_pcol(): gathered = lax.all_to_all(spread, 'pcol', 0, 0, tiled=True)  85.5 us
    all_to_all x2, blocking collectives, reduce_gather_pcol(): gathered = lax.all_to_all(spread, 'pcol', 0, 0, tiled=True)  42.3 us
    all_to_all x3, blocking collectives, reduce_gather_prow(): got = lax.all_to_all(pieces, 'prow', 0, 0, tiled=True)  38 us
    all_to_all x2, blocking collectives, reduce_gather_pcol(): got = lax.all_to_all(pieces, 'pcol', 0, 0, tiled=True)  37.7 us
    all_to_all x1, starting transfers between devices, reduce_gather_pcol(): gathered = lax.all_to_all(spread, 'pcol', 0, 0, tiled=True)  18 us
    all_to_all x1, starting transfers between devices, reduce_route(): got = lax.all_to_all(pieces, 'pcol', 0, 0, tiled=True)  12 us
    all_to_all x2, waiting for transfers between devices, reduce_gather_prow(): gathered = lax.all_to_all(spread, 'prow', 0, 0, tiled=True)  10.4 us
    ppermute x4, starting transfers between devices, local(): shifted.append(lax.ppermute(sent, ('prow', 'pcol'), pairs))  9.93 us
  transfers between devices with their start and end apart: 11, of which 6 were waited for; matrix products, arithmetic and copies ran while one was open for 5% of the time, Pallas kernels for 0%

profile of v2, /device:TPU:1, one launch (start us, length us, event | category | flops | bytes accessed | tf_op | source)
XLA Modules:
  0.0 355.7 jit_solution(13990451987338257107)
XLA Ops:
  0.0 7.7 %copy.50 = bf16[16,1,4,1,256,256]{5,4,0,2,3,1:T(8,128)(2,1)} copy(bf16[16,1,4,1,256,256]{5,4,3,2,1,0:T(8,128)(2,1)} %param.11) | data formatting | bytes 16777216 | tf_op args[0]
  10.9 12.0 %all-to-all-start = ((bf16[32,4,8,256]{3,2,1,0:T(8,128)(2,1)}), bf16[32,4,8,256]{3,2,1,0:T(8,128)(2,1)S(1)}, u32[]{:S(2)}, u32[]{:S(2)}) async-start(bf16[32,4,8,256]{3,2,1,0:T(8,128)(2,1)} %bitcast.181), calls=%async_computation | async-start | bytes 1048576 | tf_op jit(solution)/shard_map/all_to_all | solution.py:112
  23.3 3.5 fusion.38
  27.9 9.3 %all-to-all-done = bf16[32,4,8,256]{3,2,1,0:T(8,128)(2,1)S(1)} async-done(((bf16[32,4,8,256]{3,2,1,0:T(8,128)(2,1)}), bf16[32,4,8,256]{3,2,1,0:T(8,128)(2,1)S(1)}, u32[]{:S(2)}, u32[]{:S(2)}) %all-to-all-start) | async-done | bytes 524320 | tf_op jit(solution)/shard_map/all_to_all | solution.py:112
  38.0 7.8 %all-to-all-start.1 = ((bf16[8,4,8,256]{3,2,1,0:T(8,128)(2,1)}), bf16[8,4,8,256]{3,2,1,0:T(8,128)(2,1)S(1)}, u32[]{:S(2)}, u32[]{:S(2)}) async-start(bf16[8,4,8,256]{3,2,1,0:T(8,128)(2,1)} %broadcast_in_dim.14), calls=%async_computation.1 | async-start | bytes 262144 | tf_op jit(solution)/shard_map/all_to_all | solution.py:115
  46.6 4.5 %all-to-all-done.1 = bf16[8,4,8,256]{3,2,1,0:T(8,128)(2,1)S(1)} async-done(((bf16[8,4,8,256]{3,2,1,0:T(8,128)(2,1)}), bf16[8,4,8,256]{3,2,1,0:T(8,128)(2,1)S(1)}, u32[]{:S(2)}, u32[]{:S(2)}) %all-to-all-start.1) | async-done | bytes 131104 | tf_op jit(solution)/shard_map/all_to_all | solution.py:115
  51.7 5.3 %all-to-all-start.2 = ((bf16[32,8,256]{2,1,0:T(8,128)(2,1)}), bf16[32,8,256]{2,1,0:T(8,128)(2,1)S(1)}, u32[]{:S(2)}, u32[]{:S(2)}) async-start(bf16[32,8,256]{2,1,0:T(8,128)(2,1)} %bitcast.10), calls=%async_computation.2 | async-start | bytes 262144 | tf_op jit(solution)/shard_map/all_to_all | solution.py:117
  58.0 8.3 %all-to-all-done.2 = bf16[32,8,256]{2,1,0:T(8,128)(2,1)S(1)} async-done(((bf16[32,8,256]{2,1,0:T(8,128)(2,1)}), bf16[32,8,256]{2,1,0:T(8,128)(2,1)S(1)}, u32[]{:S(2)}, u32[]{:S(2)}) %all-to-all-start.2) | async-done | bytes 131104 | tf_op jit(solution)/shard_map/all_to_all | solution.py:117
  69.3 4.7 %all-to-all-start.3 = ((bf16[32,4,8,256]{3,2,1,0:T(8,128)(2,1)}), bf16[32,4,8,256]{3,2,1,0:T(8,128)(2,1)}, u32[]{:S(2)}, u32[]{:S(2)}) async-start(bf16[32,4,8,256]{3,2,1,0:T(8,128)(2,1)} %copy_bitcast_fusion.3), calls=%async_computation.3 | async-start | bytes 1048576 | tf_op jit(solution)/shard_map/all_to_all | solution.py:123
  75.9 5.7 %collective-permute-start.3 = (bf16[3,256,256]{2,1,0:T(8,128)(2,1)}, bf16[3,256,256]{2,1,0:T(8,128)(2,1)}, u32[]{:S(2)}, u32[]{:S(2)}) collective-permute-start(bf16[3,256,256]{2,1,0:T(8,128)(2,1)} %pad_maximum_fusion.5), channel_id=1, source_target_pairs={{0,24},{1,56},{2,88},{3,120},{4,152},{5,184},{6,216},{7,248},{8,0}... | collective-permute-start | bytes 1179656 | tf_op jit(solution)/shard_map/ppermute | solution.py:90
  92.9 18.0 %all-to-all-start.4 = ((bf16[32,4,8,256]{3,2,1,0:T(8,128)(2,1)}), bf16[32,4,8,256]{3,2,1,0:T(8,128)(2,1)}, u32[]{:S(2)}, u32[]{:S(2)}) async-start(bf16[32,4,8,256]{3,2,1,0:T(8,128)(2,1)} %broadcast_in_dim.15), calls=%async_computation.4 | async-start | bytes 1048576 | tf_op jit(solution)/shard_map/all_to_all | solution.py:126
  114.2 85.5 %all-to-all-done.4 = bf16[32,4,8,256]{3,2,1,0:T(8,128)(2,1)} async-done(((bf16[32,4,8,256]{3,2,1,0:T(8,128)(2,1)}), bf16[32,4,8,256]{3,2,1,0:T(8,128)(2,1)}, u32[]{:S(2)}, u32[]{:S(2)}) %all-to-all-start.4) | async-done | bytes 524320 | tf_op jit(solution)/shard_map/all_to_all | solution.py:126
  201.2 13.6 %all_to_all.75 = bf16[8,32,256]{2,1,0:T(8,128)(2,1)S(1)} all-to-all(bf16[8,32,256]{2,1,0:T(8,128)(2,1)S(1)} %bitcast.195), channel_id=1, replica_groups=mesh['prow'=8,'pcol'=32] {'prow'}, dimensions={0} | all-to-all | bytes 262144 | tf_op jit(solution)/shard_map/all_to_all | solution.py:131
  215.5 4.1 %all-to-all-start.6 = ((bf16[8,32,256]{2,1,0:T(8,128)(2,1)}), bf16[8,32,256]{2,1,0:T(8,128)(2,1)S(1)}, u32[]{:S(2)}, u32[]{:S(2)}) async-start(bf16[8,32,256]{2,1,0:T(8,128)(2,1)} %broadcast_in_dim.16), calls=%async_computation.6 | async-start | bytes 262144 | tf_op jit(solution)/shard_map/all_to_all | solution.py:134
  219.7 5.2 %all-to-all-done.6 = bf16[8,32,256]{2,1,0:T(8,128)(2,1)S(1)} async-done(((bf16[8,32,256]{2,1,0:T(8,128)(2,1)}), bf16[8,32,256]{2,1,0:T(8,128)(2,1)S(1)}, u32[]{:S(2)}, u32[]{:S(2)}) %all-to-all-start.6) | async-done | bytes 131104 | tf_op jit(solution)/shard_map/all_to_all | solution.py:134
  226.9 18.9 %all_to_all.76 = bf16[32,4,8,256]{3,2,1,0:T(8,128)(2,1)S(1)} all-to-all(bf16[32,4,8,256]{3,2,1,0:T(8,128)(2,1)S(1)} %copy_bitcast_fusion.2), channel_id=1, replica_groups=mesh['prow'=8,'pcol'=32] {'pcol'}, dimensions={0} | all-to-all | bytes 1048576 | tf_op jit(solution)/shard_map/all_to_all | solution.py:123
  246.0 21.2 %all_to_all.77 = bf16[32,4,8,256]{3,2,1,0:T(8,128)(2,1)S(1)} all-to-all(bf16[32,4,8,256]{3,2,1,0:T(8,128)(2,1)S(1)} %broadcast_in_dim.17), channel_id=1, replica_groups=mesh['prow'=8,'pcol'=32] {'pcol'}, dimensions={0} | all-to-all | bytes 1048576 | tf_op jit(solution)/shard_map/all_to_all | solution.py:126
  268.7 12.2 %all_to_all.78 = bf16[8,32,256]{2,1,0:T(8,128)(2,1)S(1)} all-to-all(bf16[8,32,256]{2,1,0:T(8,128)(2,1)S(1)} %bitcast.196), channel_id=1, replica_groups=mesh['prow'=8,'pcol'=32] {'prow'}, dimensions={0} | all-to-all | bytes 262144 | tf_op jit(solution)/shard_map/all_to_all | solution.py:131
  281.6 4.1 %all-to-all-start.10 = ((bf16[8,32,256]{2,1,0:T(8,128)(2,1)}), bf16[8,32,256]{2,1,0:T(8,128)(2,1)S(1)}, u32[]{:S(2)}, u32[]{:S(2)}) async-start(bf16[8,32,256]{2,1,0:T(8,128)(2,1)} %broadcast_in_dim.18), calls=%async_computation.10 | async-start | bytes 262144 | tf_op jit(solution)/shard_map/all_to_all | solution.py:134
  285.9 5.2 %all-to-all-done.10 = bf16[8,32,256]{2,1,0:T(8,128)(2,1)S(1)} async-done(((bf16[8,32,256]{2,1,0:T(8,128)(2,1)}), bf16[8,32,256]{2,1,0:T(8,128)(2,1)S(1)}, u32[]{:S(2)}, u32[]{:S(2)}) %all-to-all-start.10) | async-done | bytes 131104 | tf_op jit(solution)/shard_map/all_to_all | solution.py:134
  292.5 18.8 %all_to_all.79 = bf16[32,4,8,256]{3,2,1,0:T(8,128)(2,1)S(1)} all-to-all(bf16[32,4,8,256]{3,2,1,0:T(8,128)(2,1)S(1)} %bitcast.187), channel_id=1, replica_groups=mesh['prow'=8,'pcol'=32] {'pcol'}, dimensions={0} | all-to-all | bytes 1048576 | tf_op jit(solution)/shard_map/all_to_all | solution.py:123
  311.5 21.2 %all_to_all.80 = bf16[32,4,8,256]{3,2,1,0:T(8,128)(2,1)S(1)} all-to-all(bf16[32,4,8,256]{3,2,1,0:T(8,128)(2,1)S(1)} %broadcast_in_dim.19), channel_id=1, replica_groups=mesh['prow'=8,'pcol'=32] {'pcol'}, dimensions={0} | all-to-all | bytes 1048576 | tf_op jit(solution)/shard_map/all_to_all | solution.py:126
  334.1 12.2 %all_to_all.81 = bf16[8,32,256]{2,1,0:T(8,128)(2,1)S(1)} all-to-all(bf16[8,32,256]{2,1,0:T(8,128)(2,1)S(1)} %bitcast.194), channel_id=1, replica_groups=mesh['prow'=8,'pcol'=32] {'prow'}, dimensions={0} | all-to-all | bytes 262144 | tf_op jit(solution)/shard_map/all_to_all | solution.py:131
  346.3 8.5 %all_to_all.82 = bf16[8,32,256]{2,1,0:T(8,128)(2,1)S(1)} all-to-all(bf16[8,32,256]{2,1,0:T(8,128)(2,1)S(1)} %broadcast_in_dim.20), channel_id=1, replica_groups=mesh['prow'=8,'pcol'=32] {'prow'}, dimensions={0} | all-to-all | bytes 262144 | tf_op jit(solution)/shard_map/all_to_all | solution.py:134
  (97 shorter events, 37.6 us)
Async XLA Ops:
  0.0 7.7 %copy-start.9 = (s32[15]{0:T(128)S(1)}, s32[15]{0:T(128)}, u32[]{:S(2)}) copy-start(s32[15]{0:T(128)} %param.13) | copy-start | bytes 184
  0.0 7.7 %copy-start.10 = (s32[15]{0:T(128)S(1)}, s32[15]{0:T(128)}, u32[]{:S(2)}) copy-start(s32[15]{0:T(128)} %constant.244.clone) | copy-start | bytes 184
  0.0 8.7 %copy-start.7 = (bf16[4,1,256,256]{3,2,1,0:T(8,128)(2,1)S(1)}, bf16[4,1,256,256]{3,2,1,0:T(8,128)(2,1)}, u32[]{:S(2)}) copy-start(bf16[4,1,256,256]{3,2,1,0:T(8,128)(2,1)} %param.12) | copy-start | bytes 1572868
  7.7 15.4 %copy-start.8 = (s32[15,128]{1,0:T(8,128)S(1)}, s32[15,128]{1,0:T(8,128)}, u32[]{:S(2)}) copy-start(s32[15,128]{1,0:T(8,128)} %param.14) | copy-start | bytes 23044
  10.9 26.3 %all-to-all-start = ((bf16[32,4,8,256]{3,2,1,0:T(8,128)(2,1)}), bf16[32,4,8,256]{3,2,1,0:T(8,128)(2,1)S(1)}, u32[]{:S(2)}, u32[]{:S(2)}) async-start(bf16[32,4,8,256]{3,2,1,0:T(8,128)(2,1)} %bitcast.181), calls=%async_computation | async-start | bytes 1048576 | tf_op jit(solution)/shard_map/all_to_all | solution.py:112
  38.0 13.1 %all-to-all-start.1 = ((bf16[8,4,8,256]{3,2,1,0:T(8,128)(2,1)}), bf16[8,4,8,256]{3,2,1,0:T(8,128)(2,1)S(1)}, u32[]{:S(2)}, u32[]{:S(2)}) async-start(bf16[8,4,8,256]{3,2,1,0:T(8,128)(2,1)} %broadcast_in_dim.14), calls=%async_computation.1 | async-start | bytes 262144 | tf_op jit(solution)/shard_map/all_to_all | solution.py:115
  51.7 14.5 %all-to-all-start.2 = ((bf16[32,8,256]{2,1,0:T(8,128)(2,1)}), bf16[32,8,256]{2,1,0:T(8,128)(2,1)S(1)}, u32[]{:S(2)}, u32[]{:S(2)}) async-start(bf16[32,8,256]{2,1,0:T(8,128)(2,1)} %bitcast.10), calls=%async_computation.2 | async-start | bytes 262144 | tf_op jit(solution)/shard_map/all_to_all | solution.py:117
  69.3 18.4 %copy-start.4 = (bf16[1,256,256]{2,1,0:T(8,128)(2,1)S(1)}, bf16[1,256,256]{2,1,0:T(8,128)(2,1)}, u32[]{:S(2)}) copy-start(bf16[1,256,256]{2,1,0:T(8,128)(2,1)} %get-tuple-element.52) | copy-start | bytes 393220
  69.3 18.4 %copy-start.5 = (bf16[1,256,256]{2,1,0:T(8,128)(2,1)S(1)}, bf16[1,256,256]{2,1,0:T(8,128)(2,1)}, u32[]{:S(2)}) copy-start(bf16[1,256,256]{2,1,0:T(8,128)(2,1)} %get-tuple-element.69) | copy-start | bytes 393220
  69.3 21.6 %all-to-all-start.3 = ((bf16[32,4,8,256]{3,2,1,0:T(8,128)(2,1)}), bf16[32,4,8,256]{3,2,1,0:T(8,128)(2,1)}, u32[]{:S(2)}, u32[]{:S(2)}) async-start(bf16[32,4,8,256]{3,2,1,0:T(8,128)(2,1)} %copy_bitcast_fusion.3), calls=%async_computation.3 | async-start | bytes 1048576 | tf_op jit(solution)/shard_map/all_to_all | solution.py:123
  74.0 13.6 %copy-start.6 = (bf16[1,256,256]{2,1,0:T(8,128)(2,1)S(1)}, bf16[1,256,256]{2,1,0:T(8,128)(2,1)}, u32[]{:S(2)}) copy-start(bf16[1,256,256]{2,1,0:T(8,128)(2,1)} %get-tuple-element.44) | copy-start | bytes 393220
  75.9 35.2 %collective-permute-start.3 = (bf16[3,256,256]{2,1,0:T(8,128)(2,1)}, bf16[3,256,256]{2,1,0:T(8,128)(2,1)}, u32[]{:S(2)}, u32[]{:S(2)}) collective-permute-start(bf16[3,256,256]{2,1,0:T(8,128)(2,1)} %pad_maximum_fusion.5), channel_id=1, source_target_pairs={{0,24},{1,56},{2,88},{3,120},{4,152},{5,184},{6,216},{7,248},{8,0}... | collective-permute-start | bytes 1179656 | tf_op jit(solution)/shard_map/ppermute | solution.py:90
  83.5 27.6 %collective-permute-start.2 = (bf16[3,256,256]{2,1,0:T(8,128)(2,1)}, bf16[3,256,256]{2,1,0:T(8,128)(2,1)}, u32[]{:S(2)}, u32[]{:S(2)}) collective-permute-start(bf16[3,256,256]{2,1,0:T(8,128)(2,1)} %pad_maximum_fusion.4), channel_id=1, source_target_pairs={{0,16},{1,48},{2,80},{3,112},{4,144},{5,176},{6,208},{7,240},{8,24... | collective-permute-start | bytes 1179656 | tf_op jit(solution)/shard_map/ppermute | solution.py:90
  85.6 25.5 %collective-permute-start.1 = (bf16[3,256,256]{2,1,0:T(8,128)(2,1)}, bf16[3,256,256]{2,1,0:T(8,128)(2,1)}, u32[]{:S(2)}, u32[]{:S(2)}) collective-permute-start(bf16[3,256,256]{2,1,0:T(8,128)(2,1)} %pad_maximum_fusion.3), channel_id=1, source_target_pairs={{0,8},{1,40},{2,72},{3,104},{4,136},{5,168},{6,200},{7,232},{8,16}... | collective-permute-start | bytes 1179656 | tf_op jit(solution)/shard_map/ppermute | solution.py:90
  88.4 22.7 %collective-permute-start = (bf16[3,256,256]{2,1,0:T(8,128)(2,1)}, bf16[3,256,256]{2,1,0:T(8,128)(2,1)}, u32[]{:S(2)}, u32[]{:S(2)}) collective-permute-start(bf16[3,256,256]{2,1,0:T(8,128)(2,1)} %pad_maximum_fusion.2), channel_id=1, source_target_pairs={{0,0},{1,32},{2,64},{3,96},{4,128},{5,160},{6,192},{7,224},{8,8},{... | collective-permute-start | bytes 1179656 | tf_op jit(solution)/shard_map/ppermute | solution.py:90
  92.9 106.8 %all-to-all-start.4 = ((bf16[32,4,8,256]{3,2,1,0:T(8,128)(2,1)}), bf16[32,4,8,256]{3,2,1,0:T(8,128)(2,1)}, u32[]{:S(2)}, u32[]{:S(2)}) async-start(bf16[32,4,8,256]{3,2,1,0:T(8,128)(2,1)} %broadcast_in_dim.15), calls=%async_computation.4 | async-start | bytes 1048576 | tf_op jit(solution)/shard_map/all_to_all | solution.py:126
  215.5 9.4 %all-to-all-start.6 = ((bf16[8,32,256]{2,1,0:T(8,128)(2,1)}), bf16[8,32,256]{2,1,0:T(8,128)(2,1)S(1)}, u32[]{:S(2)}, u32[]{:S(2)}) async-start(bf16[8,32,256]{2,1,0:T(8,128)(2,1)} %broadcast_in_dim.16), calls=%async_computation.6 | async-start | bytes 262144 | tf_op jit(solution)/shard_map/all_to_all | solution.py:134
  224.9 1.7 copy-start.3
  226.7 40.5 %copy-start = (f32[8,256,256]{2,1,0:T(8,128)}, f32[8,256,256]{2,1,0:T(8,128)S(1)}, u32[]{:S(2)}) copy-start(f32[8,256,256]{2,1,0:T(8,128)S(1)} %slice_add_fusion) | copy-start | bytes 6291460
  245.9 45.1 %copy-start.2 = (f32[256,256]{1,0:T(8,128)S(1)}, f32[256,256]{1,0:T(8,128)}, u32[]{:S(2)}) copy-start(f32[256,256]{1,0:T(8,128)} %get-tuple-element.60) | copy-start | bytes 786436
  267.2 23.9 %copy-start.1 = (f32[8,256,256]{2,1,0:T(8,128)S(1)}, f32[8,256,256]{2,1,0:T(8,128)}, u32[]{:S(2)}) copy-start(f32[8,256,256]{2,1,0:T(8,128)} %copy-done) | copy-start | bytes 6291460
  281.6 9.4 %all-to-all-start.10 = ((bf16[8,32,256]{2,1,0:T(8,128)(2,1)}), bf16[8,32,256]{2,1,0:T(8,128)(2,1)S(1)}, u32[]{:S(2)}, u32[]{:S(2)}) async-start(bf16[8,32,256]{2,1,0:T(8,128)(2,1)} %broadcast_in_dim.18), calls=%async_computation.10 | async-start | bytes 262144 | tf_op jit(solution)/shard_map/all_to_all | solution.py:134

commit v3 on v2

--- a/solution.py
+++ b/solution.py
@@ -36,7 +36,9 @@
 
 
 def panel_products(tile_stack, live_bits, vector):
-    products = jnp.einsum("nxy,yw->nxw", tile_stack, vector, preferred_element_type=jnp.float32)
+    products = jnp.stack(
+        [jnp.dot(tile_stack[n], vector, preferred_element_type=jnp.float32) for n in range(tile_stack.shape[0])]
+    )
     return products * live_bits.astype(jnp.float32)[:, None, None]
 
 
@@ -85,6 +87,8 @@
         for p_src in range(prow_count):
             for c_src in range(pcol_count):
                 k_dst = (c_src // prow_count + shift) % level_groups
+                if c_src > k_dst * prow_count + p_src:
+                    continue
                 dst = (c_src % prow_count) * pcol_count + k_dst * prow_count + p_src
                 pairs.append((p_src * pcol_count + c_src, dst))
         shifted.append(lax.ppermute(sent, ("prow", "pcol"), pairs))

time: 357 us -> 376 us (1.053)
  matrix products: 10.9 us -> 35 us
  blocking collectives: 127 us -> 151 us
  waiting for transfers between devices: 118 us -> 94.5 us
  local copies, waits for them, and re-layouts: 17.9 us -> 10.6 us
  other arithmetic: 15.8 us -> 20.3 us
    all_to_all x1, waiting for transfers between devices: 85.5 us -> 59.7 us  [reduce_gather_pcol(): gathered = lax.all_to_all(spread, 'pcol', 0, 0, tiled=True)]
    dot_general x4 -> x28, matrix products: 6.39 us -> 30.7 us  [panel_products(): jnp.dot(tile_stack[n], vector, preferred_element_type=jnp.float32)]
    all_to_all x3, blocking collectives: 38 us -> 60.1 us  [reduce_gather_prow(): got = lax.all_to_all(pieces, 'prow', 0, 0, tiled=True)]
    all_to_all x1, starting transfers between devices: 18 us -> 7.42 us  [reduce_gather_pcol(): gathered = lax.all_to_all(spread, 'pcol', 0, 0, tiled=True)]
    unnamed x23 -> x10, local copies, waits for them, and re-layouts: 7.7 us -> 0.52 us
    ppermute x4, starting transfers between devices: 9.93 us -> 17 us  [local(): shifted.append(lax.ppermute(sent, ('prow', 'pcol'), pairs))]
  transfers between devices with their start and end apart: 11 -> 11, of which waited for: 6 -> 7; matrix products, arithmetic and copies ran while one was open for 5% -> 5% of each run, Pallas kernels for 0% -> 0%
where the time goes in v3:
time: 376 us; the launch traced here: 374 us
  blocking collectives  151 us (40%)
  waiting for transfers between devices  94.5 us (25%)
  starting transfers between devices  62.5 us (17%)
  matrix products  35 us (9%)
  other arithmetic  20.3 us (5%)
  local copies, waits for them, and re-layouts  10.6 us (3%)
    all_to_all x3, blocking collectives, reduce_gather_prow(): got = lax.all_to_all(pieces, 'prow', 0, 0, tiled=True)  60.1 us
    all_to_all x1, waiting for transfers between devices, reduce_gather_pcol(): gathered = lax.all_to_all(spread, 'pcol', 0, 0, tiled=True)  59.7 us
    all_to_all x2, blocking collectives, reduce_gather_pcol(): gathered = lax.all_to_all(spread, 'pcol', 0, 0, tiled=True)  42.3 us
    all_to_all x2, blocking collectives, reduce_gather_pcol(): got = lax.all_to_all(pieces, 'pcol', 0, 0, tiled=True)  39.7 us
    dot_general x28, matrix products, panel_products(): jnp.dot(tile_stack[n], vector, preferred_element_type=jnp.float32)  30.7 us
    ppermute x4, starting transfers between devices, local(): shifted.append(lax.ppermute(sent, ('prow', 'pcol'), pairs))  17 us
    all_to_all x1, starting transfers between devices, reduce_route(): got = lax.all_to_all(pieces, 'pcol', 0, 0, tiled=True)  12 us
    all_to_all x2, waiting for transfers between devices, reduce_gather_prow(): gathered = lax.all_to_all(spread, 'prow', 0, 0, tiled=True)  10.4 us
  transfers between devices with their start and end apart: 11, of which 7 were waited for; matrix products, arithmetic and copies ran while one was open for 5% of the time, Pallas kernels for 0%

profile of v3, /device:TPU:1, one launch (start us, length us, event | category | flops | bytes accessed | tf_op | source)
XLA Modules:
  0.0 374.3 jit_solution(3898722056560657459)
XLA Ops:
  8.0 12.0 %all-to-all-start = ((bf16[32,4,8,256]{3,2,1,0:T(8,128)(2,1)}), bf16[32,4,8,256]{3,2,1,0:T(8,128)(2,1)S(1)}, u32[]{:S(2)}, u32[]{:S(2)}) async-start(bf16[32,4,8,256]{3,2,1,0:T(8,128)(2,1)} %copy.21), calls=%async_computation | async-start | bytes 1048576 | tf_op jit(solution)/shard_map/all_to_all | solution.py:116
  20.5 3.5 fusion.73
  25.0 9.3 %all-to-all-done = bf16[32,4,8,256]{3,2,1,0:T(8,128)(2,1)S(1)} async-done(((bf16[32,4,8,256]{3,2,1,0:T(8,128)(2,1)}), bf16[32,4,8,256]{3,2,1,0:T(8,128)(2,1)S(1)}, u32[]{:S(2)}, u32[]{:S(2)}) %all-to-all-start) | async-done | bytes 524320 | tf_op jit(solution)/shard_map/all_to_all | solution.py:116
  35.1 7.8 %all-to-all-start.1 = ((bf16[8,4,8,256]{3,2,1,0:T(8,128)(2,1)}), bf16[8,4,8,256]{3,2,1,0:T(8,128)(2,1)S(1)}, u32[]{:S(2)}, u32[]{:S(2)}) async-start(bf16[8,4,8,256]{3,2,1,0:T(8,128)(2,1)} %broadcast_in_dim.14), calls=%async_computation.1 | async-start | bytes 262144 | tf_op jit(solution)/shard_map/all_to_all | solution.py:119
  43.7 4.5 %all-to-all-done.1 = bf16[8,4,8,256]{3,2,1,0:T(8,128)(2,1)S(1)} async-done(((bf16[8,4,8,256]{3,2,1,0:T(8,128)(2,1)}), bf16[8,4,8,256]{3,2,1,0:T(8,128)(2,1)S(1)}, u32[]{:S(2)}, u32[]{:S(2)}) %all-to-all-start.1) | async-done | bytes 131104 | tf_op jit(solution)/shard_map/all_to_all | solution.py:119
  48.9 5.3 %all-to-all-start.2 = ((bf16[32,8,256]{2,1,0:T(8,128)(2,1)}), bf16[32,8,256]{2,1,0:T(8,128)(2,1)S(1)}, u32[]{:S(2)}, u32[]{:S(2)}) async-start(bf16[32,8,256]{2,1,0:T(8,128)(2,1)} %bitcast.17), calls=%async_computation.2 | async-start | bytes 262144 | tf_op jit(solution)/shard_map/all_to_all | solution.py:121
  55.1 8.2 %all-to-all-done.2 = bf16[32,8,256]{2,1,0:T(8,128)(2,1)S(1)} async-done(((bf16[32,8,256]{2,1,0:T(8,128)(2,1)}), bf16[32,8,256]{2,1,0:T(8,128)(2,1)S(1)}, u32[]{:S(2)}, u32[]{:S(2)}) %all-to-all-start.2) | async-done | bytes 131104 | tf_op jit(solution)/shard_map/all_to_all | solution.py:121
  77.9 4.6 %all-to-all-start.3 = ((bf16[32,4,8,256]{3,2,1,0:T(8,128)(2,1)}), bf16[32,4,8,256]{3,2,1,0:T(8,128)(2,1)}, u32[]{:S(2)}, u32[]{:S(2)}) async-start(bf16[32,4,8,256]{3,2,1,0:T(8,128)(2,1)} %copy_bitcast_fusion.2), calls=%async_computation.3 | async-start | bytes 1048576 | tf_op jit(solution)/shard_map/all_to_all | solution.py:127
  84.4 8.4 %collective-permute-start.3 = (bf16[3,256,256]{2,1,0:T(8,128)(2,1)}, bf16[3,256,256]{2,1,0:T(8,128)(2,1)}, u32[]{:S(2)}, u32[]{:S(2)}) collective-permute-start(bf16[3,256,256]{2,1,0:T(8,128)(2,1)} %pad_maximum_fusion.5), channel_id=1, source_target_pairs={{0,24},{1,56},{2,88},{3,120},{4,152},{5,184},{6,216},{7,248},{32,2... | collective-permute-start | bytes 1179656 | tf_op jit(solution)/shard_map/ppermute | solution.py:94
  102.4 4.5 %collective-permute-start = (bf16[3,256,256]{2,1,0:T(8,128)(2,1)}, bf16[3,256,256]{2,1,0:T(8,128)(2,1)}, u32[]{:S(2)}, u32[]{:S(2)}) collective-permute-start(bf16[3,256,256]{2,1,0:T(8,128)(2,1)} %pad_maximum_fusion.2), channel_id=1, source_target_pairs={{0,0},{8,8},{16,16},{24,24},{32,1},{33,33},{40,9},{41,41},{48,17},... | collective-permute-start | bytes 1179656 | tf_op jit(solution)/shard_map/ppermute | solution.py:94
  109.4 7.4 %all-to-all-start.4 = ((bf16[32,4,8,256]{3,2,1,0:T(8,128)(2,1)}), bf16[32,4,8,256]{3,2,1,0:T(8,128)(2,1)}, u32[]{:S(2)}, u32[]{:S(2)}) async-start(bf16[32,4,8,256]{3,2,1,0:T(8,128)(2,1)} %broadcast_in_dim.15), calls=%async_computation.4 | async-start | bytes 1048576 | tf_op jit(solution)/shard_map/all_to_all | solution.py:130
  122.4 59.7 %all-to-all-done.4 = bf16[32,4,8,256]{3,2,1,0:T(8,128)(2,1)} async-done(((bf16[32,4,8,256]{3,2,1,0:T(8,128)(2,1)}), bf16[32,4,8,256]{3,2,1,0:T(8,128)(2,1)}, u32[]{:S(2)}, u32[]{:S(2)}) %all-to-all-start.4) | async-done | bytes 524320 | tf_op jit(solution)/shard_map/all_to_all | solution.py:130
  183.7 35.6 %all_to_all.75 = bf16[8,32,256]{2,1,0:T(8,128)(2,1)S(1)} all-to-all(bf16[8,32,256]{2,1,0:T(8,128)(2,1)S(1)} %bitcast.457), channel_id=1, replica_groups=mesh['prow'=8,'pcol'=32] {'prow'}, dimensions={0} | all-to-all | bytes 262144 | tf_op jit(solution)/shard_map/all_to_all | solution.py:135
  220.0 4.1 %all-to-all-start.6 = ((bf16[8,32,256]{2,1,0:T(8,128)(2,1)}), bf16[8,32,256]{2,1,0:T(8,128)(2,1)S(1)}, u32[]{:S(2)}, u32[]{:S(2)}) async-start(bf16[8,32,256]{2,1,0:T(8,128)(2,1)} %broadcast_in_dim.16), calls=%async_computation.6 | async-start | bytes 262144 | tf_op jit(solution)/shard_map/all_to_all | solution.py:138
  224.2 5.2 %all-to-all-done.6 = bf16[8,32,256]{2,1,0:T(8,128)(2,1)S(1)} async-done(((bf16[8,32,256]{2,1,0:T(8,128)(2,1)}), bf16[8,32,256]{2,1,0:T(8,128)(2,1)S(1)}, u32[]{:S(2)}, u32[]{:S(2)}) %all-to-all-start.6) | async-done | bytes 131104 | tf_op jit(solution)/shard_map/all_to_all | solution.py:138
  239.4 20.9 %all_to_all.76 = bf16[32,4,8,256]{3,2,1,0:T(8,128)(2,1)S(1)} all-to-all(bf16[32,4,8,256]{3,2,1,0:T(8,128)(2,1)S(1)} %copy_bitcast_fusion.1), channel_id=1, replica_groups=mesh['prow'=8,'pcol'=32] {'pcol'}, dimensions={0} | all-to-all | bytes 1048576 | tf_op jit(solution)/shard_map/all_to_all | solution.py:127
  260.4 21.2 %all_to_all.77 = bf16[32,4,8,256]{3,2,1,0:T(8,128)(2,1)S(1)} all-to-all(bf16[32,4,8,256]{3,2,1,0:T(8,128)(2,1)S(1)} %broadcast_in_dim.17), channel_id=1, replica_groups=mesh['prow'=8,'pcol'=32] {'pcol'}, dimensions={0} | all-to-all | bytes 1048576 | tf_op jit(solution)/shard_map/all_to_all | solution.py:130
  283.0 12.3 %all_to_all.78 = bf16[8,32,256]{2,1,0:T(8,128)(2,1)S(1)} all-to-all(bf16[8,32,256]{2,1,0:T(8,128)(2,1)S(1)} %bitcast.458), channel_id=1, replica_groups=mesh['prow'=8,'pcol'=32] {'prow'}, dimensions={0} | all-to-all | bytes 262144 | tf_op jit(solution)/shard_map/all_to_all | solution.py:135
  296.0 4.1 %all-to-all-start.10 = ((bf16[8,32,256]{2,1,0:T(8,128)(2,1)}), bf16[8,32,256]{2,1,0:T(8,128)(2,1)S(1)}, u32[]{:S(2)}, u32[]{:S(2)}) async-start(bf16[8,32,256]{2,1,0:T(8,128)(2,1)} %broadcast_in_dim.18), calls=%async_computation.10 | async-start | bytes 262144 | tf_op jit(solution)/shard_map/all_to_all | solution.py:138
  300.3 5.2 %all-to-all-done.10 = bf16[8,32,256]{2,1,0:T(8,128)(2,1)S(1)} async-done(((bf16[8,32,256]{2,1,0:T(8,128)(2,1)}), bf16[8,32,256]{2,1,0:T(8,128)(2,1)S(1)}, u32[]{:S(2)}, u32[]{:S(2)}) %all-to-all-start.10) | async-done | bytes 131104 | tf_op jit(solution)/shard_map/all_to_all | solution.py:138
  311.1 18.8 %all_to_all.79 = bf16[32,4,8,256]{3,2,1,0:T(8,128)(2,1)S(1)} all-to-all(bf16[32,4,8,256]{3,2,1,0:T(8,128)(2,1)S(1)} %copy_bitcast_fusion), channel_id=1, replica_groups=mesh['prow'=8,'pcol'=32] {'pcol'}, dimensions={0} | all-to-all | bytes 1048576 | tf_op jit(solution)/shard_map/all_to_all | solution.py:127
  330.1 21.2 %all_to_all.80 = bf16[32,4,8,256]{3,2,1,0:T(8,128)(2,1)S(1)} all-to-all(bf16[32,4,8,256]{3,2,1,0:T(8,128)(2,1)S(1)} %broadcast_in_dim.19), channel_id=1, replica_groups=mesh['prow'=8,'pcol'=32] {'pcol'}, dimensions={0} | all-to-all | bytes 1048576 | tf_op jit(solution)/shard_map/all_to_all | solution.py:130
  352.6 12.2 %all_to_all.81 = bf16[8,32,256]{2,1,0:T(8,128)(2,1)S(1)} all-to-all(bf16[8,32,256]{2,1,0:T(8,128)(2,1)S(1)} %bitcast.456), channel_id=1, replica_groups=mesh['prow'=8,'pcol'=32] {'prow'}, dimensions={0} | all-to-all | bytes 262144 | tf_op jit(solution)/shard_map/all_to_all | solution.py:135
  364.9 8.5 %all_to_all.82 = bf16[8,32,256]{2,1,0:T(8,128)(2,1)S(1)} all-to-all(bf16[8,32,256]{2,1,0:T(8,128)(2,1)S(1)} %broadcast_in_dim.20), channel_id=1, replica_groups=mesh['prow'=8,'pcol'=32] {'prow'}, dimensions={0} | all-to-all | bytes 262144 | tf_op jit(solution)/shard_map/all_to_all | solution.py:138
  (111 shorter events, 68.8 us)
Async XLA Ops:
  0.0 20.2 %copy-start.4 = (s32[15,128]{1,0:T(8,128)S(1)}, s32[15,128]{1,0:T(8,128)}, u32[]{:S(2)}) copy-start(s32[15,128]{1,0:T(8,128)} %param.14) | copy-start | bytes 23044
  8.0 26.3 %all-to-all-start = ((bf16[32,4,8,256]{3,2,1,0:T(8,128)(2,1)}), bf16[32,4,8,256]{3,2,1,0:T(8,128)(2,1)S(1)}, u32[]{:S(2)}, u32[]{:S(2)}) async-start(bf16[32,4,8,256]{3,2,1,0:T(8,128)(2,1)} %copy.21), calls=%async_computation | async-start | bytes 1048576 | tf_op jit(solution)/shard_map/all_to_all | solution.py:116
  23.9 30.3 %copy-start.2 = (bf16[4,1,256,256]{3,2,1,0:T(8,128)(2,1)S(1)}, bf16[4,1,256,256]{3,2,1,0:T(8,128)(2,1)}, u32[]{:S(2)}) copy-start(bf16[4,1,256,256]{3,2,1,0:T(8,128)(2,1)} %param.12) | copy-start | bytes 1572868
  35.1 13.1 %all-to-all-start.1 = ((bf16[8,4,8,256]{3,2,1,0:T(8,128)(2,1)}), bf16[8,4,8,256]{3,2,1,0:T(8,128)(2,1)S(1)}, u32[]{:S(2)}, u32[]{:S(2)}) async-start(bf16[8,4,8,256]{3,2,1,0:T(8,128)(2,1)} %broadcast_in_dim.14), calls=%async_computation.1 | async-start | bytes 262144 | tf_op jit(solution)/shard_map/all_to_all | solution.py:119
  48.9 14.5 %all-to-all-start.2 = ((bf16[32,8,256]{2,1,0:T(8,128)(2,1)}), bf16[32,8,256]{2,1,0:T(8,128)(2,1)S(1)}, u32[]{:S(2)}, u32[]{:S(2)}) async-start(bf16[32,8,256]{2,1,0:T(8,128)(2,1)} %bitcast.17), calls=%async_computation.2 | async-start | bytes 262144 | tf_op jit(solution)/shard_map/all_to_all | solution.py:121
  77.9 29.4 %all-to-all-start.3 = ((bf16[32,4,8,256]{3,2,1,0:T(8,128)(2,1)}), bf16[32,4,8,256]{3,2,1,0:T(8,128)(2,1)}, u32[]{:S(2)}, u32[]{:S(2)}) async-start(bf16[32,4,8,256]{3,2,1,0:T(8,128)(2,1)} %copy_bitcast_fusion.2), calls=%async_computation.3 | async-start | bytes 1048576 | tf_op jit(solution)/shard_map/all_to_all | solution.py:127
  84.4 32.7 %collective-permute-start.3 = (bf16[3,256,256]{2,1,0:T(8,128)(2,1)}, bf16[3,256,256]{2,1,0:T(8,128)(2,1)}, u32[]{:S(2)}, u32[]{:S(2)}) collective-permute-start(bf16[3,256,256]{2,1,0:T(8,128)(2,1)} %pad_maximum_fusion.5), channel_id=1, source_target_pairs={{0,24},{1,56},{2,88},{3,120},{4,152},{5,184},{6,216},{7,248},{32,2... | collective-permute-start | bytes 1179656 | tf_op jit(solution)/shard_map/ppermute | solution.py:94
  94.6 22.4 %collective-permute-start.2 = (bf16[3,256,256]{2,1,0:T(8,128)(2,1)}, bf16[3,256,256]{2,1,0:T(8,128)(2,1)}, u32[]{:S(2)}, u32[]{:S(2)}) collective-permute-start(bf16[3,256,256]{2,1,0:T(8,128)(2,1)} %pad_maximum_fusion.4), channel_id=1, source_target_pairs={{0,16},{1,48},{2,80},{3,112},{4,144},{5,176},{6,208},{7,240},{8,24... | collective-permute-start | bytes 1179656 | tf_op jit(solution)/shard_map/ppermute | solution.py:94
  98.5 18.6 %collective-permute-start.1 = (bf16[3,256,256]{2,1,0:T(8,128)(2,1)}, bf16[3,256,256]{2,1,0:T(8,128)(2,1)}, u32[]{:S(2)}, u32[]{:S(2)}) collective-permute-start(bf16[3,256,256]{2,1,0:T(8,128)(2,1)} %pad_maximum_fusion.3), channel_id=1, source_target_pairs={{0,8},{1,40},{2,72},{3,104},{4,136},{5,168},{6,200},{7,232},{8,16}... | collective-permute-start | bytes 1179656 | tf_op jit(solution)/shard_map/ppermute | solution.py:94
  102.4 17.0 %collective-permute-start = (bf16[3,256,256]{2,1,0:T(8,128)(2,1)}, bf16[3,256,256]{2,1,0:T(8,128)(2,1)}, u32[]{:S(2)}, u32[]{:S(2)}) collective-permute-start(bf16[3,256,256]{2,1,0:T(8,128)(2,1)} %pad_maximum_fusion.2), channel_id=1, source_target_pairs={{0,0},{8,8},{16,16},{24,24},{32,1},{33,33},{40,9},{41,41},{48,17},... | collective-permute-start | bytes 1179656 | tf_op jit(solution)/shard_map/ppermute | solution.py:94
  109.4 72.8 %all-to-all-start.4 = ((bf16[32,4,8,256]{3,2,1,0:T(8,128)(2,1)}), bf16[32,4,8,256]{3,2,1,0:T(8,128)(2,1)}, u32[]{:S(2)}, u32[]{:S(2)}) async-start(bf16[32,4,8,256]{3,2,1,0:T(8,128)(2,1)} %broadcast_in_dim.15), calls=%async_computation.4 | async-start | bytes 1048576 | tf_op jit(solution)/shard_map/all_to_all | solution.py:130
  220.0 9.4 %all-to-all-start.6 = ((bf16[8,32,256]{2,1,0:T(8,128)(2,1)}), bf16[8,32,256]{2,1,0:T(8,128)(2,1)S(1)}, u32[]{:S(2)}, u32[]{:S(2)}) async-start(bf16[8,32,256]{2,1,0:T(8,128)(2,1)} %broadcast_in_dim.16), calls=%async_computation.6 | async-start | bytes 262144 | tf_op jit(solution)/shard_map/all_to_all | solution.py:138
  238.2 1.0 copy-start.3
  238.6 44.4 %copy-start = (f32[8,256,256]{2,1,0:T(8,128)}, f32[8,256,256]{2,1,0:T(8,128)S(1)}, u32[]{:S(2)}) copy-start(f32[8,256,256]{2,1,0:T(8,128)S(1)} %slice_add_fusion) | copy-start | bytes 6291460
  283.0 26.9 %copy-start.1 = (f32[8,256,256]{2,1,0:T(8,128)S(1)}, f32[8,256,256]{2,1,0:T(8,128)}, u32[]{:S(2)}) copy-start(f32[8,256,256]{2,1,0:T(8,128)} %copy-done) | copy-start | bytes 6291460
  296.0 9.4 %all-to-all-start.10 = ((bf16[8,32,256]{2,1,0:T(8,128)(2,1)}), bf16[8,32,256]{2,1,0:T(8,128)(2,1)S(1)}, u32[]{:S(2)}, u32[]{:S(2)}) async-start(bf16[8,32,256]{2,1,0:T(8,128)(2,1)} %broadcast_in_dim.18), calls=%async_computation.10 | async-start | bytes 262144 | tf_op jit(solution)/shard_map/all_to_all | solution.py:138

commit v4 on v1

--- a/solution.py
+++ b/solution.py
@@ -52,6 +52,10 @@
     level_rows = pcol_count // prow_count
     piece_rows = block_size // pcol_count
     tile_grid = factor.reshape(rows_local, cols_local, block_size, block_size)
+    tile_rows = factor.reshape(rows_local, cols_local * block_size, block_size)
+
+    def column_tiles(first, col):
+        return tile_rows[first:, col * block_size:(col + 1) * block_size]
     columns_in = right_side.reshape(cols_local, block_size, right_side.shape[3])
     block_node = node_table(node_blocks, total_blocks)
     row_ids = jnp.arange(rows_local, dtype=jnp.int32) * prow_count + prow_index
@@ -92,7 +96,7 @@
             update = reduce_route(partial_value[first_row:after_row]).astype(jnp.float32)
             rhs_column = (columns_in[section_now].astype(jnp.float32) - update).astype(jnp.bfloat16)
         diag_terms = panel_products(
-            tile_grid[first_row:after_row, section_now],
+            column_tiles(first_row, section_now)[:level_rows],
             diag_bits[first_row:after_row, section_now],
             rhs_column,
         )
@@ -100,7 +104,7 @@
         solved_list.append(solved)
         if section_now + 1 < LEVELS:
             update_terms = panel_products(
-                tile_grid[after_row:, section_now], front_bits[after_row:, section_now], solved
+                column_tiles(after_row, section_now), front_bits[after_row:, section_now], solved
             )
             partial_value = partial_value.at[after_row:].add(update_terms)
     solution = jnp.stack(solved_list)

time: 346 us -> 339 us (0.980)
  local copies, waits for them, and re-layouts: 13 us -> 5.34 us
    unnamed x9 -> x12, local copies, waits for them, and re-layouts: 9 us -> 1.36 us
where the time goes in v4:
time: 339 us; the launch traced here: 337 us
  blocking collectives  232 us (68%)
  waiting for transfers between devices  45.8 us (14%)
  starting transfers between devices  35.6 us (11%)
  matrix products  10.4 us (3%)
  other arithmetic  7.72 us (2%)
  local copies, waits for them, and re-layouts  5.34 us (2%)
    all_to_all x6, blocking collectives, reduce_route(): got = lax.all_to_all(pieces, 'pcol', 0, 0, tiled=True)  98 us
    all_to_all x6, blocking collectives, reduce_route(): gathered = lax.all_to_all(spread, 'prow', 0, 0, tiled=True)  77.1 us
    all_to_all x4, blocking collectives, reduce_route(): arrived = lax.all_to_all(by_row, 'pcol', 0, 0, tiled=True)  56.8 us
    all_to_all x3, waiting for transfers between devices, reduce_route(): arrived = lax.all_to_all(by_row, 'pcol', 0, 0, tiled=True)  26.4 us
    all_to_all x3, starting transfers between devices, reduce_route(): arrived = lax.all_to_all(by_row, 'pcol', 0, 0, tiled=True)  15.8 us
    all_to_all x1, waiting for transfers between devices, reduce_route(): got = lax.all_to_all(pieces, 'pcol', 0, 0, tiled=True)  14.2 us
    all_to_all x1, starting transfers between devices, reduce_route(): got = lax.all_to_all(pieces, 'pcol', 0, 0, tiled=True)  12 us
    dot_general x7, matrix products, panel_products(): jnp.einsum('nxy,yw->nxw', tile_stack, vector, preferred_element_type=jnp....  10.4 us
  transfers between devices with their start and end apart: 5, of which 5 were waited for; matrix products, arithmetic and copies ran while one was open for 0% of the time, Pallas kernels for 0%

profile of v4, /device:TPU:1, one launch (start us, length us, event | category | flops | bytes accessed | tf_op | source)
XLA Modules:
  0.0 337.1 jit_solution(3370209411748571198)
XLA Ops:
  5.2 12.0 %all-to-all-start = ((bf16[32,4,8,256]{3,2,1,0:T(8,128)(2,1)}), bf16[32,4,8,256]{3,2,1,0:T(8,128)(2,1)S(1)}, u32[]{:S(2)}, u32[]{:S(2)}) async-start(bf16[32,4,8,256]{3,2,1,0:T(8,128)(2,1)} %bitcast.161), calls=%async_computation | async-start | bytes 1048576 | tf_op jit(solution)/shard_map/all_to_all | solution.py:79
  17.3 14.2 %all-to-all-done = bf16[32,4,8,256]{3,2,1,0:T(8,128)(2,1)S(1)} async-done(((bf16[32,4,8,256]{3,2,1,0:T(8,128)(2,1)}), bf16[32,4,8,256]{3,2,1,0:T(8,128)(2,1)S(1)}, u32[]{:S(2)}, u32[]{:S(2)}) %all-to-all-start) | async-done | bytes 524320 | tf_op jit(solution)/shard_map/all_to_all | solution.py:79
  32.3 7.8 %all-to-all-start.1 = ((bf16[8,4,8,256]{3,2,1,0:T(8,128)(2,1)}), bf16[8,4,8,256]{3,2,1,0:T(8,128)(2,1)S(1)}, u32[]{:S(2)}, u32[]{:S(2)}) async-start(bf16[8,4,8,256]{3,2,1,0:T(8,128)(2,1)} %broadcast_in_dim.14), calls=%async_computation.1 | async-start | bytes 262144 | tf_op jit(solution)/shard_map/all_to_all | solution.py:82
  46.0 5.3 %all-to-all-start.2 = ((bf16[32,8,256]{2,1,0:T(8,128)(2,1)}), bf16[32,8,256]{2,1,0:T(8,128)(2,1)S(1)}, u32[]{:S(2)}, u32[]{:S(2)}) async-start(bf16[32,8,256]{2,1,0:T(8,128)(2,1)} %bitcast.9), calls=%async_computation.2 | async-start | bytes 262144 | tf_op jit(solution)/shard_map/all_to_all | solution.py:84
  51.6 8.9 %all-to-all-done.2 = bf16[32,8,256]{2,1,0:T(8,128)(2,1)S(1)} async-done(((bf16[32,8,256]{2,1,0:T(8,128)(2,1)}), bf16[32,8,256]{2,1,0:T(8,128)(2,1)S(1)}, u32[]{:S(2)}, u32[]{:S(2)}) %all-to-all-start.2) | async-done | bytes 131104 | tf_op jit(solution)/shard_map/all_to_all | solution.py:84
  62.6 16.4 %all_to_all.105 = bf16[32,4,8,256]{3,2,1,0:T(8,128)(2,1)} all-to-all(bf16[32,4,8,256]{3,2,1,0:T(8,128)(2,1)S(1)} %copy_bitcast_fusion.5), channel_id=1, replica_groups=mesh['prow'=8,'pcol'=32] {'pcol'}, dimensions={0} | all-to-all | bytes 1048576 | tf_op jit(solution)/shard_map/all_to_all | solution.py:79
  80.2 12.9 %all_to_all.106 = bf16[8,4,8,256]{3,2,1,0:T(8,128)(2,1)S(1)} all-to-all(bf16[8,4,8,256]{3,2,1,0:T(8,128)(2,1)S(1)} %broadcast_in_dim.15), channel_id=1, replica_groups=mesh['prow'=8,'pcol'=32] {'prow'}, dimensions={0} | all-to-all | bytes 262144 | tf_op jit(solution)/shard_map/all_to_all | solution.py:82
  93.0 14.1 %all_to_all.107 = bf16[32,8,256]{2,1,0:T(8,128)(2,1)S(1)} all-to-all(bf16[32,8,256]{2,1,0:T(8,128)(2,1)S(1)} %bitcast.176), channel_id=1, replica_groups=mesh['prow'=8,'pcol'=32] {'pcol'}, dimensions={0} | all-to-all | bytes 262144 | tf_op jit(solution)/shard_map/all_to_all | solution.py:84
  108.7 16.4 %all_to_all.108 = bf16[32,4,8,256]{3,2,1,0:T(8,128)(2,1)} all-to-all(bf16[32,4,8,256]{3,2,1,0:T(8,128)(2,1)S(1)} %bitcast.169), channel_id=1, replica_groups=mesh['prow'=8,'pcol'=32] {'pcol'}, dimensions={0} | all-to-all | bytes 1048576 | tf_op jit(solution)/shard_map/all_to_all | solution.py:79
  126.3 12.8 %all_to_all.109 = bf16[8,4,8,256]{3,2,1,0:T(8,128)(2,1)S(1)} all-to-all(bf16[8,4,8,256]{3,2,1,0:T(8,128)(2,1)S(1)} %broadcast_in_dim.16), channel_id=1, replica_groups=mesh['prow'=8,'pcol'=32] {'prow'}, dimensions={0} | all-to-all | bytes 262144 | tf_op jit(solution)/shard_map/all_to_all | solution.py:82
  145.0 9.1 %all-to-all-done.8 = bf16[32,8,256]{2,1,0:T(8,128)(2,1)S(1)} async-done(((bf16[32,8,256]{2,1,0:T(8,128)(2,1)}), bf16[32,8,256]{2,1,0:T(8,128)(2,1)S(1)}, u32[]{:S(2)}, u32[]{:S(2)}) %all-to-all-start.8) | async-done | bytes 131104 | tf_op jit(solution)/shard_map/all_to_all | solution.py:84
  157.2 16.4 %all_to_all.110 = bf16[32,4,8,256]{3,2,1,0:T(8,128)(2,1)S(1)} all-to-all(bf16[32,4,8,256]{3,2,1,0:T(8,128)(2,1)S(1)} %copy_bitcast_fusion.3), channel_id=1, replica_groups=mesh['prow'=8,'pcol'=32] {'pcol'}, dimensions={0} | all-to-all | bytes 1048576 | tf_op jit(solution)/shard_map/all_to_all | solution.py:79
  173.7 13.0 %all_to_all.111 = bf16[8,4,8,256]{3,2,1,0:T(8,128)(2,1)S(1)} all-to-all(bf16[8,4,8,256]{3,2,1,0:T(8,128)(2,1)S(1)} %broadcast_in_dim.17), channel_id=1, replica_groups=mesh['prow'=8,'pcol'=32] {'prow'}, dimensions={0} | all-to-all | bytes 262144 | tf_op jit(solution)/shard_map/all_to_all | solution.py:82
  186.7 14.2 %all_to_all.112 = bf16[32,8,256]{2,1,0:T(8,128)(2,1)S(1)} all-to-all(bf16[32,8,256]{2,1,0:T(8,128)(2,1)S(1)} %bitcast.177), channel_id=1, replica_groups=mesh['prow'=8,'pcol'=32] {'pcol'}, dimensions={0} | all-to-all | bytes 262144 | tf_op jit(solution)/shard_map/all_to_all | solution.py:84
  202.3 16.3 %all_to_all.113 = bf16[32,4,8,256]{3,2,1,0:T(8,128)(2,1)S(1)} all-to-all(bf16[32,4,8,256]{3,2,1,0:T(8,128)(2,1)S(1)} %bitcast.170), channel_id=1, replica_groups=mesh['prow'=8,'pcol'=32] {'pcol'}, dimensions={0} | all-to-all | bytes 1048576 | tf_op jit(solution)/shard_map/all_to_all | solution.py:79
  218.7 12.8 %all_to_all.114 = bf16[8,4,8,256]{3,2,1,0:T(8,128)(2,1)S(1)} all-to-all(bf16[8,4,8,256]{3,2,1,0:T(8,128)(2,1)S(1)} %broadcast_in_dim.18), channel_id=1, replica_groups=mesh['prow'=8,'pcol'=32] {'prow'}, dimensions={0} | all-to-all | bytes 262144 | tf_op jit(solution)/shard_map/all_to_all | solution.py:82
  232.2 5.3 %all-to-all-start.14 = ((bf16[32,8,256]{2,1,0:T(8,128)(2,1)}), bf16[32,8,256]{2,1,0:T(8,128)(2,1)S(1)}, u32[]{:S(2)}, u32[]{:S(2)}) async-start(bf16[32,8,256]{2,1,0:T(8,128)(2,1)} %bitcast.45), calls=%async_computation.14 | async-start | bytes 262144 | tf_op jit(solution)/shard_map/all_to_all | solution.py:84
  238.2 8.4 %all-to-all-done.14 = bf16[32,8,256]{2,1,0:T(8,128)(2,1)S(1)} async-done(((bf16[32,8,256]{2,1,0:T(8,128)(2,1)}), bf16[32,8,256]{2,1,0:T(8,128)(2,1)S(1)}, u32[]{:S(2)}, u32[]{:S(2)}) %all-to-all-start.14) | async-done | bytes 131104 | tf_op jit(solution)/shard_map/all_to_all | solution.py:84
  248.0 16.3 %all_to_all.115 = bf16[32,4,8,256]{3,2,1,0:T(8,128)(2,1)S(1)} all-to-all(bf16[32,4,8,256]{3,2,1,0:T(8,128)(2,1)S(1)} %bitcast.171), channel_id=1, replica_groups=mesh['prow'=8,'pcol'=32] {'pcol'}, dimensions={0} | all-to-all | bytes 1048576 | tf_op jit(solution)/shard_map/all_to_all | solution.py:79
  264.4 12.8 %all_to_all.116 = bf16[8,4,8,256]{3,2,1,0:T(8,128)(2,1)S(1)} all-to-all(bf16[8,4,8,256]{3,2,1,0:T(8,128)(2,1)S(1)} %broadcast_in_dim.19), channel_id=1, replica_groups=mesh['prow'=8,'pcol'=32] {'prow'}, dimensions={0} | all-to-all | bytes 262144 | tf_op jit(solution)/shard_map/all_to_all | solution.py:82
  277.2 14.2 %all_to_all.117 = bf16[32,8,256]{2,1,0:T(8,128)(2,1)S(1)} all-to-all(bf16[32,8,256]{2,1,0:T(8,128)(2,1)S(1)} %bitcast.178), channel_id=1, replica_groups=mesh['prow'=8,'pcol'=32] {'pcol'}, dimensions={0} | all-to-all | bytes 262144 | tf_op jit(solution)/shard_map/all_to_all | solution.py:84
  292.8 16.3 %all_to_all.118 = bf16[32,4,8,256]{3,2,1,0:T(8,128)(2,1)S(1)} all-to-all(bf16[32,4,8,256]{3,2,1,0:T(8,128)(2,1)S(1)} %bitcast.172), channel_id=1, replica_groups=mesh['prow'=8,'pcol'=32] {'pcol'}, dimensions={0} | all-to-all | bytes 1048576 | tf_op jit(solution)/shard_map/all_to_all | solution.py:79
  309.2 12.8 %all_to_all.119 = bf16[8,4,8,256]{3,2,1,0:T(8,128)(2,1)S(1)} all-to-all(bf16[8,4,8,256]{3,2,1,0:T(8,128)(2,1)S(1)} %broadcast_in_dim.20), channel_id=1, replica_groups=mesh['prow'=8,'pcol'=32] {'prow'}, dimensions={0} | all-to-all | bytes 262144 | tf_op jit(solution)/shard_map/all_to_all | solution.py:82
  322.0 14.2 %all_to_all.120 = bf16[32,8,256]{2,1,0:T(8,128)(2,1)S(1)} all-to-all(bf16[32,8,256]{2,1,0:T(8,128)(2,1)S(1)} %bitcast.179), channel_id=1, replica_groups=mesh['prow'=8,'pcol'=32] {'pcol'}, dimensions={0} | all-to-all | bytes 262144 | tf_op jit(solution)/shard_map/all_to_all | solution.py:84
  (67 shorter events, 33.9 us)
Async XLA Ops:
  0.0 40.1 %copy-start.3 = (s32[15,128]{1,0:T(8,128)S(1)}, s32[15,128]{1,0:T(8,128)}, u32[]{:S(2)}) copy-start(s32[15,128]{1,0:T(8,128)} %param.14) | copy-start | bytes 23044
  5.2 26.4 %all-to-all-start = ((bf16[32,4,8,256]{3,2,1,0:T(8,128)(2,1)}), bf16[32,4,8,256]{3,2,1,0:T(8,128)(2,1)S(1)}, u32[]{:S(2)}, u32[]{:S(2)}) async-start(bf16[32,4,8,256]{3,2,1,0:T(8,128)(2,1)} %bitcast.161), calls=%async_computation | async-start | bytes 1048576 | tf_op jit(solution)/shard_map/all_to_all | solution.py:79
  32.3 13.1 %all-to-all-start.1 = ((bf16[8,4,8,256]{3,2,1,0:T(8,128)(2,1)}), bf16[8,4,8,256]{3,2,1,0:T(8,128)(2,1)S(1)}, u32[]{:S(2)}, u32[]{:S(2)}) async-start(bf16[8,4,8,256]{3,2,1,0:T(8,128)(2,1)} %broadcast_in_dim.14), calls=%async_computation.1 | async-start | bytes 262144 | tf_op jit(solution)/shard_map/all_to_all | solution.py:82
  46.0 14.5 %all-to-all-start.2 = ((bf16[32,8,256]{2,1,0:T(8,128)(2,1)}), bf16[32,8,256]{2,1,0:T(8,128)(2,1)S(1)}, u32[]{:S(2)}, u32[]{:S(2)}) async-start(bf16[32,8,256]{2,1,0:T(8,128)(2,1)} %bitcast.9), calls=%async_computation.2 | async-start | bytes 262144 | tf_op jit(solution)/shard_map/all_to_all | solution.py:84
  51.5 93.4 %copy-start.5 = (s32[16,4]{0,1:T(4,128)}, s32[16,4]{0,1:T(4,128)S(1)}, u32[]{:S(2)}) copy-start(s32[16,4]{0,1:T(4,128)S(1)} %multiply_reduce_fusion) | copy-start | bytes 772
  139.8 14.3 %all-to-all-start.8 = ((bf16[32,8,256]{2,1,0:T(8,128)(2,1)}), bf16[32,8,256]{2,1,0:T(8,128)(2,1)S(1)}, u32[]{:S(2)}, u32[]{:S(2)}) async-start(bf16[32,8,256]{2,1,0:T(8,128)(2,1)} %bitcast.27), calls=%async_computation.8 | async-start | bytes 262144 | tf_op jit(solution)/shard_map/all_to_all | solution.py:84
  155.8 1.4 copy-start
  157.1 43.8 %copy-start.2 = (bf16[4,1,256,256]{3,2,1,0:T(8,128)(2,1)S(1)}, bf16[4,1,256,256]{3,2,1,0:T(8,128)(2,1)}, u32[]{:S(2)}) copy-start(bf16[4,1,256,256]{3,2,1,0:T(8,128)(2,1)} %param.12) | copy-start | bytes 1572868
  173.6 73.0 %copy-start.1 = (f32[8,256,256]{2,1,0:T(8,128)S(1)}, f32[8,256,256]{2,1,0:T(8,128)}, u32[]{:S(2)}) copy-start(f32[8,256,256]{2,1,0:T(8,128)} %copy-done) | copy-start | bytes 6291460
  231.5 59.9 %copy-start.4 = (f32[4]{0:T(128)S(1)}, f32[4]{0:T(128)}, u32[]{:S(2)}) copy-start(f32[4]{0:T(128)} %get-tuple-element.42) | copy-start | bytes 52
  232.2 14.4 %all-to-all-start.14 = ((bf16[32,8,256]{2,1,0:T(8,128)(2,1)}), bf16[32,8,256]{2,1,0:T(8,128)(2,1)S(1)}, u32[]{:S(2)}, u32[]{:S(2)}) async-start(bf16[32,8,256]{2,1,0:T(8,128)(2,1)} %bitcast.45), calls=%async_computation.14 | async-start | bytes 262144 | tf_op jit(solution)/shard_map/all_to_all | solution.py:84

commit v5 on v2

--- a/solution.py
+++ b/solution.py
@@ -53,6 +53,10 @@
     piece_rows = block_size // pcol_count
     prow_piece = block_size // prow_count
     tile_grid = factor.reshape(rows_local, cols_local, block_size, block_size)
+    tile_rows = factor.reshape(rows_local, cols_local * block_size, block_size)
+
+    def column_tiles(first, col):
+        return tile_rows[first:, col * block_size:(col + 1) * block_size]
     columns_in = right_side.reshape(cols_local, block_size, right_side.shape[3])
     rhs_width = columns_in.shape[2]
     block_node = node_table(node_blocks, total_blocks)
@@ -78,13 +82,16 @@
         sent = jnp.stack(
             [
                 lax.dynamic_index_in_dim(tile_grid[:, level], level * level_groups + pick_k, 0, False)
-                for level in range(1, LEVELS)
+                for level in range(LEVELS)
             ]
+            + [columns_in[0]]
         )
         pairs = []
         for p_src in range(prow_count):
             for c_src in range(pcol_count):
                 k_dst = (c_src // prow_count + shift) % level_groups
+                if c_src > k_dst * prow_count + p_src:
+                    continue
                 dst = (c_src % prow_count) * pcol_count + k_dst * prow_count + p_src
                 pairs.append((p_src * pcol_count + c_src, dst))
         shifted.append(lax.ppermute(sent, ("prow", "pcol"), pairs))
@@ -96,26 +103,15 @@
         ],
         axis=1,
     )
-    own_row = jnp.arange(1, LEVELS, dtype=jnp.int32)[:, None] * pcol_count + pcol_index
+    own_row = jnp.arange(LEVELS, dtype=jnp.int32)[:, None] * pcol_count + pcol_index
     group_cols = (
-        jnp.arange(1, LEVELS, dtype=jnp.int32)[:, None] * pcol_count
+        jnp.arange(LEVELS, dtype=jnp.int32)[:, None] * pcol_count
         + prow_index
         + prow_count * jnp.arange(level_groups, dtype=jnp.int32)[None, :]
     )
     own_node = lookup(block_node, own_row.reshape(-1)).reshape(own_row.shape)
     group_node = lookup(block_node, group_cols.reshape(-1)).reshape(group_cols.shape)
     group_bits = ((own_node == group_node) & (own_row >= group_cols)).astype(jnp.float32)
-
-    def reduce_route(level_terms):
-        pieces = level_terms.astype(jnp.bfloat16).reshape(level_rows, pcol_count, piece_rows, rhs_width)
-        pieces = jnp.transpose(pieces, (1, 0, 2, 3))
-        got = lax.all_to_all(pieces, "pcol", 0, 0, tiled=True)
-        summed = jnp.sum(got.astype(jnp.float32), axis=0).astype(jnp.bfloat16)
-        spread = jnp.broadcast_to(summed[None], (prow_count,) + summed.shape)
-        gathered = lax.all_to_all(spread, "prow", 0, 0, tiled=True)
-        by_row = jnp.transpose(gathered, (1, 0, 2, 3)).reshape(pcol_count, piece_rows, rhs_width)
-        arrived = lax.all_to_all(by_row, "pcol", 0, 0, tiled=True)
-        return arrived.reshape(block_size, rhs_width)
 
     def reduce_gather_pcol(level_terms):
         pieces = level_terms.astype(jnp.bfloat16).reshape(level_rows, pcol_count, piece_rows, rhs_width)
@@ -143,25 +139,18 @@
         first_row = section_now * level_rows
         after_row = first_row + level_rows
         if section_now == 0:
-            diag_terms = panel_products(
-                tile_grid[first_row:after_row, 0], diag_bits[first_row:after_row, 0], columns_in[0]
-            )
-            solved = reduce_route(diag_terms)
+            rhs_group = diag_tiles[LEVELS]
         else:
             own_b = columns_in[section_now].astype(jnp.float32)
             contrib = partial_value[first_row:after_row] - owns_row[:, None, None] * own_b[None]
             rhs_group = reduce_gather_pcol(contrib)
-            tiles = diag_tiles[section_now - 1] * group_bits[section_now - 1][:, None, None].astype(
-                jnp.bfloat16
-            )
-            row_terms = jnp.einsum(
-                "mxy,myw->xw", tiles, rhs_group, preferred_element_type=jnp.float32
-            )
-            solved = reduce_gather_prow(row_terms)
+        tiles = diag_tiles[section_now] * group_bits[section_now][:, None, None].astype(jnp.bfloat16)
+        row_terms = jnp.einsum("mxy,myw->xw", tiles, rhs_group, preferred_element_type=jnp.float32)
+        solved = reduce_gather_prow(row_terms)
         solved_list.append(solved)
         if section_now + 1 < LEVELS:
             update_terms = panel_products(
-                tile_grid[after_row:, section_now], front_bits[after_row:, section_now], solved
+                column_tiles(after_row, section_now), front_bits[after_row:, section_now], solved
             )
             partial_value = partial_value.at[after_row:].add(update_terms)
     solution = jnp.stack(solved_list)

time: 357 us -> 416 us (1.17)
  starting transfers between devices: 66.1 us -> 174 us
  waiting for transfers between devices: 118 us -> 39.9 us
  blocking collectives: 127 us -> 167 us
  other arithmetic: 15.8 us -> 4.82 us
    all_to_all x5 -> x1, waiting for transfers between devices: 108 us -> 5.03 us  [reduce_gather_prow(): got = lax.all_to_all(pieces, 'prow', 0, 0, tiled=True)]
    all_to_all x5 -> x1, starting transfers between devices: 47.9 us -> 146 us  [reduce_gather_prow(): got = lax.all_to_all(pieces, 'prow', 0, 0, tiled=True)]
    all_to_all x2 -> x3, blocking collectives: 42.3 us -> 63.5 us  [reduce_gather_pcol(): gathered = lax.all_to_all(spread, 'pcol', 0, 0, tiled=True)]
    all_to_all x2 -> x3, blocking collectives: 37.7 us -> 58.8 us  [reduce_gather_pcol(): got = lax.all_to_all(pieces, 'pcol', 0, 0, tiled=True)]
    ppermute x4, waiting for transfers between devices: 0.01 us -> 19.2 us  [local(): shifted.append(lax.ppermute(sent, ('prow', 'pcol'), pairs))]
    another operation x6 -> x2, other arithmetic: 6.64 us -> 0.27 us  [the longest x4 6.37 us: local(): jnp.stack([lax.dynamic_index_in_dim(tile_grid[:, level], level * level_gr...]
    ppermute x4, starting transfers between devices: 9.93 us -> 15.2 us  [local(): shifted.append(lax.ppermute(sent, ('prow', 'pcol'), pairs))]
    all_to_all x2 -> x3, waiting for transfers between devices: 10.4 us -> 15.7 us  [reduce_gather_prow(): gathered = lax.all_to_all(spread, 'prow', 0, 0, tiled=True)]
  transfers between devices with their start and end apart: 11 -> 8, of which waited for: 6 -> 7; matrix products, arithmetic and copies ran while one was open for 5% -> 1% of each run, Pallas kernels for 0% -> 0%
where the time goes in v5:
time: 416 us; the launch traced here: 415 us
  starting transfers between devices  174 us (42%)
  blocking collectives  167 us (40%)
  waiting for transfers between devices  39.9 us (10%)
  local copies, waits for them, and re-layouts  17.9 us (4%)
  matrix products  10.6 us (3%)
  other arithmetic  4.82 us (1%)
    all_to_all x1, starting transfers between devices, reduce_gather_prow(): got = lax.all_to_all(pieces, 'prow', 0, 0, tiled=True)  146 us
    all_to_all x3, blocking collectives, reduce_gather_pcol(): gathered = lax.all_to_all(spread, 'pcol', 0, 0, tiled=True)  63.5 us
    all_to_all x3, blocking collectives, reduce_gather_pcol(): got = lax.all_to_all(pieces, 'pcol', 0, 0, tiled=True)  58.8 us
    all_to_all x3, blocking collectives, reduce_gather_prow(): got = lax.all_to_all(pieces, 'prow', 0, 0, tiled=True)  36.6 us
    ppermute x4, waiting for transfers between devices, local(): shifted.append(lax.ppermute(sent, ('prow', 'pcol'), pairs))  19.2 us
    all_to_all x3, waiting for transfers between devices, reduce_gather_prow(): gathered = lax.all_to_all(spread, 'prow', 0, 0, tiled=True)  15.7 us
    ppermute x4, starting transfers between devices, local(): shifted.append(lax.ppermute(sent, ('prow', 'pcol'), pairs))  15.2 us
    all_to_all x3, starting transfers between devices, reduce_gather_prow(): gathered = lax.all_to_all(spread, 'prow', 0, 0, tiled=True)  12.4 us
  transfers between devices with their start and end apart: 8, of which 7 were waited for; matrix products, arithmetic and copies ran while one was open for 1% of the time, Pallas kernels for 0%

profile of v5, /device:TPU:1, one launch (start us, length us, event | category | flops | bytes accessed | tf_op | source)
XLA Modules:
  0.0 414.8 jit_solution(13930970178155351129)
XLA Ops:
  0.0 5.7 %fusion.38 = (bf16[16,1,256,256]{3,2,1,0:T(8,128)(2,1)S(1)}, bf16[16,1,256,256]{3,2,1,0:T(8,128)(2,1)}, bf16[16,1,256,256]{3,2,1,0:T(8,128)(2,1)}, bf16[16,1,256,256]{3,2,1,0:T(8,128)(2,1)}) fusion(bf16[16,4,256,256]{3,2,1,0:T(8,128)(2,1)} %bitcast.179), kind=kLoop, calls=%fused_computation.114 | loop fusion | bytes 16777216 | tf_op jit(solution)/shard_map/slice | solution.py:84
  13.2 6.0 %collective-permute-start.1 = (bf16[5,256,256]{2,1,0:T(8,128)(2,1)}, bf16[5,256,256]{2,1,0:T(8,128)(2,1)S(1)}, u32[]{:S(2)}, u32[]{:S(2)}) collective-permute-start(bf16[5,256,256]{2,1,0:T(8,128)(2,1)} %get-tuple-element.71), channel_id=1, source_target_pairs={{0,8},{1,40},{2,72},{3,104},{4,136},{5,168},{6,200},{7,232},{8,16}... | collective-permute-start | bytes 1966088 | tf_op jit(solution)/shard_map/ppermute | solution.py:97
  19.2 3.8 collective-permute-start.2
  24.3 4.1 collective-permute-start
  34.7 8.0 %collective-permute-done.3 = bf16[5,256,256]{2,1,0:T(8,128)(2,1)S(1)} collective-permute-done((bf16[5,256,256]{2,1,0:T(8,128)(2,1)}, bf16[5,256,256]{2,1,0:T(8,128)(2,1)S(1)}, u32[]{:S(2)}, u32[]{:S(2)}) %collective-permute-start.3) | collective-permute-done | bytes 655392 | tf_op jit(solution)/shard_map/ppermute | solution.py:97
  42.8 7.8 %collective-permute-done = bf16[5,256,256]{2,1,0:T(8,128)(2,1)S(1)} collective-permute-done((bf16[5,256,256]{2,1,0:T(8,128)(2,1)}, bf16[5,256,256]{2,1,0:T(8,128)(2,1)S(1)}, u32[]{:S(2)}, u32[]{:S(2)}) %collective-permute-start) | collective-permute-done | bytes 655392 | tf_op jit(solution)/shard_map/ppermute | solution.py:97
  54.0 146.2 %all-to-all-start = ((bf16[8,32,256]{2,1,0:T(8,128)(2,1)}), bf16[8,32,256]{2,1,0:T(8,128)(2,1)S(1)}, u32[]{:S(2)}, u32[]{:S(2)}) async-start(bf16[8,32,256]{2,1,0:T(8,128)(2,1)} %bitcast.32), calls=%async_computation | async-start | bytes 262144 | tf_op jit(solution)/shard_map/all_to_all | solution.py:127
  200.4 5.0 %all-to-all-done = bf16[8,32,256]{2,1,0:T(8,128)(2,1)S(1)} async-done(((bf16[8,32,256]{2,1,0:T(8,128)(2,1)}), bf16[8,32,256]{2,1,0:T(8,128)(2,1)S(1)}, u32[]{:S(2)}, u32[]{:S(2)}) %all-to-all-start) | async-done | bytes 131104 | tf_op jit(solution)/shard_map/all_to_all | solution.py:127
  206.1 4.1 all-to-all-start.1
  210.3 5.2 %all-to-all-done.1 = bf16[8,32,256]{2,1,0:T(8,128)(2,1)S(1)} async-done(((bf16[8,32,256]{2,1,0:T(8,128)(2,1)}), bf16[8,32,256]{2,1,0:T(8,128)(2,1)S(1)}, u32[]{:S(2)}, u32[]{:S(2)}) %all-to-all-start.1) | async-done | bytes 131104 | tf_op jit(solution)/shard_map/all_to_all | solution.py:130
  217.8 21.2 %all_to_all.70 = bf16[32,4,8,256]{3,2,1,0:T(8,128)(2,1)S(1)} all-to-all(bf16[32,4,8,256]{3,2,1,0:T(8,128)(2,1)S(1)} %copy_bitcast_fusion.2), channel_id=1, replica_groups=mesh['prow'=8,'pcol'=32] {'pcol'}, dimensions={0} | all-to-all | bytes 1048576 | tf_op jit(solution)/shard_map/all_to_all | solution.py:119
  239.1 21.2 %all_to_all.71 = bf16[32,4,8,256]{3,2,1,0:T(8,128)(2,1)S(1)} all-to-all(bf16[32,4,8,256]{3,2,1,0:T(8,128)(2,1)S(1)} %broadcast_in_dim.15), channel_id=1, replica_groups=mesh['prow'=8,'pcol'=32] {'pcol'}, dimensions={0} | all-to-all | bytes 1048576 | tf_op jit(solution)/shard_map/all_to_all | solution.py:122
  261.7 12.2 %all_to_all.72 = bf16[8,32,256]{2,1,0:T(8,128)(2,1)S(1)} all-to-all(bf16[8,32,256]{2,1,0:T(8,128)(2,1)S(1)} %bitcast.196), channel_id=1, replica_groups=mesh['prow'=8,'pcol'=32] {'prow'}, dimensions={0} | all-to-all | bytes 262144 | tf_op jit(solution)/shard_map/all_to_all | solution.py:127
  274.6 4.1 all-to-all-start.5
  278.8 5.2 %all-to-all-done.5 = bf16[8,32,256]{2,1,0:T(8,128)(2,1)S(1)} async-done(((bf16[8,32,256]{2,1,0:T(8,128)(2,1)}), bf16[8,32,256]{2,1,0:T(8,128)(2,1)S(1)}, u32[]{:S(2)}, u32[]{:S(2)}) %all-to-all-start.5) | async-done | bytes 131104 | tf_op jit(solution)/shard_map/all_to_all | solution.py:130
  286.0 18.8 %all_to_all.73 = bf16[32,4,8,256]{3,2,1,0:T(8,128)(2,1)S(1)} all-to-all(bf16[32,4,8,256]{3,2,1,0:T(8,128)(2,1)S(1)} %copy_bitcast_fusion.1), channel_id=1, replica_groups=mesh['prow'=8,'pcol'=32] {'pcol'}, dimensions={0} | all-to-all | bytes 1048576 | tf_op jit(solution)/shard_map/all_to_all | solution.py:119
  305.0 21.2 %all_to_all.74 = bf16[32,4,8,256]{3,2,1,0:T(8,128)(2,1)S(1)} all-to-all(bf16[32,4,8,256]{3,2,1,0:T(8,128)(2,1)S(1)} %broadcast_in_dim.17), channel_id=1, replica_groups=mesh['prow'=8,'pcol'=32] {'pcol'}, dimensions={0} | all-to-all | bytes 1048576 | tf_op jit(solution)/shard_map/all_to_all | solution.py:122
  327.5 12.2 %all_to_all.75 = bf16[8,32,256]{2,1,0:T(8,128)(2,1)S(1)} all-to-all(bf16[8,32,256]{2,1,0:T(8,128)(2,1)S(1)} %bitcast.197), channel_id=1, replica_groups=mesh['prow'=8,'pcol'=32] {'prow'}, dimensions={0} | all-to-all | bytes 262144 | tf_op jit(solution)/shard_map/all_to_all | solution.py:127
  340.4 4.1 all-to-all-start.9
  344.7 5.2 %all-to-all-done.9 = bf16[8,32,256]{2,1,0:T(8,128)(2,1)S(1)} async-done(((bf16[8,32,256]{2,1,0:T(8,128)(2,1)}), bf16[8,32,256]{2,1,0:T(8,128)(2,1)S(1)}, u32[]{:S(2)}, u32[]{:S(2)}) %all-to-all-start.9) | async-done | bytes 131104 | tf_op jit(solution)/shard_map/all_to_all | solution.py:130
  351.7 18.8 %all_to_all.76 = bf16[32,4,8,256]{3,2,1,0:T(8,128)(2,1)S(1)} all-to-all(bf16[32,4,8,256]{3,2,1,0:T(8,128)(2,1)S(1)} %bitcast.183), channel_id=1, replica_groups=mesh['prow'=8,'pcol'=32] {'pcol'}, dimensions={0} | all-to-all | bytes 1048576 | tf_op jit(solution)/shard_map/all_to_all | solution.py:119
  370.6 21.2 %all_to_all.77 = bf16[32,4,8,256]{3,2,1,0:T(8,128)(2,1)S(1)} all-to-all(bf16[32,4,8,256]{3,2,1,0:T(8,128)(2,1)S(1)} %broadcast_in_dim.19), channel_id=1, replica_groups=mesh['prow'=8,'pcol'=32] {'pcol'}, dimensions={0} | all-to-all | bytes 1048576 | tf_op jit(solution)/shard_map/all_to_all | solution.py:122
  393.2 12.2 %all_to_all.78 = bf16[8,32,256]{2,1,0:T(8,128)(2,1)S(1)} all-to-all(bf16[8,32,256]{2,1,0:T(8,128)(2,1)S(1)} %bitcast.195), channel_id=1, replica_groups=mesh['prow'=8,'pcol'=32] {'prow'}, dimensions={0} | all-to-all | bytes 262144 | tf_op jit(solution)/shard_map/all_to_all | solution.py:127
  405.5 8.5 %all_to_all.79 = bf16[8,32,256]{2,1,0:T(8,128)(2,1)S(1)} all-to-all(bf16[8,32,256]{2,1,0:T(8,128)(2,1)S(1)} %broadcast_in_dim.20), channel_id=1, replica_groups=mesh['prow'=8,'pcol'=32] {'prow'}, dimensions={0} | all-to-all | bytes 262144 | tf_op jit(solution)/shard_map/all_to_all | solution.py:130
  (82 shorter events, 32.3 us)
Async XLA Ops:
  5.7 6.7 %copy-start.4 = (bf16[4,1,256,256]{3,2,1,0:T(8,128)(2,1)S(1)}, bf16[4,1,256,256]{3,2,1,0:T(8,128)(2,1)}, u32[]{:S(2)}) copy-start(bf16[4,1,256,256]{3,2,1,0:T(8,128)(2,1)} %param.12) | copy-start | bytes 1572868
  5.7 23.0 %copy-start.8 = (s32[15]{0:T(128)S(1)}, s32[15]{0:T(128)}, u32[]{:S(2)}) copy-start(s32[15]{0:T(128)} %param.13) | copy-start | bytes 184
  5.7 23.0 %copy-start.9 = (s32[15]{0:T(128)S(1)}, s32[15]{0:T(128)}, u32[]{:S(2)}) copy-start(s32[15]{0:T(128)} %constant.255.clone) | copy-start | bytes 184
  13.2 18.2 %collective-permute-start.1 = (bf16[5,256,256]{2,1,0:T(8,128)(2,1)}, bf16[5,256,256]{2,1,0:T(8,128)(2,1)S(1)}, u32[]{:S(2)}, u32[]{:S(2)}) collective-permute-start(bf16[5,256,256]{2,1,0:T(8,128)(2,1)} %get-tuple-element.71), channel_id=1, source_target_pairs={{0,8},{1,40},{2,72},{3,104},{4,136},{5,168},{6,200},{7,232},{8,16}... | collective-permute-start | bytes 1966088 | tf_op jit(solution)/shard_map/ppermute | solution.py:97
  19.2 15.6 %collective-permute-start.2 = (bf16[5,256,256]{2,1,0:T(8,128)(2,1)}, bf16[5,256,256]{2,1,0:T(8,128)(2,1)S(1)}, u32[]{:S(2)}, u32[]{:S(2)}) collective-permute-start(bf16[5,256,256]{2,1,0:T(8,128)(2,1)} %get-tuple-element.70), channel_id=1, source_target_pairs={{0,16},{1,48},{2,80},{3,112},{4,144},{5,176},{6,208},{7,240},{8,24... | collective-permute-start | bytes 1966088 | tf_op jit(solution)/shard_map/ppermute | solution.py:97
  23.0 19.8 %collective-permute-start.3 = (bf16[5,256,256]{2,1,0:T(8,128)(2,1)}, bf16[5,256,256]{2,1,0:T(8,128)(2,1)S(1)}, u32[]{:S(2)}, u32[]{:S(2)}) collective-permute-start(bf16[5,256,256]{2,1,0:T(8,128)(2,1)} %get-tuple-element.69), channel_id=1, source_target_pairs={{0,24},{1,56},{2,88},{3,120},{4,152},{5,184},{6,216},{7,248},{32,2... | collective-permute-start | bytes 1966088 | tf_op jit(solution)/shard_map/ppermute | solution.py:97
  24.3 26.2 %collective-permute-start = (bf16[5,256,256]{2,1,0:T(8,128)(2,1)}, bf16[5,256,256]{2,1,0:T(8,128)(2,1)S(1)}, u32[]{:S(2)}, u32[]{:S(2)}) collective-permute-start(bf16[5,256,256]{2,1,0:T(8,128)(2,1)} %get-tuple-element.68), channel_id=1, source_target_pairs={{0,0},{8,8},{16,16},{24,24},{32,1},{33,33},{40,9},{41,41},{48,17},... | collective-permute-start | bytes 1966088 | tf_op jit(solution)/shard_map/ppermute | solution.py:97
  51.1 149.0 %copy-start.5 = (s32[15,128]{1,0:T(8,128)S(1)}, s32[15,128]{1,0:T(8,128)}, u32[]{:S(2)}) copy-start(s32[15,128]{1,0:T(8,128)} %param.14) | copy-start | bytes 23044
  51.5 1.5 copy-start.1
  54.0 151.5 %all-to-all-start = ((bf16[8,32,256]{2,1,0:T(8,128)(2,1)}), bf16[8,32,256]{2,1,0:T(8,128)(2,1)S(1)}, u32[]{:S(2)}, u32[]{:S(2)}) async-start(bf16[8,32,256]{2,1,0:T(8,128)(2,1)} %bitcast.32), calls=%async_computation | async-start | bytes 262144 | tf_op jit(solution)/shard_map/all_to_all | solution.py:127
  206.1 9.4 %all-to-all-start.1 = ((bf16[8,32,256]{2,1,0:T(8,128)(2,1)}), bf16[8,32,256]{2,1,0:T(8,128)(2,1)S(1)}, u32[]{:S(2)}, u32[]{:S(2)}) async-start(bf16[8,32,256]{2,1,0:T(8,128)(2,1)} %broadcast_in_dim.14), calls=%async_computation.1 | async-start | bytes 262144 | tf_op jit(solution)/shard_map/all_to_all | solution.py:130
  217.5 42.7 %copy-start.7 = (bf16[4]{0:T(256)(128)(2,1)S(1)}, bf16[4]{0:T(256)(128)(2,1)}, u32[]{:S(2)}) copy-start(bf16[4]{0:T(256)(128)(2,1)} %get-tuple-element.74) | copy-start | bytes 28
  274.6 9.4 %all-to-all-start.5 = ((bf16[8,32,256]{2,1,0:T(8,128)(2,1)}), bf16[8,32,256]{2,1,0:T(8,128)(2,1)S(1)}, u32[]{:S(2)}, u32[]{:S(2)}) async-start(bf16[8,32,256]{2,1,0:T(8,128)(2,1)} %broadcast_in_dim.16), calls=%async_computation.5 | async-start | bytes 262144 | tf_op jit(solution)/shard_map/all_to_all | solution.py:130
  284.0 1.7 copy-start.3
  285.7 41.8 %copy-start = (f32[8,256,256]{2,1,0:T(8,128)}, f32[8,256,256]{2,1,0:T(8,128)S(1)}, u32[]{:S(2)}) copy-start(f32[8,256,256]{2,1,0:T(8,128)S(1)} %slice_add_fusion) | copy-start | bytes 6291460
  285.7 40.4 %copy-start.6 = (bf16[4]{0:T(256)(128)(2,1)S(1)}, bf16[4]{0:T(256)(128)(2,1)}, u32[]{:S(2)}) copy-start(bf16[4]{0:T(256)(128)(2,1)} %get-tuple-element.73) | copy-start | bytes 28
  304.8 45.1 %copy-start.2 = (f32[256,256]{1,0:T(8,128)S(1)}, f32[256,256]{1,0:T(8,128)}, u32[]{:S(2)}) copy-start(f32[256,256]{1,0:T(8,128)} %get-tuple-element.65) | copy-start | bytes 786436
  340.4 9.4 %all-to-all-start.9 = ((bf16[8,32,256]{2,1,0:T(8,128)(2,1)}), bf16[8,32,256]{2,1,0:T(8,128)(2,1)S(1)}, u32[]{:S(2)}, u32[]{:S(2)}) async-start(bf16[8,32,256]{2,1,0:T(8,128)(2,1)} %broadcast_in_dim.18), calls=%async_computation.9 | async-start | bytes 262144 | tf_op jit(solution)/shard_map/all_to_all | solution.py:130

commit v6 on v4

--- a/solution.py
+++ b/solution.py
@@ -4,6 +4,9 @@
 from jax.sharding import PartitionSpec as P
 
 LEVELS = 4
+PROW = ("x", "core")
+PCOL = ("y", "z")
+RING = "z"
 
 
 def node_order():
@@ -44,10 +47,12 @@
     rows_local = factor.shape[0]
     cols_local = factor.shape[2]
     block_size = factor.shape[4]
-    prow_count = lax.axis_size("prow")
-    pcol_count = lax.axis_size("pcol")
-    prow_index = lax.axis_index("prow")
-    pcol_index = lax.axis_index("pcol")
+    prow_count = lax.axis_size(PROW)
+    pcol_count = lax.axis_size(PCOL)
+    prow_index = lax.axis_index(PROW)
+    pcol_index = lax.axis_index(PCOL)
+    ring = lax.axis_size(RING)
+    chunk_rows = block_size // ring
     total_blocks = rows_local * prow_count
     level_rows = pcol_count // prow_count
     piece_rows = block_size // pcol_count
@@ -74,14 +79,12 @@
 
     def reduce_route(level_terms):
         rhs_width = level_terms.shape[2]
-        pieces = level_terms.astype(jnp.bfloat16).reshape(level_rows, pcol_count, piece_rows, rhs_width)
-        pieces = jnp.transpose(pieces, (1, 0, 2, 3))
-        got = lax.all_to_all(pieces, "pcol", 0, 0, tiled=True)
+        pieces = level_terms.astype(jnp.bfloat16).reshape(pcol_count, chunk_rows, rhs_width)
+        got = lax.all_to_all(pieces, PCOL, 0, 0, tiled=True)
         summed = jnp.sum(got.astype(jnp.float32), axis=0).astype(jnp.bfloat16)
         spread = jnp.broadcast_to(summed[None], (prow_count,) + summed.shape)
-        gathered = lax.all_to_all(spread, "prow", 0, 0, tiled=True)
-        by_row = jnp.transpose(gathered, (1, 0, 2, 3)).reshape(pcol_count, piece_rows, rhs_width)
-        arrived = lax.all_to_all(by_row, "pcol", 0, 0, tiled=True)
+        gathered = lax.all_to_all(spread, PROW, 0, 0, tiled=True)
+        arrived = lax.all_to_all(gathered, RING, 0, 0, tiled=True)
         return arrived.reshape(block_size, rhs_width)
 
     rhs_width = columns_in.shape[2]
@@ -112,6 +115,9 @@
 
 
 def solution(mesh):
-    in_specs = (P(None, "prow", None, "pcol", None, None), P(None, "pcol", None, None), P(), P())
-    out_specs = P(None, "pcol", None, None)
-    return jax.shard_map(local, mesh=mesh, in_specs=in_specs, out_specs=out_specs, check_vma=False)
+    fine = jax.sharding.Mesh(
+        mesh.devices.reshape(4, mesh.devices.shape[0] // 4, 4, mesh.devices.shape[1] // 4), PROW + PCOL
+    )
+    in_specs = (P(None, PROW, None, PCOL, None, None), P(None, PCOL, None, None), P(), P())
+    out_specs = P(None, PCOL, None, None)
+    return jax.shard_map(local, mesh=fine, in_specs=in_specs, out_specs=out_specs, check_vma=False)

time: 339 us -> 317 us (0.935)
  blocking collectives: 232 us -> 220 us
  waiting for transfers between devices: 45.8 us -> 42 us
  starting transfers between devices: 35.6 us -> 32.2 us
    all_to_all x16, blocking collectives: 232 us -> 220 us  [the longest x6 94.6 us: reduce_route(): got = lax.all_to_all(pieces, PCOL, 0, 0, tiled=True)]
    all_to_all x5, waiting for transfers between devices: 45.8 us -> 42 us  [the longest x3 23.2 us: reduce_route(): arrived = lax.all_to_all(gathered, RING, 0, 0, tiled=True)]
    all_to_all x5, starting transfers between devices: 35.6 us -> 32.2 us  [the longest x3 12.4 us: reduce_route(): arrived = lax.all_to_all(gathered, RING, 0, 0, tiled=True)]
where the time goes in v6:
time: 317 us; the launch traced here: 316 us
  blocking collectives  220 us (69%)
  waiting for transfers between devices  42 us (13%)
  starting transfers between devices  32.2 us (10%)
  matrix products  11.8 us (4%)
  other arithmetic  7.18 us (2%)
    all_to_all x6, blocking collectives, reduce_route(): got = lax.all_to_all(pieces, PCOL, 0, 0, tiled=True)  94.6 us
    all_to_all x6, blocking collectives, reduce_route(): gathered = lax.all_to_all(spread, PROW, 0, 0, tiled=True)  79.8 us
    all_to_all x4, blocking collectives, reduce_route(): arrived = lax.all_to_all(gathered, RING, 0, 0, tiled=True)  46 us
    all_to_all x3, waiting for transfers between devices, reduce_route(): arrived = lax.all_to_all(gathered, RING, 0, 0, tiled=True)  23.2 us
    all_to_all x1, waiting for transfers between devices, reduce_route(): got = lax.all_to_all(pieces, PCOL, 0, 0, tiled=True)  14.2 us
    all_to_all x3, starting transfers between devices, reduce_route(): arrived = lax.all_to_all(gathered, RING, 0, 0, tiled=True)  12.4 us
    all_to_all x1, starting transfers between devices, reduce_route(): got = lax.all_to_all(pieces, PCOL, 0, 0, tiled=True)  12 us
    dot_general x7, matrix products, panel_products(): jnp.einsum('nxy,yw->nxw', tile_stack, vector, preferred_element_type=jnp....  11.8 us
  transfers between devices with their start and end apart: 5, of which 5 were waited for; matrix products, arithmetic and copies ran while one was open for 0% of the time, Pallas kernels for 0%

profile of v6, /device:TPU:1, one launch (start us, length us, event | category | flops | bytes accessed | tf_op | source)
XLA Modules:
  0.0 315.9 jit_solution(15803270476594512828)
XLA Ops:
  4.6 12.0 %all-to-all-start = ((bf16[32,32,256]{2,1,0:T(8,128)(2,1)}), bf16[32,32,256]{2,1,0:T(8,128)(2,1)S(1)}, u32[]{:S(2)}, u32[]{:S(2)}) async-start(bf16[32,32,256]{2,1,0:T(8,128)(2,1)} %bitcast.6), calls=%async_computation | async-start | bytes 1048576 | tf_op jit(solution)/shard_map/all_to_all | solution.py:83
  16.7 14.2 %all-to-all-done = bf16[32,32,256]{2,1,0:T(8,128)(2,1)S(1)} async-done(((bf16[32,32,256]{2,1,0:T(8,128)(2,1)}), bf16[32,32,256]{2,1,0:T(8,128)(2,1)S(1)}, u32[]{:S(2)}, u32[]{:S(2)}) %all-to-all-start) | async-done | bytes 524320 | tf_op jit(solution)/shard_map/all_to_all | solution.py:83
  31.7 7.8 %all-to-all-start.1 = ((bf16[8,32,256]{2,1,0:T(8,128)(2,1)}), bf16[8,32,256]{2,1,0:T(8,128)(2,1)}, u32[]{:S(2)}, u32[]{:S(2)}) async-start(bf16[8,32,256]{2,1,0:T(8,128)(2,1)} %broadcast_in_dim.14), calls=%async_computation.1 | async-start | bytes 262144 | tf_op jit(solution)/shard_map/all_to_all | solution.py:86
  40.3 4.6 %all-to-all-done.1 = bf16[8,32,256]{2,1,0:T(8,128)(2,1)} async-done(((bf16[8,32,256]{2,1,0:T(8,128)(2,1)}), bf16[8,32,256]{2,1,0:T(8,128)(2,1)}, u32[]{:S(2)}, u32[]{:S(2)}) %all-to-all-start.1) | async-done | bytes 131104 | tf_op jit(solution)/shard_map/all_to_all | solution.py:86
  44.9 4.1 %all-to-all-start.2 = ((bf16[8,32,256]{2,1,0:T(8,128)(2,1)}), bf16[8,32,256]{2,1,0:T(8,128)(2,1)S(1)}, u32[]{:S(2)}, u32[]{:S(2)}) async-start(bf16[8,32,256]{2,1,0:T(8,128)(2,1)} %all-to-all-done.1), calls=%async_computation.2 | async-start | bytes 262144 | tf_op jit(solution)/shard_map/all_to_all | solution.py:87
  49.2 7.6 %all-to-all-done.2 = bf16[8,32,256]{2,1,0:T(8,128)(2,1)S(1)} async-done(((bf16[8,32,256]{2,1,0:T(8,128)(2,1)}), bf16[8,32,256]{2,1,0:T(8,128)(2,1)S(1)}, u32[]{:S(2)}, u32[]{:S(2)}) %all-to-all-start.2) | async-done | bytes 131104 | tf_op jit(solution)/shard_map/all_to_all | solution.py:87
  58.9 16.2 %all_to_all.105 = bf16[32,32,256]{2,1,0:T(8,128)(2,1)} all-to-all(bf16[32,32,256]{2,1,0:T(8,128)(2,1)S(1)} %bitcast.97), channel_id=1, replica_groups=mesh['x'=4,'core'=2,'y'=4,'z'=8] {'y','z'}, dimensions={0} | all-to-all | bytes 1048576 | tf_op jit(solution)/shard_map/all_to_all | solution.py:83
  76.3 12.9 %all_to_all.106 = bf16[8,32,256]{2,1,0:T(8,128)(2,1)S(1)} all-to-all(bf16[8,32,256]{2,1,0:T(8,128)(2,1)S(1)} %broadcast_in_dim.15), channel_id=1, replica_groups=mesh['x'=4,'core'=2,'y'=4,'z'=8] {'x','core'}, dimensions={0} | all-to-all | bytes 262144 | tf_op jit(solution)/shard_map/all_to_all | solution.py:86
  89.2 11.8 %all_to_all.107 = bf16[8,32,256]{2,1,0:T(8,128)(2,1)S(1)} all-to-all(bf16[8,32,256]{2,1,0:T(8,128)(2,1)S(1)} %all_to_all.106), channel_id=1, replica_groups=mesh['x'=4,'core'=2,'y'=4,'z'=8] {'z'}, dimensions={0} | all-to-all | bytes 262144 | tf_op jit(solution)/shard_map/all_to_all | solution.py:87
  102.3 16.2 %all_to_all.108 = bf16[32,32,256]{2,1,0:T(8,128)(2,1)} all-to-all(bf16[32,32,256]{2,1,0:T(8,128)(2,1)S(1)} %bitcast.112), channel_id=1, replica_groups=mesh['x'=4,'core'=2,'y'=4,'z'=8] {'y','z'}, dimensions={0} | all-to-all | bytes 1048576 | tf_op jit(solution)/shard_map/all_to_all | solution.py:83
  119.7 13.6 %all_to_all.109 = bf16[8,32,256]{2,1,0:T(8,128)(2,1)} all-to-all(bf16[8,32,256]{2,1,0:T(8,128)(2,1)S(1)} %broadcast_in_dim.16), channel_id=1, replica_groups=mesh['x'=4,'core'=2,'y'=4,'z'=8] {'x','core'}, dimensions={0} | all-to-all | bytes 262144 | tf_op jit(solution)/shard_map/all_to_all | solution.py:86
  137.5 7.8 %all-to-all-done.8 = bf16[8,32,256]{2,1,0:T(8,128)(2,1)S(1)} async-done(((bf16[8,32,256]{2,1,0:T(8,128)(2,1)}), bf16[8,32,256]{2,1,0:T(8,128)(2,1)S(1)}, u32[]{:S(2)}, u32[]{:S(2)}) %all-to-all-start.8) | async-done | bytes 131104 | tf_op jit(solution)/shard_map/all_to_all | solution.py:87
  148.3 15.5 %all_to_all.110 = bf16[32,32,256]{2,1,0:T(8,128)(2,1)S(1)} all-to-all(bf16[32,32,256]{2,1,0:T(8,128)(2,1)S(1)} %bitcast.98), channel_id=1, replica_groups=mesh['x'=4,'core'=2,'y'=4,'z'=8] {'y','z'}, dimensions={0} | all-to-all | bytes 1048576 | tf_op jit(solution)/shard_map/all_to_all | solution.py:83
  164.0 13.3 %all_to_all.111 = bf16[8,32,256]{2,1,0:T(8,128)(2,1)S(1)} all-to-all(bf16[8,32,256]{2,1,0:T(8,128)(2,1)S(1)} %broadcast_in_dim.17), channel_id=1, replica_groups=mesh['x'=4,'core'=2,'y'=4,'z'=8] {'x','core'}, dimensions={0} | all-to-all | bytes 262144 | tf_op jit(solution)/shard_map/all_to_all | solution.py:86
  177.3 11.4 %all_to_all.112 = bf16[8,32,256]{2,1,0:T(8,128)(2,1)S(1)} all-to-all(bf16[8,32,256]{2,1,0:T(8,128)(2,1)S(1)} %all_to_all.111), channel_id=1, replica_groups=mesh['x'=4,'core'=2,'y'=4,'z'=8] {'z'}, dimensions={0} | all-to-all | bytes 262144 | tf_op jit(solution)/shard_map/all_to_all | solution.py:87
  190.1 15.5 %all_to_all.113 = bf16[32,32,256]{2,1,0:T(8,128)(2,1)S(1)} all-to-all(bf16[32,32,256]{2,1,0:T(8,128)(2,1)S(1)} %bitcast.113), channel_id=1, replica_groups=mesh['x'=4,'core'=2,'y'=4,'z'=8] {'y','z'}, dimensions={0} | all-to-all | bytes 1048576 | tf_op jit(solution)/shard_map/all_to_all | solution.py:83
  205.7 13.6 %all_to_all.114 = bf16[8,32,256]{2,1,0:T(8,128)(2,1)} all-to-all(bf16[8,32,256]{2,1,0:T(8,128)(2,1)S(1)} %broadcast_in_dim.18), channel_id=1, replica_groups=mesh['x'=4,'core'=2,'y'=4,'z'=8] {'x','core'}, dimensions={0} | all-to-all | bytes 262144 | tf_op jit(solution)/shard_map/all_to_all | solution.py:86
  223.5 7.8 %all-to-all-done.14 = bf16[8,32,256]{2,1,0:T(8,128)(2,1)S(1)} async-done(((bf16[8,32,256]{2,1,0:T(8,128)(2,1)}), bf16[8,32,256]{2,1,0:T(8,128)(2,1)S(1)}, u32[]{:S(2)}, u32[]{:S(2)}) %all-to-all-start.14) | async-done | bytes 131104 | tf_op jit(solution)/shard_map/all_to_all | solution.py:87
  233.0 15.5 %all_to_all.115 = bf16[32,32,256]{2,1,0:T(8,128)(2,1)S(1)} all-to-all(bf16[32,32,256]{2,1,0:T(8,128)(2,1)S(1)} %bitcast.96), channel_id=1, replica_groups=mesh['x'=4,'core'=2,'y'=4,'z'=8] {'y','z'}, dimensions={0} | all-to-all | bytes 1048576 | tf_op jit(solution)/shard_map/all_to_all | solution.py:83
  248.6 13.3 %all_to_all.116 = bf16[8,32,256]{2,1,0:T(8,128)(2,1)S(1)} all-to-all(bf16[8,32,256]{2,1,0:T(8,128)(2,1)S(1)} %broadcast_in_dim.19), channel_id=1, replica_groups=mesh['x'=4,'core'=2,'y'=4,'z'=8] {'x','core'}, dimensions={0} | all-to-all | bytes 262144 | tf_op jit(solution)/shard_map/all_to_all | solution.py:86
  261.9 11.4 %all_to_all.117 = bf16[8,32,256]{2,1,0:T(8,128)(2,1)S(1)} all-to-all(bf16[8,32,256]{2,1,0:T(8,128)(2,1)S(1)} %all_to_all.116), channel_id=1, replica_groups=mesh['x'=4,'core'=2,'y'=4,'z'=8] {'z'}, dimensions={0} | all-to-all | bytes 262144 | tf_op jit(solution)/shard_map/all_to_all | solution.py:87
  274.7 15.6 %all_to_all.118 = bf16[32,32,256]{2,1,0:T(8,128)(2,1)S(1)} all-to-all(bf16[32,32,256]{2,1,0:T(8,128)(2,1)S(1)} %bitcast.114), channel_id=1, replica_groups=mesh['x'=4,'core'=2,'y'=4,'z'=8] {'y','z'}, dimensions={0} | all-to-all | bytes 1048576 | tf_op jit(solution)/shard_map/all_to_all | solution.py:83
  290.4 13.2 %all_to_all.119 = bf16[8,32,256]{2,1,0:T(8,128)(2,1)S(1)} all-to-all(bf16[8,32,256]{2,1,0:T(8,128)(2,1)S(1)} %broadcast_in_dim.20), channel_id=1, replica_groups=mesh['x'=4,'core'=2,'y'=4,'z'=8] {'x','core'}, dimensions={0} | all-to-all | bytes 262144 | tf_op jit(solution)/shard_map/all_to_all | solution.py:86
  303.6 11.4 %all_to_all.120 = bf16[8,32,256]{2,1,0:T(8,128)(2,1)S(1)} all-to-all(bf16[8,32,256]{2,1,0:T(8,128)(2,1)S(1)} %all_to_all.119), channel_id=1, replica_groups=mesh['x'=4,'core'=2,'y'=4,'z'=8] {'z'}, dimensions={0} | all-to-all | bytes 262144 | tf_op jit(solution)/shard_map/all_to_all | solution.py:87
  (45 shorter events, 29.4 us)
Async XLA Ops:
  4.6 26.3 %all-to-all-start = ((bf16[32,32,256]{2,1,0:T(8,128)(2,1)}), bf16[32,32,256]{2,1,0:T(8,128)(2,1)S(1)}, u32[]{:S(2)}, u32[]{:S(2)}) async-start(bf16[32,32,256]{2,1,0:T(8,128)(2,1)} %bitcast.6), calls=%async_computation | async-start | bytes 1048576 | tf_op jit(solution)/shard_map/all_to_all | solution.py:83
  31.7 13.2 %all-to-all-start.1 = ((bf16[8,32,256]{2,1,0:T(8,128)(2,1)}), bf16[8,32,256]{2,1,0:T(8,128)(2,1)}, u32[]{:S(2)}, u32[]{:S(2)}) async-start(bf16[8,32,256]{2,1,0:T(8,128)(2,1)} %broadcast_in_dim.14), calls=%async_computation.1 | async-start | bytes 262144 | tf_op jit(solution)/shard_map/all_to_all | solution.py:86
  44.9 12.0 %all-to-all-start.2 = ((bf16[8,32,256]{2,1,0:T(8,128)(2,1)}), bf16[8,32,256]{2,1,0:T(8,128)(2,1)S(1)}, u32[]{:S(2)}, u32[]{:S(2)}) async-start(bf16[8,32,256]{2,1,0:T(8,128)(2,1)} %all-to-all-done.1), calls=%async_computation.2 | async-start | bytes 262144 | tf_op jit(solution)/shard_map/all_to_all | solution.py:87
  133.3 12.0 %all-to-all-start.8 = ((bf16[8,32,256]{2,1,0:T(8,128)(2,1)}), bf16[8,32,256]{2,1,0:T(8,128)(2,1)S(1)}, u32[]{:S(2)}, u32[]{:S(2)}) async-start(bf16[8,32,256]{2,1,0:T(8,128)(2,1)} %all_to_all.109), calls=%async_computation.8 | async-start | bytes 262144 | tf_op jit(solution)/shard_map/all_to_all | solution.py:87
  146.9 1.4 copy-start
  219.3 12.0 %all-to-all-start.14 = ((bf16[8,32,256]{2,1,0:T(8,128)(2,1)}), bf16[8,32,256]{2,1,0:T(8,128)(2,1)S(1)}, u32[]{:S(2)}, u32[]{:S(2)}) async-start(bf16[8,32,256]{2,1,0:T(8,128)(2,1)} %all_to_all.114), calls=%async_computation.14 | async-start | bytes 262144 | tf_op jit(solution)/shard_map/all_to_all | solution.py:87

commit v7 on v6

--- a/solution.py
+++ b/solution.py
@@ -88,6 +88,8 @@
         return arrived.reshape(block_size, rhs_width)
 
     rhs_width = columns_in.shape[2]
+    row_in_group = prow_index + prow_count * jnp.arange(level_rows, dtype=jnp.int32)
+    owns_row = (row_in_group == pcol_index).astype(jnp.float32)
     partial_value = jnp.zeros((rows_local, block_size, rhs_width), jnp.float32)
     solved_list = []
     for section_now in range(LEVELS):
@@ -96,8 +98,9 @@
         if section_now == 0:
             rhs_column = columns_in[0]
         else:
-            update = reduce_route(partial_value[first_row:after_row]).astype(jnp.float32)
-            rhs_column = (columns_in[section_now].astype(jnp.float32) - update).astype(jnp.bfloat16)
+            own_b = columns_in[section_now].astype(jnp.float32)
+            contrib = owns_row[:, None, None] * own_b[None] - partial_value[first_row:after_row]
+            rhs_column = reduce_route(contrib)
         diag_terms = panel_products(
             column_tiles(first_row, section_now)[:level_rows],
             diag_bits[first_row:after_row, section_now],

time: 317 us -> 318 us (level)
  transfers between devices with their start and end apart: 5 -> 5, of which waited for: 5 -> 5; matrix products, arithmetic and copies ran while one was open for 0% -> 1% of each run, Pallas kernels for 0% -> 0%
where the time goes in v7:
time: 318 us; the launch traced here: 317 us
  blocking collectives  221 us (69%)
  waiting for transfers between devices  40.8 us (13%)
  starting transfers between devices  32.2 us (10%)
  matrix products  11.2 us (4%)
  other arithmetic  9.41 us (3%)
    all_to_all x6, blocking collectives, reduce_route(): got = lax.all_to_all(pieces, PCOL, 0, 0, tiled=True)  94.8 us
    all_to_all x6, blocking collectives, reduce_route(): gathered = lax.all_to_all(spread, PROW, 0, 0, tiled=True)  79.8 us
    all_to_all x4, blocking collectives, reduce_route(): arrived = lax.all_to_all(gathered, RING, 0, 0, tiled=True)  46 us
    all_to_all x3, waiting for transfers between devices, reduce_route(): arrived = lax.all_to_all(gathered, RING, 0, 0, tiled=True)  23.3 us
    all_to_all x3, starting transfers between devices, reduce_route(): arrived = lax.all_to_all(gathered, RING, 0, 0, tiled=True)  12.4 us
    all_to_all x1, waiting for transfers between devices, reduce_route(): got = lax.all_to_all(pieces, PCOL, 0, 0, tiled=True)  12.3 us
    all_to_all x1, starting transfers between devices, reduce_route(): got = lax.all_to_all(pieces, PCOL, 0, 0, tiled=True)  12 us
    dot_general x7, matrix products, panel_products(): jnp.einsum('nxy,yw->nxw', tile_stack, vector, preferred_element_type=jnp....  11.2 us
  transfers between devices with their start and end apart: 5, of which 5 were waited for; matrix products, arithmetic and copies ran while one was open for 1% of the time, Pallas kernels for 0%

profile of v7, /device:TPU:1, one launch (start us, length us, event | category | flops | bytes accessed | tf_op | source)
XLA Modules:
  0.0 316.5 jit_solution(12861412189971288255)
XLA Ops:
  5.2 12.0 %all-to-all-start = ((bf16[32,32,256]{2,1,0:T(8,128)(2,1)}), bf16[32,32,256]{2,1,0:T(8,128)(2,1)S(1)}, u32[]{:S(2)}, u32[]{:S(2)}) async-start(bf16[32,32,256]{2,1,0:T(8,128)(2,1)} %bitcast.6), calls=%async_computation | async-start | bytes 1048576 | tf_op jit(solution)/shard_map/all_to_all | solution.py:83
  19.2 12.3 %all-to-all-done = bf16[32,32,256]{2,1,0:T(8,128)(2,1)S(1)} async-done(((bf16[32,32,256]{2,1,0:T(8,128)(2,1)}), bf16[32,32,256]{2,1,0:T(8,128)(2,1)S(1)}, u32[]{:S(2)}, u32[]{:S(2)}) %all-to-all-start) | async-done | bytes 524320 | tf_op jit(solution)/shard_map/all_to_all | solution.py:83
  32.3 7.8 %all-to-all-start.1 = ((bf16[8,32,256]{2,1,0:T(8,128)(2,1)}), bf16[8,32,256]{2,1,0:T(8,128)(2,1)}, u32[]{:S(2)}, u32[]{:S(2)}) async-start(bf16[8,32,256]{2,1,0:T(8,128)(2,1)} %broadcast_in_dim.14), calls=%async_computation.1 | async-start | bytes 262144 | tf_op jit(solution)/shard_map/all_to_all | solution.py:86
  40.3 5.1 %all-to-all-done.1 = bf16[8,32,256]{2,1,0:T(8,128)(2,1)} async-done(((bf16[8,32,256]{2,1,0:T(8,128)(2,1)}), bf16[8,32,256]{2,1,0:T(8,128)(2,1)}, u32[]{:S(2)}, u32[]{:S(2)}) %all-to-all-start.1) | async-done | bytes 131104 | tf_op jit(solution)/shard_map/all_to_all | solution.py:86
  45.5 4.1 %all-to-all-start.2 = ((bf16[8,32,256]{2,1,0:T(8,128)(2,1)}), bf16[8,32,256]{2,1,0:T(8,128)(2,1)S(1)}, u32[]{:S(2)}, u32[]{:S(2)}) async-start(bf16[8,32,256]{2,1,0:T(8,128)(2,1)} %all-to-all-done.1), calls=%async_computation.2 | async-start | bytes 262144 | tf_op jit(solution)/shard_map/all_to_all | solution.py:87
  49.7 7.8 %all-to-all-done.2 = bf16[8,32,256]{2,1,0:T(8,128)(2,1)S(1)} async-done(((bf16[8,32,256]{2,1,0:T(8,128)(2,1)}), bf16[8,32,256]{2,1,0:T(8,128)(2,1)S(1)}, u32[]{:S(2)}, u32[]{:S(2)}) %all-to-all-start.2) | async-done | bytes 131104 | tf_op jit(solution)/shard_map/all_to_all | solution.py:87
  59.7 16.2 %all_to_all.105 = bf16[32,32,256]{2,1,0:T(8,128)(2,1)} all-to-all(bf16[32,32,256]{2,1,0:T(8,128)(2,1)S(1)} %bitcast.87), channel_id=1, replica_groups=mesh['x'=4,'core'=2,'y'=4,'z'=8] {'y','z'}, dimensions={0} | all-to-all | bytes 1048576 | tf_op jit(solution)/shard_map/all_to_all | solution.py:83
  77.0 12.9 %all_to_all.106 = bf16[8,32,256]{2,1,0:T(8,128)(2,1)S(1)} all-to-all(bf16[8,32,256]{2,1,0:T(8,128)(2,1)S(1)} %broadcast_in_dim.15), channel_id=1, replica_groups=mesh['x'=4,'core'=2,'y'=4,'z'=8] {'x','core'}, dimensions={0} | all-to-all | bytes 262144 | tf_op jit(solution)/shard_map/all_to_all | solution.py:86
  89.9 11.8 %all_to_all.107 = bf16[8,32,256]{2,1,0:T(8,128)(2,1)S(1)} all-to-all(bf16[8,32,256]{2,1,0:T(8,128)(2,1)S(1)} %all_to_all.106), channel_id=1, replica_groups=mesh['x'=4,'core'=2,'y'=4,'z'=8] {'z'}, dimensions={0} | all-to-all | bytes 262144 | tf_op jit(solution)/shard_map/all_to_all | solution.py:87
  103.0 16.2 %all_to_all.108 = bf16[32,32,256]{2,1,0:T(8,128)(2,1)} all-to-all(bf16[32,32,256]{2,1,0:T(8,128)(2,1)S(1)} %bitcast.102), channel_id=1, replica_groups=mesh['x'=4,'core'=2,'y'=4,'z'=8] {'y','z'}, dimensions={0} | all-to-all | bytes 1048576 | tf_op jit(solution)/shard_map/all_to_all | solution.py:83
  120.4 13.6 %all_to_all.109 = bf16[8,32,256]{2,1,0:T(8,128)(2,1)} all-to-all(bf16[8,32,256]{2,1,0:T(8,128)(2,1)S(1)} %broadcast_in_dim.16), channel_id=1, replica_groups=mesh['x'=4,'core'=2,'y'=4,'z'=8] {'x','core'}, dimensions={0} | all-to-all | bytes 262144 | tf_op jit(solution)/shard_map/all_to_all | solution.py:86
  138.2 7.8 %all-to-all-done.8 = bf16[8,32,256]{2,1,0:T(8,128)(2,1)S(1)} async-done(((bf16[8,32,256]{2,1,0:T(8,128)(2,1)}), bf16[8,32,256]{2,1,0:T(8,128)(2,1)S(1)}, u32[]{:S(2)}, u32[]{:S(2)}) %all-to-all-start.8) | async-done | bytes 131104 | tf_op jit(solution)/shard_map/all_to_all | solution.py:87
  149.3 15.7 %all_to_all.110 = bf16[32,32,256]{2,1,0:T(8,128)(2,1)S(1)} all-to-all(bf16[32,32,256]{2,1,0:T(8,128)(2,1)S(1)} %bitcast.88), channel_id=1, replica_groups=mesh['x'=4,'core'=2,'y'=4,'z'=8] {'y','z'}, dimensions={0} | all-to-all | bytes 1048576 | tf_op jit(solution)/shard_map/all_to_all | solution.py:83
  165.0 13.3 %all_to_all.111 = bf16[8,32,256]{2,1,0:T(8,128)(2,1)S(1)} all-to-all(bf16[8,32,256]{2,1,0:T(8,128)(2,1)S(1)} %broadcast_in_dim.17), channel_id=1, replica_groups=mesh['x'=4,'core'=2,'y'=4,'z'=8] {'x','core'}, dimensions={0} | all-to-all | bytes 262144 | tf_op jit(solution)/shard_map/all_to_all | solution.py:86
  178.3 11.4 %all_to_all.112 = bf16[8,32,256]{2,1,0:T(8,128)(2,1)S(1)} all-to-all(bf16[8,32,256]{2,1,0:T(8,128)(2,1)S(1)} %all_to_all.111), channel_id=1, replica_groups=mesh['x'=4,'core'=2,'y'=4,'z'=8] {'z'}, dimensions={0} | all-to-all | bytes 262144 | tf_op jit(solution)/shard_map/all_to_all | solution.py:87
  191.1 15.5 %all_to_all.113 = bf16[32,32,256]{2,1,0:T(8,128)(2,1)S(1)} all-to-all(bf16[32,32,256]{2,1,0:T(8,128)(2,1)S(1)} %bitcast.103), channel_id=1, replica_groups=mesh['x'=4,'core'=2,'y'=4,'z'=8] {'y','z'}, dimensions={0} | all-to-all | bytes 1048576 | tf_op jit(solution)/shard_map/all_to_all | solution.py:83
  206.7 13.6 %all_to_all.114 = bf16[8,32,256]{2,1,0:T(8,128)(2,1)} all-to-all(bf16[8,32,256]{2,1,0:T(8,128)(2,1)S(1)} %broadcast_in_dim.18), channel_id=1, replica_groups=mesh['x'=4,'core'=2,'y'=4,'z'=8] {'x','core'}, dimensions={0} | all-to-all | bytes 262144 | tf_op jit(solution)/shard_map/all_to_all | solution.py:86
  224.5 7.8 %all-to-all-done.14 = bf16[8,32,256]{2,1,0:T(8,128)(2,1)S(1)} async-done(((bf16[8,32,256]{2,1,0:T(8,128)(2,1)}), bf16[8,32,256]{2,1,0:T(8,128)(2,1)S(1)}, u32[]{:S(2)}, u32[]{:S(2)}) %all-to-all-start.14) | async-done | bytes 131104 | tf_op jit(solution)/shard_map/all_to_all | solution.py:87
  233.7 15.5 %all_to_all.115 = bf16[32,32,256]{2,1,0:T(8,128)(2,1)S(1)} all-to-all(bf16[32,32,256]{2,1,0:T(8,128)(2,1)S(1)} %bitcast.86), channel_id=1, replica_groups=mesh['x'=4,'core'=2,'y'=4,'z'=8] {'y','z'}, dimensions={0} | all-to-all | bytes 1048576 | tf_op jit(solution)/shard_map/all_to_all | solution.py:83
  249.3 13.3 %all_to_all.116 = bf16[8,32,256]{2,1,0:T(8,128)(2,1)S(1)} all-to-all(bf16[8,32,256]{2,1,0:T(8,128)(2,1)S(1)} %broadcast_in_dim.19), channel_id=1, replica_groups=mesh['x'=4,'core'=2,'y'=4,'z'=8] {'x','core'}, dimensions={0} | all-to-all | bytes 262144 | tf_op jit(solution)/shard_map/all_to_all | solution.py:86
  262.6 11.4 %all_to_all.117 = bf16[8,32,256]{2,1,0:T(8,128)(2,1)S(1)} all-to-all(bf16[8,32,256]{2,1,0:T(8,128)(2,1)S(1)} %all_to_all.116), channel_id=1, replica_groups=mesh['x'=4,'core'=2,'y'=4,'z'=8] {'z'}, dimensions={0} | all-to-all | bytes 262144 | tf_op jit(solution)/shard_map/all_to_all | solution.py:87
  275.3 15.6 %all_to_all.118 = bf16[32,32,256]{2,1,0:T(8,128)(2,1)S(1)} all-to-all(bf16[32,32,256]{2,1,0:T(8,128)(2,1)S(1)} %bitcast.104), channel_id=1, replica_groups=mesh['x'=4,'core'=2,'y'=4,'z'=8] {'y','z'}, dimensions={0} | all-to-all | bytes 1048576 | tf_op jit(solution)/shard_map/all_to_all | solution.py:83
  291.0 13.2 %all_to_all.119 = bf16[8,32,256]{2,1,0:T(8,128)(2,1)S(1)} all-to-all(bf16[8,32,256]{2,1,0:T(8,128)(2,1)S(1)} %broadcast_in_dim.20), channel_id=1, replica_groups=mesh['x'=4,'core'=2,'y'=4,'z'=8] {'x','core'}, dimensions={0} | all-to-all | bytes 262144 | tf_op jit(solution)/shard_map/all_to_all | solution.py:86
  304.2 11.4 %all_to_all.120 = bf16[8,32,256]{2,1,0:T(8,128)(2,1)S(1)} all-to-all(bf16[8,32,256]{2,1,0:T(8,128)(2,1)S(1)} %all_to_all.119), channel_id=1, replica_groups=mesh['x'=4,'core'=2,'y'=4,'z'=8] {'z'}, dimensions={0} | all-to-all | bytes 262144 | tf_op jit(solution)/shard_map/all_to_all | solution.py:87
  (59 shorter events, 31.0 us)
Async XLA Ops:
  0.0 40.1 %copy-start.4 = (s32[15,128]{1,0:T(8,128)S(1)}, s32[15,128]{1,0:T(8,128)}, u32[]{:S(2)}) copy-start(s32[15,128]{1,0:T(8,128)} %param.14) | copy-start | bytes 23044
  5.2 26.3 %all-to-all-start = ((bf16[32,32,256]{2,1,0:T(8,128)(2,1)}), bf16[32,32,256]{2,1,0:T(8,128)(2,1)S(1)}, u32[]{:S(2)}, u32[]{:S(2)}) async-start(bf16[32,32,256]{2,1,0:T(8,128)(2,1)} %bitcast.6), calls=%async_computation | async-start | bytes 1048576 | tf_op jit(solution)/shard_map/all_to_all | solution.py:83
  32.3 13.2 %all-to-all-start.1 = ((bf16[8,32,256]{2,1,0:T(8,128)(2,1)}), bf16[8,32,256]{2,1,0:T(8,128)(2,1)}, u32[]{:S(2)}, u32[]{:S(2)}) async-start(bf16[8,32,256]{2,1,0:T(8,128)(2,1)} %broadcast_in_dim.14), calls=%async_computation.1 | async-start | bytes 262144 | tf_op jit(solution)/shard_map/all_to_all | solution.py:86
  45.5 12.0 %all-to-all-start.2 = ((bf16[8,32,256]{2,1,0:T(8,128)(2,1)}), bf16[8,32,256]{2,1,0:T(8,128)(2,1)S(1)}, u32[]{:S(2)}, u32[]{:S(2)}) async-start(bf16[8,32,256]{2,1,0:T(8,128)(2,1)} %all-to-all-done.1), calls=%async_computation.2 | async-start | bytes 262144 | tf_op jit(solution)/shard_map/all_to_all | solution.py:87
  59.4 42.2 %copy-start.6 = (f32[4]{0:T(128)S(1)}, f32[4]{0:T(128)}, u32[]{:S(2)}) copy-start(f32[4]{0:T(128)} %get-tuple-element.46) | copy-start | bytes 52
  134.0 12.0 %all-to-all-start.8 = ((bf16[8,32,256]{2,1,0:T(8,128)(2,1)}), bf16[8,32,256]{2,1,0:T(8,128)(2,1)S(1)}, u32[]{:S(2)}, u32[]{:S(2)}) async-start(bf16[8,32,256]{2,1,0:T(8,128)(2,1)} %all_to_all.109), calls=%async_computation.8 | async-start | bytes 262144 | tf_op jit(solution)/shard_map/all_to_all | solution.py:87
  145.9 3.1 copy-start.3
  147.7 1.4 copy-start
  147.7 42.0 %copy-start.5 = (f32[4]{0:T(128)S(1)}, f32[4]{0:T(128)}, u32[]{:S(2)}) copy-start(f32[4]{0:T(128)} %get-tuple-element.45) | copy-start | bytes 52
  149.2 83.0 %copy-start.1 = (f32[8,256,256]{2,1,0:T(8,128)S(1)}, f32[8,256,256]{2,1,0:T(8,128)}, u32[]{:S(2)}) copy-start(f32[8,256,256]{2,1,0:T(8,128)} %copy-done) | copy-start | bytes 6291460
  149.3 83.0 %copy-start.2 = (f32[256,256]{1,0:T(8,128)S(1)}, f32[256,256]{1,0:T(8,128)}, u32[]{:S(2)}) copy-start(f32[256,256]{1,0:T(8,128)} %get-tuple-element.41) | copy-start | bytes 786436
  220.3 12.0 %all-to-all-start.14 = ((bf16[8,32,256]{2,1,0:T(8,128)(2,1)}), bf16[8,32,256]{2,1,0:T(8,128)(2,1)S(1)}, u32[]{:S(2)}, u32[]{:S(2)}) async-start(bf16[8,32,256]{2,1,0:T(8,128)(2,1)} %all_to_all.114), calls=%async_computation.14 | async-start | bytes 262144 | tf_op jit(solution)/shard_map/all_to_all | solution.py:87

commit v8 on v7

--- a/solution.py
+++ b/solution.py
@@ -62,6 +62,7 @@
     def column_tiles(first, col):
         return tile_rows[first:, col * block_size:(col + 1) * block_size]
     columns_in = right_side.reshape(cols_local, block_size, right_side.shape[3])
+    rhs_width = columns_in.shape[2]
     block_node = node_table(node_blocks, total_blocks)
     row_ids = jnp.arange(rows_local, dtype=jnp.int32) * prow_count + prow_index
     col_ids = jnp.arange(cols_local, dtype=jnp.int32) * pcol_count + pcol_index
@@ -77,36 +78,61 @@
         (row_nodes[:, None] == col_nodes[None, :]) & (row_ids[:, None] >= col_ids[None, :])
     ).astype(jnp.int32)
 
-    def reduce_route(level_terms):
-        rhs_width = level_terms.shape[2]
+    def reduce_gather(level_terms):
         pieces = level_terms.astype(jnp.bfloat16).reshape(pcol_count, chunk_rows, rhs_width)
         got = lax.all_to_all(pieces, PCOL, 0, 0, tiled=True)
         summed = jnp.sum(got.astype(jnp.float32), axis=0).astype(jnp.bfloat16)
         spread = jnp.broadcast_to(summed[None], (prow_count,) + summed.shape)
-        gathered = lax.all_to_all(spread, PROW, 0, 0, tiled=True)
-        arrived = lax.all_to_all(gathered, RING, 0, 0, tiled=True)
-        return arrived.reshape(block_size, rhs_width)
+        return lax.all_to_all(spread, PROW, 0, 0, tiled=True)
 
-    rhs_width = columns_in.shape[2]
+    def route_ring(gathered, extra):
+        flat = gathered.reshape(ring, chunk_rows * rhs_width)
+        if extra is not None:
+            flat = jnp.concatenate([flat, extra], axis=1)
+        arrived = lax.all_to_all(flat, RING, 0, 0, tiled=True)
+        solved = arrived[:, : chunk_rows * rhs_width].reshape(block_size, rhs_width)
+        return solved, (arrived[:, chunk_rows * rhs_width :] if extra is not None else None)
+
+    def ring_chunks(section):
+        tiles = column_tiles(section * level_rows, section)[:level_rows]
+        split = tiles.reshape(level_rows, block_size, ring, chunk_rows)
+        return jnp.transpose(split, (2, 0, 1, 3)).reshape(ring, level_rows * block_size * chunk_rows)
+
+    ring_index = pcol_index % ring
+    group_base = pcol_index - ring_index
     row_in_group = prow_index + prow_count * jnp.arange(level_rows, dtype=jnp.int32)
     owns_row = (row_in_group == pcol_index).astype(jnp.float32)
+    ring_cols = group_base + jnp.arange(ring, dtype=jnp.int32)
+
     partial_value = jnp.zeros((rows_local, block_size, rhs_width), jnp.float32)
     solved_list = []
+    chunks_in = None
     for section_now in range(LEVELS):
         first_row = section_now * level_rows
         after_row = first_row + level_rows
         if section_now == 0:
-            rhs_column = columns_in[0]
+            diag_terms = panel_products(
+                column_tiles(first_row, section_now)[:level_rows],
+                diag_bits[first_row:after_row, section_now],
+                columns_in[0],
+            )
         else:
             own_b = columns_in[section_now].astype(jnp.float32)
             contrib = owns_row[:, None, None] * own_b[None] - partial_value[first_row:after_row]
-            rhs_column = reduce_route(contrib)
-        diag_terms = panel_products(
-            column_tiles(first_row, section_now)[:level_rows],
-            diag_bits[first_row:after_row, section_now],
-            rhs_column,
-        )
-        solved = reduce_route(diag_terms)
+            rhs_chunks = reduce_gather(contrib)
+            level_row_ids = section_now * pcol_count + row_in_group
+            level_col_ids = section_now * pcol_count + ring_cols
+            row_node = lookup(block_node, level_row_ids)
+            col_node = lookup(block_node, level_col_ids)
+            live = (col_node[:, None] == row_node[None, :]) & (level_col_ids[:, None] <= level_row_ids[None, :])
+            tiles = chunks_in.reshape(ring, level_rows, block_size, chunk_rows)
+            tiles = tiles * live.astype(jnp.bfloat16)[:, :, None, None]
+            tiles = jnp.transpose(tiles, (1, 2, 0, 3)).reshape(level_rows, block_size, block_size)
+            diag_terms = jnp.einsum(
+                "kxy,yw->kxw", tiles, rhs_chunks.reshape(block_size, rhs_width), preferred_element_type=jnp.float32
+            )
+        extra = ring_chunks(section_now + 1) if section_now + 1 < LEVELS else None
+        solved, chunks_in = route_ring(reduce_gather(diag_terms), extra)
         solved_list.append(solved)
         if section_now + 1 < LEVELS:
             update_terms = panel_products(

time: 318 us -> 377 us (1.19)
  blocking collectives: 221 us -> 131 us
  local copies, waits for them, and re-layouts: 2.1 us -> 53.6 us
  waiting for transfers between devices: 40.8 us -> 90.6 us
  starting transfers between devices: 32.2 us -> 66.2 us
  other arithmetic: 9.41 us -> 20.5 us
    all_to_all x16 -> x7, blocking collectives: 221 us -> 131 us  [the longest x6 120 us: reduce_gather(): got = lax.all_to_all(pieces, PCOL, 0, 0, tiled=True)]
    all_to_all x5 -> x11, waiting for transfers between devices: 40.8 us -> 90.6 us  [the longest x4 68.1 us: route_ring(): arrived = lax.all_to_all(flat, RING, 0, 0, tiled=True)]
    all_to_all x5 -> x11, starting transfers between devices: 32.2 us -> 66.2 us  [the longest x6 45.1 us: reduce_gather(): return lax.all_to_all(spread, PROW, 0, 0, tiled=True)]
    unnamed x14 -> x64, local copies, waits for them, and re-layouts: 1.36 us -> 20.1 us
    reshape x0 -> x9, local copies, waits for them, and re-layouts: none -> 17 us  [the longest x3 9.01 us: ring_chunks(): jnp.transpose(split, (2, 0, 1, 3))]
    all_to_all x0 -> x8, other arithmetic: none -> 9.19 us  [route_ring(): arrived = lax.all_to_all(flat, RING, 0, 0, tiled=True)]
    slice x0 -> x10, local copies, waits for them, and re-layouts: none -> 6.88 us  [the longest x3 4.69 us: ring_chunks(): tiles = column_tiles(section * level_rows, section)[:level_rows]]
    dot_general x0 -> x3, matrix products: none -> 5.91 us  [local(): jnp.einsum('kxy,yw->kxw', tiles, rhs_chunks.reshape(block_size, rhs_width...]
  transfers between devices with their start and end apart: 5 -> 11, of which waited for: 5 -> 8; matrix products, arithmetic and copies ran while one was open for 1% -> 8% of each run, Pallas kernels for 0% -> 0%
where the time goes in v8:
time: 377 us; the launch traced here: 375 us
  blocking collectives  131 us (35%)
  waiting for transfers between devices  90.6 us (24%)
  starting transfers between devices  66.2 us (18%)
  local copies, waits for them, and re-layouts  53.6 us (14%)
  other arithmetic  20.5 us (5%)
  matrix products  12.6 us (3%)
    all_to_all x6, blocking collectives, reduce_gather(): got = lax.all_to_all(pieces, PCOL, 0, 0, tiled=True)  120 us
    all_to_all x4, waiting for transfers between devices, route_ring(): arrived = lax.all_to_all(flat, RING, 0, 0, tiled=True)  68.1 us
    all_to_all x6, starting transfers between devices, reduce_gather(): return lax.all_to_all(spread, PROW, 0, 0, tiled=True)  45.1 us
    unnamed x64, local copies, waits for them, and re-layouts  20.1 us
    all_to_all x4, starting transfers between devices, route_ring(): arrived = lax.all_to_all(flat, RING, 0, 0, tiled=True)  16.5 us
    all_to_all x1, waiting for transfers between devices, reduce_gather(): got = lax.all_to_all(pieces, PCOL, 0, 0, tiled=True)  13.6 us
    all_to_all x1, blocking collectives, reduce_gather(): return lax.all_to_all(spread, PROW, 0, 0, tiled=True)  11.6 us
    all_to_all x8, other arithmetic, route_ring(): arrived = lax.all_to_all(flat, RING, 0, 0, tiled=True)  9.19 us
  transfers between devices with their start and end apart: 11, of which 8 were waited for; matrix products, arithmetic and copies ran while one was open for 8% of the time, Pallas kernels for 0%

profile of v8, /device:TPU:1, one launch (start us, length us, event | category | flops | bytes accessed | tf_op | source)
XLA Modules:
  0.0 375.4 jit_solution(16830855403257870382)
XLA Ops:
  4.3 26.1 %all_to_all.116 = bf16[32,32,256]{2,1,0:T(8,128)(2,1)S(1)} all-to-all(bf16[32,32,256]{2,1,0:T(8,128)(2,1)S(1)} %bitcast.158), channel_id=1, replica_groups=mesh['x'=4,'core'=2,'y'=4,'z'=8] {'y','z'}, dimensions={0} | all-to-all | bytes 1048576 | tf_op jit(solution)/shard_map/all_to_all | solution.py:83
  31.2 7.8 %all-to-all-start.1 = ((bf16[8,32,256]{2,1,0:T(8,128)(2,1)}), bf16[8,32,256]{2,1,0:T(8,128)(2,1)S(1)}, u32[]{:S(2)}, u32[]{:S(2)}) async-start(bf16[8,32,256]{2,1,0:T(8,128)(2,1)} %broadcast_in_dim.14), calls=%async_computation.1 | async-start | bytes 262144 | tf_op jit(solution)/shard_map/all_to_all | solution.py:86
  48.1 4.1 %all-to-all-start.2 = ((bf16[8,2,20480]{2,1,0:T(2,128)(2,1)}), bf16[8,2,20480]{2,1,0:T(2,128)(2,1)S(1)}, u32[]{:S(2)}, u32[]{:S(2)}) async-start(bf16[8,2,20480]{2,1,0:T(2,128)(2,1)} %reshape.578), calls=%async_computation.2 | async-start | bytes 1310720 | tf_op jit(solution)/shard_map/all_to_all | solution.py:92
  54.0 19.0 %all-to-all-done.2 = bf16[8,2,20480]{2,1,0:T(2,128)(2,1)S(1)} async-done(((bf16[8,2,20480]{2,1,0:T(2,128)(2,1)}), bf16[8,2,20480]{2,1,0:T(2,128)(2,1)S(1)}, u32[]{:S(2)}, u32[]{:S(2)}) %all-to-all-start.2) | async-done | bytes 655392 | tf_op jit(solution)/shard_map/all_to_all | solution.py:92
  79.0 4.6 %all-to-all-start.3 = ((bf16[32,32,256]{2,1,0:T(8,128)(2,1)}), bf16[32,32,256]{2,1,0:T(8,128)(2,1)}, u32[]{:S(2)}, u32[]{:S(2)}) async-start(bf16[32,32,256]{2,1,0:T(8,128)(2,1)} %bitcast.149), calls=%async_computation.3 | async-start | bytes 1048576 | tf_op jit(solution)/shard_map/all_to_all | solution.py:83
  84.4 13.6 %all-to-all-done.3 = bf16[32,32,256]{2,1,0:T(8,128)(2,1)} async-done(((bf16[32,32,256]{2,1,0:T(8,128)(2,1)}), bf16[32,32,256]{2,1,0:T(8,128)(2,1)}, u32[]{:S(2)}, u32[]{:S(2)}) %all-to-all-start.3) | async-done | bytes 524320 | tf_op jit(solution)/shard_map/all_to_all | solution.py:83
  99.8 7.6 %all-to-all-start.4 = ((bf16[8,32,256]{2,1,0:T(8,128)(2,1)}), bf16[8,32,256]{2,1,0:T(8,128)(2,1)S(1)}, u32[]{:S(2)}, u32[]{:S(2)}) async-start(bf16[8,32,256]{2,1,0:T(8,128)(2,1)} %broadcast_in_dim.15), calls=%async_computation.4 | async-start | bytes 262144 | tf_op jit(solution)/shard_map/all_to_all | solution.py:86
  116.7 20.2 %all_to_all.117 = bf16[32,32,256]{2,1,0:T(8,128)(2,1)} all-to-all(bf16[32,32,256]{2,1,0:T(8,128)(2,1)S(1)} %bitcast.155), channel_id=1, replica_groups=mesh['x'=4,'core'=2,'y'=4,'z'=8] {'y','z'}, dimensions={0} | all-to-all | bytes 1048576 | tf_op jit(solution)/shard_map/all_to_all | solution.py:83
  138.7 7.3 %all-to-all-start.6 = ((bf16[8,32,256]{2,1,0:T(8,128)(2,1)}), bf16[8,32,256]{2,1,0:T(8,128)(2,1)S(1)}, u32[]{:S(2)}, u32[]{:S(2)}) async-start(bf16[8,32,256]{2,1,0:T(8,128)(2,1)} %broadcast_in_dim.16), calls=%async_computation.6 | async-start | bytes 262144 | tf_op jit(solution)/shard_map/all_to_all | solution.py:86
  150.7 4.6 %reshape.548 = bf16[8,32768]{1,0:T(8,128)(2,1)} reshape(bf16[8,4,256,32]{3,2,1,0:T(8,128)(2,1)} %copy.47) | data formatting | bytes 1048576 | tf_op jit(solution)/shard_map/reshape | solution.py:99
  162.6 4.3 %all-to-all-start.7 = ((bf16[8,2,20480]{2,1,0:T(2,128)(2,1)}), bf16[8,2,20480]{2,1,0:T(2,128)(2,1)}, u32[]{:S(2)}, u32[]{:S(2)}) async-start(bf16[8,2,20480]{2,1,0:T(2,128)(2,1)} %reshape.580), calls=%async_computation.7 | async-start | bytes 1310720 | tf_op jit(solution)/shard_map/all_to_all | solution.py:92
  166.9 20.8 %all-to-all-done.7 = bf16[8,2,20480]{2,1,0:T(2,128)(2,1)} async-done(((bf16[8,2,20480]{2,1,0:T(2,128)(2,1)}), bf16[8,2,20480]{2,1,0:T(2,128)(2,1)}, u32[]{:S(2)}, u32[]{:S(2)}) %all-to-all-start.7) | async-done | bytes 655392 | tf_op jit(solution)/shard_map/all_to_all | solution.py:92
  197.7 17.7 %all_to_all.118 = bf16[32,32,256]{2,1,0:T(8,128)(2,1)S(1)} all-to-all(bf16[32,32,256]{2,1,0:T(8,128)(2,1)S(1)} %bitcast.151), channel_id=1, replica_groups=mesh['x'=4,'core'=2,'y'=4,'z'=8] {'y','z'}, dimensions={0} | all-to-all | bytes 1048576 | tf_op jit(solution)/shard_map/all_to_all | solution.py:83
  216.1 7.7 %all-to-all-start.9 = ((bf16[8,32,256]{2,1,0:T(8,128)(2,1)}), bf16[8,32,256]{2,1,0:T(8,128)(2,1)S(1)}, u32[]{:S(2)}, u32[]{:S(2)}) async-start(bf16[8,32,256]{2,1,0:T(8,128)(2,1)} %broadcast_in_dim.17), calls=%async_computation.9 | async-start | bytes 262144 | tf_op jit(solution)/shard_map/all_to_all | solution.py:86
  230.2 19.0 %all_to_all.119 = bf16[32,32,256]{2,1,0:T(8,128)(2,1)S(1)} all-to-all(bf16[32,32,256]{2,1,0:T(8,128)(2,1)S(1)} %bitcast.156), channel_id=1, replica_groups=mesh['x'=4,'core'=2,'y'=4,'z'=8] {'y','z'}, dimensions={0} | all-to-all | bytes 1048576 | tf_op jit(solution)/shard_map/all_to_all | solution.py:83
  250.0 7.3 %all-to-all-start.11 = ((bf16[8,32,256]{2,1,0:T(8,128)(2,1)}), bf16[8,32,256]{2,1,0:T(8,128)(2,1)S(1)}, u32[]{:S(2)}, u32[]{:S(2)}) async-start(bf16[8,32,256]{2,1,0:T(8,128)(2,1)} %broadcast_in_dim.18), calls=%async_computation.11 | async-start | bytes 262144 | tf_op jit(solution)/shard_map/all_to_all | solution.py:86
  265.1 4.2 %all-to-all-start.12 = ((bf16[8,2,20480]{2,1,0:T(2,128)(2,1)}), bf16[8,2,20480]{2,1,0:T(2,128)(2,1)}, u32[]{:S(2)}, u32[]{:S(2)}) async-start(bf16[8,2,20480]{2,1,0:T(2,128)(2,1)} %reshape.582), calls=%async_computation.12 | async-start | bytes 1310720 | tf_op jit(solution)/shard_map/all_to_all | solution.py:92
  269.4 20.7 %all-to-all-done.12 = bf16[8,2,20480]{2,1,0:T(2,128)(2,1)} async-done(((bf16[8,2,20480]{2,1,0:T(2,128)(2,1)}), bf16[8,2,20480]{2,1,0:T(2,128)(2,1)}, u32[]{:S(2)}, u32[]{:S(2)}) %all-to-all-start.12) | async-done | bytes 655392 | tf_op jit(solution)/shard_map/all_to_all | solution.py:92
  295.7 17.3 %all_to_all.120 = bf16[32,32,256]{2,1,0:T(8,128)(2,1)S(1)} all-to-all(bf16[32,32,256]{2,1,0:T(8,128)(2,1)S(1)} %bitcast.150), channel_id=1, replica_groups=mesh['x'=4,'core'=2,'y'=4,'z'=8] {'y','z'}, dimensions={0} | all-to-all | bytes 1048576 | tf_op jit(solution)/shard_map/all_to_all | solution.py:83
  313.7 7.4 %all-to-all-start.14 = ((bf16[8,32,256]{2,1,0:T(8,128)(2,1)}), bf16[8,32,256]{2,1,0:T(8,128)(2,1)}, u32[]{:S(2)}, u32[]{:S(2)}) async-start(bf16[8,32,256]{2,1,0:T(8,128)(2,1)} %broadcast_in_dim.19), calls=%async_computation.14 | async-start | bytes 262144 | tf_op jit(solution)/shard_map/all_to_all | solution.py:86
  328.6 19.3 %all_to_all.121 = bf16[32,32,256]{2,1,0:T(8,128)(2,1)S(1)} all-to-all(bf16[32,32,256]{2,1,0:T(8,128)(2,1)S(1)} %bitcast.157), channel_id=1, replica_groups=mesh['x'=4,'core'=2,'y'=4,'z'=8] {'y','z'}, dimensions={0} | all-to-all | bytes 1048576 | tf_op jit(solution)/shard_map/all_to_all | solution.py:83
  348.0 11.6 %all_to_all.122 = bf16[8,32,256]{2,1,0:T(8,128)(2,1)S(1)} all-to-all(bf16[8,32,256]{2,1,0:T(8,128)(2,1)S(1)} %broadcast_in_dim.20), channel_id=1, replica_groups=mesh['x'=4,'core'=2,'y'=4,'z'=8] {'x','core'}, dimensions={0} | all-to-all | bytes 262144 | tf_op jit(solution)/shard_map/all_to_all | solution.py:86
  361.8 3.9 %all-to-all-start.17 = ((bf16[8,2,4096]{2,1,0:T(2,128)(2,1)}), bf16[8,2,4096]{2,1,0:T(2,128)(2,1)S(1)}, u32[]{:S(2)}, u32[]{:S(2)}) async-start(bf16[8,2,4096]{2,1,0:T(2,128)(2,1)} %reshape.584), calls=%async_computation.17 | async-start | bytes 262144 | tf_op jit(solution)/shard_map/all_to_all | solution.py:92
  365.9 7.6 %all-to-all-done.17 = bf16[8,2,4096]{2,1,0:T(2,128)(2,1)S(1)} async-done(((bf16[8,2,4096]{2,1,0:T(2,128)(2,1)}), bf16[8,2,4096]{2,1,0:T(2,128)(2,1)S(1)}, u32[]{:S(2)}, u32[]{:S(2)}) %all-to-all-start.17) | async-done | bytes 131104 | tf_op jit(solution)/shard_map/all_to_all | solution.py:92
  (155 shorter events, 90.9 us)
Async XLA Ops:
  0.0 41.5 %copy-start.13 = (s32[4]{0:T(128)}, s32[4]{0:T(128)S(1)}, u32[]{:S(2)}) copy-start(s32[4]{0:T(128)S(1)} %get-tuple-element.54) | copy-start | bytes 52
  0.0 41.5 %copy-start.16 = (s32[4]{0:T(128)}, s32[4]{0:T(128)S(1)}, u32[]{:S(2)}) copy-start(s32[4]{0:T(128)S(1)} %get-tuple-element.55) | copy-start | bytes 52
  31.2 13.7 %all-to-all-start.1 = ((bf16[8,32,256]{2,1,0:T(8,128)(2,1)}), bf16[8,32,256]{2,1,0:T(8,128)(2,1)S(1)}, u32[]{:S(2)}, u32[]{:S(2)}) async-start(bf16[8,32,256]{2,1,0:T(8,128)(2,1)} %broadcast_in_dim.14), calls=%async_computation.1 | async-start | bytes 262144 | tf_op jit(solution)/shard_map/all_to_all | solution.py:86
  48.1 24.9 %all-to-all-start.2 = ((bf16[8,2,20480]{2,1,0:T(2,128)(2,1)}), bf16[8,2,20480]{2,1,0:T(2,128)(2,1)S(1)}, u32[]{:S(2)}, u32[]{:S(2)}) async-start(bf16[8,2,20480]{2,1,0:T(2,128)(2,1)} %reshape.578), calls=%async_computation.2 | async-start | bytes 1310720 | tf_op jit(solution)/shard_map/all_to_all | solution.py:92
  79.0 19.1 %all-to-all-start.3 = ((bf16[32,32,256]{2,1,0:T(8,128)(2,1)}), bf16[32,32,256]{2,1,0:T(8,128)(2,1)}, u32[]{:S(2)}, u32[]{:S(2)}) async-start(bf16[32,32,256]{2,1,0:T(8,128)(2,1)} %bitcast.149), calls=%async_computation.3 | async-start | bytes 1048576 | tf_op jit(solution)/shard_map/all_to_all | solution.py:83
  99.8 14.1 %all-to-all-start.4 = ((bf16[8,32,256]{2,1,0:T(8,128)(2,1)}), bf16[8,32,256]{2,1,0:T(8,128)(2,1)S(1)}, u32[]{:S(2)}, u32[]{:S(2)}) async-start(bf16[8,32,256]{2,1,0:T(8,128)(2,1)} %broadcast_in_dim.15), calls=%async_computation.4 | async-start | bytes 262144 | tf_op jit(solution)/shard_map/all_to_all | solution.py:86
  138.7 16.6 %all-to-all-start.6 = ((bf16[8,32,256]{2,1,0:T(8,128)(2,1)}), bf16[8,32,256]{2,1,0:T(8,128)(2,1)S(1)}, u32[]{:S(2)}, u32[]{:S(2)}) async-start(bf16[8,32,256]{2,1,0:T(8,128)(2,1)} %broadcast_in_dim.16), calls=%async_computation.6 | async-start | bytes 262144 | tf_op jit(solution)/shard_map/all_to_all | solution.py:86
  162.6 25.2 %all-to-all-start.7 = ((bf16[8,2,20480]{2,1,0:T(2,128)(2,1)}), bf16[8,2,20480]{2,1,0:T(2,128)(2,1)}, u32[]{:S(2)}, u32[]{:S(2)}) async-start(bf16[8,2,20480]{2,1,0:T(2,128)(2,1)} %reshape.580), calls=%async_computation.7 | async-start | bytes 1310720 | tf_op jit(solution)/shard_map/all_to_all | solution.py:92
  196.1 27.7 %copy-start.17 = (s32[4]{0:T(128)S(1)}, s32[4]{0:T(128)}, u32[]{:S(2)}) copy-start(s32[4]{0:T(128)} %copy-done.16) | copy-start | bytes 52
  196.1 27.7 %copy-start.18 = (s32[4]{0:T(128)S(1)}, s32[4]{0:T(128)}, u32[]{:S(2)}) copy-start(s32[4]{0:T(128)} %get-tuple-element.46) | copy-start | bytes 52
  196.1 27.7 %copy-start.23 = (s32[8]{0:T(128)S(1)}, s32[8]{0:T(128)}, u32[]{:S(2)}) copy-start(s32[8]{0:T(128)} %copy-done.22) | copy-start | bytes 100
  196.1 27.7 %copy-start.24 = (s32[8]{0:T(128)S(1)}, s32[8]{0:T(128)}, u32[]{:S(2)}) copy-start(s32[8]{0:T(128)} %get-tuple-element.42) | copy-start | bytes 100
  196.1 27.8 %copy-start.6 = (bf16[8,1,40960]{2,0,1:T(8,128)(2,1)S(1)}, bf16[8,1,40960]{2,0,1:T(8,128)(2,1)}, u32[]{:S(2)}) copy-start(bf16[8,1,40960]{2,0,1:T(8,128)(2,1)} %copy-done.5) | copy-start | bytes 1966084
  216.1 13.0 %all-to-all-start.9 = ((bf16[8,32,256]{2,1,0:T(8,128)(2,1)}), bf16[8,32,256]{2,1,0:T(8,128)(2,1)S(1)}, u32[]{:S(2)}, u32[]{:S(2)}) async-start(bf16[8,32,256]{2,1,0:T(8,128)(2,1)} %broadcast_in_dim.17), calls=%async_computation.9 | async-start | bytes 262144 | tf_op jit(solution)/shard_map/all_to_all | solution.py:86
  225.6 31.6 %copy-start.7 = (bf16[4,256,256]{2,1,0:T(8,128)(2,1)S(1)}, bf16[4,256,256]{2,1,0:T(8,128)(2,1)}, u32[]{:S(2)}) copy-start(bf16[4,256,256]{2,1,0:T(8,128)(2,1)} %get-tuple-element.49) | copy-start | bytes 1572868
  250.0 12.6 %all-to-all-start.11 = ((bf16[8,32,256]{2,1,0:T(8,128)(2,1)}), bf16[8,32,256]{2,1,0:T(8,128)(2,1)S(1)}, u32[]{:S(2)}, u32[]{:S(2)}) async-start(bf16[8,32,256]{2,1,0:T(8,128)(2,1)} %broadcast_in_dim.18), calls=%async_computation.11 | async-start | bytes 262144 | tf_op jit(solution)/shard_map/all_to_all | solution.py:86
  265.1 25.0 %all-to-all-start.12 = ((bf16[8,2,20480]{2,1,0:T(2,128)(2,1)}), bf16[8,2,20480]{2,1,0:T(2,128)(2,1)}, u32[]{:S(2)}, u32[]{:S(2)}) async-start(bf16[8,2,20480]{2,1,0:T(2,128)(2,1)} %reshape.582), calls=%async_computation.12 | async-start | bytes 1310720 | tf_op jit(solution)/shard_map/all_to_all | solution.py:92
  294.1 27.0 %copy-start.14 = (s32[4]{0:T(128)S(1)}, s32[4]{0:T(128)}, u32[]{:S(2)}) copy-start(s32[4]{0:T(128)} %copy-done.13) | copy-start | bytes 52
  294.1 27.0 %copy-start.15 = (s32[4]{0:T(128)S(1)}, s32[4]{0:T(128)}, u32[]{:S(2)}) copy-start(s32[4]{0:T(128)} %get-tuple-element.44) | copy-start | bytes 52
  294.1 27.0 %copy-start.20 = (s32[8]{0:T(128)S(1)}, s32[8]{0:T(128)}, u32[]{:S(2)}) copy-start(s32[8]{0:T(128)} %copy-done.19) | copy-start | bytes 100
  294.1 27.1 %copy-start.4 = (bf16[8,1,40960]{2,0,1:T(8,128)(2,1)S(1)}, bf16[8,1,40960]{2,0,1:T(8,128)(2,1)}, u32[]{:S(2)}) copy-start(bf16[8,1,40960]{2,0,1:T(8,128)(2,1)} %copy-done.3) | copy-start | bytes 1966084
  313.7 12.8 %all-to-all-start.14 = ((bf16[8,32,256]{2,1,0:T(8,128)(2,1)}), bf16[8,32,256]{2,1,0:T(8,128)(2,1)}, u32[]{:S(2)}, u32[]{:S(2)}) async-start(bf16[8,32,256]{2,1,0:T(8,128)(2,1)} %broadcast_in_dim.19), calls=%async_computation.14 | async-start | bytes 262144 | tf_op jit(solution)/shard_map/all_to_all | solution.py:86
  328.6 37.2 %copy-start.9 = (bf16[8,8192]{1,0:T(8,128)(2,1)S(1)}, bf16[8,8192]{1,0:T(8,128)(2,1)}, u32[]{:S(2)}) copy-start(bf16[8,8192]{1,0:T(8,128)(2,1)} %copy-done.8) | copy-start | bytes 393220
  361.8 11.8 %all-to-all-start.17 = ((bf16[8,2,4096]{2,1,0:T(2,128)(2,1)}), bf16[8,2,4096]{2,1,0:T(2,128)(2,1)S(1)}, u32[]{:S(2)}, u32[]{:S(2)}) async-start(bf16[8,2,4096]{2,1,0:T(2,128)(2,1)} %reshape.584), calls=%async_computation.17 | async-start | bytes 262144 | tf_op jit(solution)/shard_map/all_to_all | solution.py:92
  (12 other events, 77.2 us)

commit v9 on v6

--- a/solution.py
+++ b/solution.py
@@ -88,7 +88,7 @@
         return arrived.reshape(block_size, rhs_width)
 
     rhs_width = columns_in.shape[2]
-    partial_value = jnp.zeros((rows_local, block_size, rhs_width), jnp.float32)
+    partial_levels = [None] * LEVELS
     solved_list = []
     for section_now in range(LEVELS):
         first_row = section_now * level_rows
@@ -96,7 +96,7 @@
         if section_now == 0:
             rhs_column = columns_in[0]
         else:
-            update = reduce_route(partial_value[first_row:after_row]).astype(jnp.float32)
+            update = reduce_route(partial_levels[section_now]).astype(jnp.float32)
             rhs_column = (columns_in[section_now].astype(jnp.float32) - update).astype(jnp.bfloat16)
         diag_terms = panel_products(
             column_tiles(first_row, section_now)[:level_rows],
@@ -105,11 +105,17 @@
         )
         solved = reduce_route(diag_terms)
         solved_list.append(solved)
-        if section_now + 1 < LEVELS:
+        for later in range(section_now + 1, LEVELS):
+            later_row = later * level_rows
             update_terms = panel_products(
-                column_tiles(after_row, section_now), front_bits[after_row:, section_now], solved
+                column_tiles(later_row, section_now)[:level_rows],
+                front_bits[later_row:later_row + level_rows, section_now],
+                solved,
             )
-            partial_value = partial_value.at[after_row:].add(update_terms)
+            if partial_levels[later] is None:
+                partial_levels[later] = update_terms
+            else:
+                partial_levels[later] = partial_levels[later] + update_terms
     solution = jnp.stack(solved_list)
     return solution.reshape(cols_local, 1, block_size, columns_in.shape[2])
 

time: 317 us -> 313 us (0.987)
  blocking collectives: 220 us -> 206 us
  starting transfers between devices: 32.2 us -> 41.3 us
    all_to_all x6 -> x5, blocking collectives: 79.8 us -> 66.6 us  [reduce_route(): gathered = lax.all_to_all(spread, PROW, 0, 0, tiled=True)]
    all_to_all x1 -> x2, starting transfers between devices: 7.8 us -> 16.9 us  [reduce_route(): gathered = lax.all_to_all(spread, PROW, 0, 0, tiled=True)]
    all_to_all x1 -> x2, waiting for transfers between devices: 4.59 us -> 8.64 us  [reduce_route(): gathered = lax.all_to_all(spread, PROW, 0, 0, tiled=True)]
    dot_general x7 -> x10, matrix products: 11.8 us -> 14.4 us  [panel_products(): jnp.einsum('nxy,yw->nxw', tile_stack, vector, preferred_element_type=jnp....]
  transfers between devices with their start and end apart: 5 -> 6, of which waited for: 5 -> 6; matrix products, arithmetic and copies ran while one was open for 0% -> 2% of each run, Pallas kernels for 0% -> 0%
where the time goes in v9:
time: 313 us; the launch traced here: 311 us
  blocking collectives  206 us (66%)
  waiting for transfers between devices  43.5 us (14%)
  starting transfers between devices  41.3 us (13%)
  matrix products  14.4 us (5%)
  other arithmetic  4.95 us (2%)
    all_to_all x6, blocking collectives, reduce_route(): got = lax.all_to_all(pieces, PCOL, 0, 0, tiled=True)  93.3 us
    all_to_all x5, blocking collectives, reduce_route(): gathered = lax.all_to_all(spread, PROW, 0, 0, tiled=True)  66.6 us
    all_to_all x4, blocking collectives, reduce_route(): arrived = lax.all_to_all(gathered, RING, 0, 0, tiled=True)  45.7 us
    all_to_all x3, waiting for transfers between devices, reduce_route(): arrived = lax.all_to_all(gathered, RING, 0, 0, tiled=True)  20.6 us
    all_to_all x2, starting transfers between devices, reduce_route(): gathered = lax.all_to_all(spread, PROW, 0, 0, tiled=True)  16.9 us
    dot_general x10, matrix products, panel_products(): jnp.einsum('nxy,yw->nxw', tile_stack, vector, preferred_element_type=jnp....  14.4 us
    all_to_all x1, waiting for transfers between devices, reduce_route(): got = lax.all_to_all(pieces, PCOL, 0, 0, tiled=True)  14.2 us
    all_to_all x3, starting transfers between devices, reduce_route(): arrived = lax.all_to_all(gathered, RING, 0, 0, tiled=True)  12.4 us
  transfers between devices with their start and end apart: 6, of which 6 were waited for; matrix products, arithmetic and copies ran while one was open for 2% of the time, Pallas kernels for 0%

profile of v9, /device:TPU:1, one launch (start us, length us, event | category | flops | bytes accessed | tf_op | source)
XLA Modules:
  0.0 311.2 jit_solution(7036101314707102993)
XLA Ops:
  4.6 12.0 %all-to-all-start = ((bf16[32,32,256]{2,1,0:T(8,128)(2,1)}), bf16[32,32,256]{2,1,0:T(8,128)(2,1)S(1)}, u32[]{:S(2)}, u32[]{:S(2)}) async-start(bf16[32,32,256]{2,1,0:T(8,128)(2,1)} %bitcast.6), calls=%async_computation | async-start | bytes 1048576 | tf_op jit(solution)/shard_map/all_to_all | solution.py:83
  16.8 14.2 %all-to-all-done = bf16[32,32,256]{2,1,0:T(8,128)(2,1)S(1)} async-done(((bf16[32,32,256]{2,1,0:T(8,128)(2,1)}), bf16[32,32,256]{2,1,0:T(8,128)(2,1)S(1)}, u32[]{:S(2)}, u32[]{:S(2)}) %all-to-all-start) | async-done | bytes 524320 | tf_op jit(solution)/shard_map/all_to_all | solution.py:83
  31.7 7.8 %all-to-all-start.1 = ((bf16[8,32,256]{2,1,0:T(8,128)(2,1)}), bf16[8,32,256]{2,1,0:T(8,128)(2,1)}, u32[]{:S(2)}, u32[]{:S(2)}) async-start(bf16[8,32,256]{2,1,0:T(8,128)(2,1)} %broadcast_in_dim.14), calls=%async_computation.1 | async-start | bytes 262144 | tf_op jit(solution)/shard_map/all_to_all | solution.py:86
  40.3 4.6 %all-to-all-done.1 = bf16[8,32,256]{2,1,0:T(8,128)(2,1)} async-done(((bf16[8,32,256]{2,1,0:T(8,128)(2,1)}), bf16[8,32,256]{2,1,0:T(8,128)(2,1)}, u32[]{:S(2)}, u32[]{:S(2)}) %all-to-all-start.1) | async-done | bytes 131104 | tf_op jit(solution)/shard_map/all_to_all | solution.py:86
  44.9 4.1 %all-to-all-start.2 = ((bf16[8,32,256]{2,1,0:T(8,128)(2,1)}), bf16[8,32,256]{2,1,0:T(8,128)(2,1)S(1)}, u32[]{:S(2)}, u32[]{:S(2)}) async-start(bf16[8,32,256]{2,1,0:T(8,128)(2,1)} %all-to-all-done.1), calls=%async_computation.2 | async-start | bytes 262144 | tf_op jit(solution)/shard_map/all_to_all | solution.py:87
  49.3 7.6 %all-to-all-done.2 = bf16[8,32,256]{2,1,0:T(8,128)(2,1)S(1)} async-done(((bf16[8,32,256]{2,1,0:T(8,128)(2,1)}), bf16[8,32,256]{2,1,0:T(8,128)(2,1)S(1)}, u32[]{:S(2)}, u32[]{:S(2)}) %all-to-all-start.2) | async-done | bytes 131104 | tf_op jit(solution)/shard_map/all_to_all | solution.py:87
  58.2 15.5 %all_to_all.105 = bf16[32,32,256]{2,1,0:T(8,128)(2,1)S(1)} all-to-all(bf16[32,32,256]{2,1,0:T(8,128)(2,1)S(1)} %bitcast.125), channel_id=1, replica_groups=mesh['x'=4,'core'=2,'y'=4,'z'=8] {'y','z'}, dimensions={0} | all-to-all | bytes 1048576 | tf_op jit(solution)/shard_map/all_to_all | solution.py:83
  73.9 13.2 %all_to_all.106 = bf16[8,32,256]{2,1,0:T(8,128)(2,1)S(1)} all-to-all(bf16[8,32,256]{2,1,0:T(8,128)(2,1)S(1)} %broadcast_in_dim.15), channel_id=1, replica_groups=mesh['x'=4,'core'=2,'y'=4,'z'=8] {'x','core'}, dimensions={0} | all-to-all | bytes 262144 | tf_op jit(solution)/shard_map/all_to_all | solution.py:86
  87.1 11.4 %all_to_all.107 = bf16[8,32,256]{2,1,0:T(8,128)(2,1)S(1)} all-to-all(bf16[8,32,256]{2,1,0:T(8,128)(2,1)S(1)} %all_to_all.106), channel_id=1, replica_groups=mesh['x'=4,'core'=2,'y'=4,'z'=8] {'z'}, dimensions={0} | all-to-all | bytes 262144 | tf_op jit(solution)/shard_map/all_to_all | solution.py:87
  100.0 15.5 %all_to_all.108 = bf16[32,32,256]{2,1,0:T(8,128)(2,1)S(1)} all-to-all(bf16[32,32,256]{2,1,0:T(8,128)(2,1)S(1)} %bitcast.122), channel_id=1, replica_groups=mesh['x'=4,'core'=2,'y'=4,'z'=8] {'y','z'}, dimensions={0} | all-to-all | bytes 1048576 | tf_op jit(solution)/shard_map/all_to_all | solution.py:83
  115.6 13.6 %all_to_all.109 = bf16[8,32,256]{2,1,0:T(8,128)(2,1)} all-to-all(bf16[8,32,256]{2,1,0:T(8,128)(2,1)S(1)} %broadcast_in_dim.16), channel_id=1, replica_groups=mesh['x'=4,'core'=2,'y'=4,'z'=8] {'x','core'}, dimensions={0} | all-to-all | bytes 262144 | tf_op jit(solution)/shard_map/all_to_all | solution.py:86
  134.7 6.5 %all-to-all-done.8 = bf16[8,32,256]{2,1,0:T(8,128)(2,1)S(1)} async-done(((bf16[8,32,256]{2,1,0:T(8,128)(2,1)}), bf16[8,32,256]{2,1,0:T(8,128)(2,1)S(1)}, u32[]{:S(2)}, u32[]{:S(2)}) %all-to-all-start.8) | async-done | bytes 131104 | tf_op jit(solution)/shard_map/all_to_all | solution.py:87
  142.5 15.5 %all_to_all.110 = bf16[32,32,256]{2,1,0:T(8,128)(2,1)S(1)} all-to-all(bf16[32,32,256]{2,1,0:T(8,128)(2,1)S(1)} %bitcast.101), channel_id=1, replica_groups=mesh['x'=4,'core'=2,'y'=4,'z'=8] {'y','z'}, dimensions={0} | all-to-all | bytes 1048576 | tf_op jit(solution)/shard_map/all_to_all | solution.py:83
  158.2 13.3 %all_to_all.111 = bf16[8,32,256]{2,1,0:T(8,128)(2,1)S(1)} all-to-all(bf16[8,32,256]{2,1,0:T(8,128)(2,1)S(1)} %broadcast_in_dim.17), channel_id=1, replica_groups=mesh['x'=4,'core'=2,'y'=4,'z'=8] {'x','core'}, dimensions={0} | all-to-all | bytes 262144 | tf_op jit(solution)/shard_map/all_to_all | solution.py:86
  171.5 11.4 %all_to_all.112 = bf16[8,32,256]{2,1,0:T(8,128)(2,1)S(1)} all-to-all(bf16[8,32,256]{2,1,0:T(8,128)(2,1)S(1)} %all_to_all.111), channel_id=1, replica_groups=mesh['x'=4,'core'=2,'y'=4,'z'=8] {'z'}, dimensions={0} | all-to-all | bytes 262144 | tf_op jit(solution)/shard_map/all_to_all | solution.py:87
  184.2 15.5 %all_to_all.113 = bf16[32,32,256]{2,1,0:T(8,128)(2,1)S(1)} all-to-all(bf16[32,32,256]{2,1,0:T(8,128)(2,1)S(1)} %bitcast.123), channel_id=1, replica_groups=mesh['x'=4,'core'=2,'y'=4,'z'=8] {'y','z'}, dimensions={0} | all-to-all | bytes 1048576 | tf_op jit(solution)/shard_map/all_to_all | solution.py:83
  200.5 9.1 %all-to-all-start.13 = ((bf16[8,32,256]{2,1,0:T(8,128)(2,1)}), bf16[8,32,256]{2,1,0:T(8,128)(2,1)}, u32[]{:S(2)}, u32[]{:S(2)}) async-start(bf16[8,32,256]{2,1,0:T(8,128)(2,1)} %broadcast_in_dim.18), calls=%async_computation.13 | async-start | bytes 262144 | tf_op jit(solution)/shard_map/all_to_all | solution.py:86
  220.5 6.5 %all-to-all-done.14 = bf16[8,32,256]{2,1,0:T(8,128)(2,1)S(1)} async-done(((bf16[8,32,256]{2,1,0:T(8,128)(2,1)}), bf16[8,32,256]{2,1,0:T(8,128)(2,1)S(1)}, u32[]{:S(2)}, u32[]{:S(2)}) %all-to-all-start.14) | async-done | bytes 131104 | tf_op jit(solution)/shard_map/all_to_all | solution.py:87
  228.4 15.5 %all_to_all.114 = bf16[32,32,256]{2,1,0:T(8,128)(2,1)S(1)} all-to-all(bf16[32,32,256]{2,1,0:T(8,128)(2,1)S(1)} %bitcast.102), channel_id=1, replica_groups=mesh['x'=4,'core'=2,'y'=4,'z'=8] {'y','z'}, dimensions={0} | all-to-all | bytes 1048576 | tf_op jit(solution)/shard_map/all_to_all | solution.py:83
  244.0 13.3 %all_to_all.115 = bf16[8,32,256]{2,1,0:T(8,128)(2,1)S(1)} all-to-all(bf16[8,32,256]{2,1,0:T(8,128)(2,1)S(1)} %broadcast_in_dim.19), channel_id=1, replica_groups=mesh['x'=4,'core'=2,'y'=4,'z'=8] {'x','core'}, dimensions={0} | all-to-all | bytes 262144 | tf_op jit(solution)/shard_map/all_to_all | solution.py:86
  257.3 11.4 %all_to_all.116 = bf16[8,32,256]{2,1,0:T(8,128)(2,1)S(1)} all-to-all(bf16[8,32,256]{2,1,0:T(8,128)(2,1)S(1)} %all_to_all.115), channel_id=1, replica_groups=mesh['x'=4,'core'=2,'y'=4,'z'=8] {'z'}, dimensions={0} | all-to-all | bytes 262144 | tf_op jit(solution)/shard_map/all_to_all | solution.py:87
  270.1 15.5 %all_to_all.117 = bf16[32,32,256]{2,1,0:T(8,128)(2,1)S(1)} all-to-all(bf16[32,32,256]{2,1,0:T(8,128)(2,1)S(1)} %bitcast.124), channel_id=1, replica_groups=mesh['x'=4,'core'=2,'y'=4,'z'=8] {'y','z'}, dimensions={0} | all-to-all | bytes 1048576 | tf_op jit(solution)/shard_map/all_to_all | solution.py:83
  285.7 13.3 %all_to_all.118 = bf16[8,32,256]{2,1,0:T(8,128)(2,1)S(1)} all-to-all(bf16[8,32,256]{2,1,0:T(8,128)(2,1)S(1)} %broadcast_in_dim.20), channel_id=1, replica_groups=mesh['x'=4,'core'=2,'y'=4,'z'=8] {'x','core'}, dimensions={0} | all-to-all | bytes 262144 | tf_op jit(solution)/shard_map/all_to_all | solution.py:86
  299.0 11.4 %all_to_all.119 = bf16[8,32,256]{2,1,0:T(8,128)(2,1)S(1)} all-to-all(bf16[8,32,256]{2,1,0:T(8,128)(2,1)S(1)} %all_to_all.118), channel_id=1, replica_groups=mesh['x'=4,'core'=2,'y'=4,'z'=8] {'z'}, dimensions={0} | all-to-all | bytes 262144 | tf_op jit(solution)/shard_map/all_to_all | solution.py:87
  (45 shorter events, 33.0 us)
Async XLA Ops:
  2.4 180.5 %copy-start = (bf16[4,1,256,256]{3,2,1,0:T(8,128)(2,1)S(1)}, bf16[4,1,256,256]{3,2,1,0:T(8,128)(2,1)}, u32[]{:S(2)}) copy-start(bf16[4,1,256,256]{3,2,1,0:T(8,128)(2,1)} %param.6) | copy-start | bytes 1572868
  4.6 26.4 %all-to-all-start = ((bf16[32,32,256]{2,1,0:T(8,128)(2,1)}), bf16[32,32,256]{2,1,0:T(8,128)(2,1)S(1)}, u32[]{:S(2)}, u32[]{:S(2)}) async-start(bf16[32,32,256]{2,1,0:T(8,128)(2,1)} %bitcast.6), calls=%async_computation | async-start | bytes 1048576 | tf_op jit(solution)/shard_map/all_to_all | solution.py:83
  31.7 13.2 %all-to-all-start.1 = ((bf16[8,32,256]{2,1,0:T(8,128)(2,1)}), bf16[8,32,256]{2,1,0:T(8,128)(2,1)}, u32[]{:S(2)}, u32[]{:S(2)}) async-start(bf16[8,32,256]{2,1,0:T(8,128)(2,1)} %broadcast_in_dim.14), calls=%async_computation.1 | async-start | bytes 262144 | tf_op jit(solution)/shard_map/all_to_all | solution.py:86
  44.9 12.0 %all-to-all-start.2 = ((bf16[8,32,256]{2,1,0:T(8,128)(2,1)}), bf16[8,32,256]{2,1,0:T(8,128)(2,1)S(1)}, u32[]{:S(2)}, u32[]{:S(2)}) async-start(bf16[8,32,256]{2,1,0:T(8,128)(2,1)} %all-to-all-done.1), calls=%async_computation.2 | async-start | bytes 262144 | tf_op jit(solution)/shard_map/all_to_all | solution.py:87
  129.2 12.0 %all-to-all-start.8 = ((bf16[8,32,256]{2,1,0:T(8,128)(2,1)}), bf16[8,32,256]{2,1,0:T(8,128)(2,1)S(1)}, u32[]{:S(2)}, u32[]{:S(2)}) async-start(bf16[8,32,256]{2,1,0:T(8,128)(2,1)} %all_to_all.109), calls=%async_computation.8 | async-start | bytes 262144 | tf_op jit(solution)/shard_map/all_to_all | solution.py:87
  200.5 14.5 %all-to-all-start.13 = ((bf16[8,32,256]{2,1,0:T(8,128)(2,1)}), bf16[8,32,256]{2,1,0:T(8,128)(2,1)}, u32[]{:S(2)}, u32[]{:S(2)}) async-start(bf16[8,32,256]{2,1,0:T(8,128)(2,1)} %broadcast_in_dim.18), calls=%async_computation.13 | async-start | bytes 262144 | tf_op jit(solution)/shard_map/all_to_all | solution.py:86
  215.0 12.0 %all-to-all-start.14 = ((bf16[8,32,256]{2,1,0:T(8,128)(2,1)}), bf16[8,32,256]{2,1,0:T(8,128)(2,1)S(1)}, u32[]{:S(2)}, u32[]{:S(2)}) async-start(bf16[8,32,256]{2,1,0:T(8,128)(2,1)} %all-to-all-done.13), calls=%async_computation.14 | async-start | bytes 262144 | tf_op jit(solution)/shard_map/all_to_all | solution.py:87

commit v10 on v9

--- a/solution.py
+++ b/solution.py
@@ -65,7 +65,6 @@
     block_node = node_table(node_blocks, total_blocks)
     row_ids = jnp.arange(rows_local, dtype=jnp.int32) * prow_count + prow_index
     col_ids = jnp.arange(cols_local, dtype=jnp.int32) * pcol_count + pcol_index
-    row_nodes = lookup(block_node, row_ids)
     col_nodes = lookup(block_node, col_ids)
     node_ids = jnp.arange(node_blocks.shape[0], dtype=jnp.int32)
     pick_node = (col_nodes[:, None] == node_ids[None, :]).astype(jnp.int32)
@@ -73,9 +72,14 @@
     block_all = jnp.arange(total_blocks, dtype=jnp.int32)
     pick_row = (row_ids[:, None] == block_all[None, :]).astype(jnp.int32)
     front_bits = jnp.sum(pick_row[:, None, :] * front_rows[None, :, :], axis=2)
-    diag_bits = (
-        (row_nodes[:, None] == col_nodes[None, :]) & (row_ids[:, None] >= col_ids[None, :])
-    ).astype(jnp.int32)
+    ordered_ids = jnp.array(node_order(), dtype=jnp.int32)
+    pick_sizes = (ordered_ids[:, None] == node_ids[None, :]).astype(jnp.int32)
+    block_ends = jnp.cumsum(jnp.sum(pick_sizes * node_blocks[None, :], axis=1))
+    row_pos = jnp.sum((row_ids[:, None] >= block_ends[None, :]).astype(jnp.int32), axis=1)
+    col_pos = jnp.sum((col_ids[:, None] >= block_ends[None, :]).astype(jnp.int32), axis=1)
+    diag_bits = ((row_pos[:, None] == col_pos[None, :]) & (row_ids[:, None] >= col_ids[None, :])).astype(
+        jnp.int32
+    )
 
     def reduce_route(level_terms):
         rhs_width = level_terms.shape[2]
@@ -89,7 +93,7 @@
 
     rhs_width = columns_in.shape[2]
     partial_levels = [None] * LEVELS
-    solved_list = []
+    solution = jnp.zeros((LEVELS, block_size, rhs_width), columns_in.dtype)
     for section_now in range(LEVELS):
         first_row = section_now * level_rows
         after_row = first_row + level_rows
@@ -104,7 +108,7 @@
             rhs_column,
         )
         solved = reduce_route(diag_terms)
-        solved_list.append(solved)
+        solution = solution.at[section_now].set(solved)
         for later in range(section_now + 1, LEVELS):
             later_row = later * level_rows
             update_terms = panel_products(
@@ -116,7 +120,6 @@
                 partial_levels[later] = update_terms
             else:
                 partial_levels[later] = partial_levels[later] + update_terms
-    solution = jnp.stack(solved_list)
     return solution.reshape(cols_local, 1, block_size, columns_in.shape[2])
 
 

time: 313 us -> 314 us (level)
  blocking collectives: 206 us -> 181 us
  starting transfers between devices: 41.3 us -> 54.6 us
  waiting for transfers between devices: 43.5 us -> 55.7 us
    all_to_all x5 -> x4, blocking collectives: 66.6 us -> 53.3 us  [reduce_route(): gathered = lax.all_to_all(spread, PROW, 0, 0, tiled=True)]
    all_to_all x4 -> x3, blocking collectives: 45.7 us -> 34.2 us  [reduce_route(): arrived = lax.all_to_all(gathered, RING, 0, 0, tiled=True)]
    all_to_all x2 -> x3, starting transfers between devices: 16.9 us -> 26.1 us  [reduce_route(): gathered = lax.all_to_all(spread, PROW, 0, 0, tiled=True)]
    all_to_all x3 -> x4, waiting for transfers between devices: 20.6 us -> 28.5 us  [reduce_route(): arrived = lax.all_to_all(gathered, RING, 0, 0, tiled=True)]
    all_to_all x2 -> x3, waiting for transfers between devices: 8.64 us -> 14 us  [reduce_route(): gathered = lax.all_to_all(spread, PROW, 0, 0, tiled=True)]
    all_to_all x3 -> x4, starting transfers between devices: 12.4 us -> 16.5 us  [reduce_route(): arrived = lax.all_to_all(gathered, RING, 0, 0, tiled=True)]
  transfers between devices with their start and end apart: 6 -> 8, of which waited for: 6 -> 8; matrix products, arithmetic and copies ran while one was open for 2% -> 2% of each run, Pallas kernels for 0% -> 0%
where the time goes in v10:
time: 314 us; the launch traced here: 313 us
  blocking collectives  181 us (58%)
  waiting for transfers between devices  55.7 us (18%)
  starting transfers between devices  54.6 us (17%)
  matrix products  14.4 us (5%)
  other arithmetic  4.28 us (1%)
    all_to_all x6, blocking collectives, reduce_route(): got = lax.all_to_all(pieces, PCOL, 0, 0, tiled=True)  93.3 us
    all_to_all x4, blocking collectives, reduce_route(): gathered = lax.all_to_all(spread, PROW, 0, 0, tiled=True)  53.3 us
    all_to_all x3, blocking collectives, reduce_route(): arrived = lax.all_to_all(gathered, RING, 0, 0, tiled=True)  34.2 us
    all_to_all x4, waiting for transfers between devices, reduce_route(): arrived = lax.all_to_all(gathered, RING, 0, 0, tiled=True)  28.5 us
    all_to_all x3, starting transfers between devices, reduce_route(): gathered = lax.all_to_all(spread, PROW, 0, 0, tiled=True)  26.1 us
    all_to_all x4, starting transfers between devices, reduce_route(): arrived = lax.all_to_all(gathered, RING, 0, 0, tiled=True)  16.5 us
    dot_general x10, matrix products, panel_products(): jnp.einsum('nxy,yw->nxw', tile_stack, vector, preferred_element_type=jnp....  14.4 us
    all_to_all x3, waiting for transfers between devices, reduce_route(): gathered = lax.all_to_all(spread, PROW, 0, 0, tiled=True)  14 us
  transfers between devices with their start and end apart: 8, of which 8 were waited for; matrix products, arithmetic and copies ran while one was open for 2% of the time, Pallas kernels for 0%

profile of v10, /device:TPU:1, one launch (start us, length us, event | category | flops | bytes accessed | tf_op | source)
XLA Modules:
  0.0 312.7 jit_solution(14156884249449369678)
XLA Ops:
  3.8 12.0 %all-to-all-start = ((bf16[32,32,256]{2,1,0:T(8,128)(2,1)}), bf16[32,32,256]{2,1,0:T(8,128)(2,1)S(1)}, u32[]{:S(2)}, u32[]{:S(2)}) async-start(bf16[32,32,256]{2,1,0:T(8,128)(2,1)} %bitcast.6), calls=%async_computation | async-start | bytes 1048576 | tf_op jit(solution)/shard_map/all_to_all | solution.py:87
  16.9 13.2 %all-to-all-done = bf16[32,32,256]{2,1,0:T(8,128)(2,1)S(1)} async-done(((bf16[32,32,256]{2,1,0:T(8,128)(2,1)}), bf16[32,32,256]{2,1,0:T(8,128)(2,1)S(1)}, u32[]{:S(2)}, u32[]{:S(2)}) %all-to-all-start) | async-done | bytes 524320 | tf_op jit(solution)/shard_map/all_to_all | solution.py:87
  30.9 7.8 %all-to-all-start.1 = ((bf16[8,32,256]{2,1,0:T(8,128)(2,1)}), bf16[8,32,256]{2,1,0:T(8,128)(2,1)}, u32[]{:S(2)}, u32[]{:S(2)}) async-start(bf16[8,32,256]{2,1,0:T(8,128)(2,1)} %broadcast_in_dim.14), calls=%async_computation.1 | async-start | bytes 262144 | tf_op jit(solution)/shard_map/all_to_all | solution.py:90
  39.5 4.6 %all-to-all-done.1 = bf16[8,32,256]{2,1,0:T(8,128)(2,1)} async-done(((bf16[8,32,256]{2,1,0:T(8,128)(2,1)}), bf16[8,32,256]{2,1,0:T(8,128)(2,1)}, u32[]{:S(2)}, u32[]{:S(2)}) %all-to-all-start.1) | async-done | bytes 131104 | tf_op jit(solution)/shard_map/all_to_all | solution.py:90
  48.4 7.6 %all-to-all-done.2 = bf16[8,32,256]{2,1,0:T(8,128)(2,1)S(1)} async-done(((bf16[8,32,256]{2,1,0:T(8,128)(2,1)}), bf16[8,32,256]{2,1,0:T(8,128)(2,1)S(1)}, u32[]{:S(2)}, u32[]{:S(2)}) %all-to-all-start.2) | async-done | bytes 131104 | tf_op jit(solution)/shard_map/all_to_all | solution.py:91
  57.4 15.5 %all_to_all.105 = bf16[32,32,256]{2,1,0:T(8,128)(2,1)S(1)} all-to-all(bf16[32,32,256]{2,1,0:T(8,128)(2,1)S(1)} %bitcast.125), channel_id=1, replica_groups=mesh['x'=4,'core'=2,'y'=4,'z'=8] {'y','z'}, dimensions={0} | all-to-all | bytes 1048576 | tf_op jit(solution)/shard_map/all_to_all | solution.py:87
  73.1 13.2 %all_to_all.106 = bf16[8,32,256]{2,1,0:T(8,128)(2,1)S(1)} all-to-all(bf16[8,32,256]{2,1,0:T(8,128)(2,1)S(1)} %broadcast_in_dim.15), channel_id=1, replica_groups=mesh['x'=4,'core'=2,'y'=4,'z'=8] {'x','core'}, dimensions={0} | all-to-all | bytes 262144 | tf_op jit(solution)/shard_map/all_to_all | solution.py:90
  86.3 11.4 %all_to_all.107 = bf16[8,32,256]{2,1,0:T(8,128)(2,1)S(1)} all-to-all(bf16[8,32,256]{2,1,0:T(8,128)(2,1)S(1)} %all_to_all.106), channel_id=1, replica_groups=mesh['x'=4,'core'=2,'y'=4,'z'=8] {'z'}, dimensions={0} | all-to-all | bytes 262144 | tf_op jit(solution)/shard_map/all_to_all | solution.py:91
  99.2 15.5 %all_to_all.108 = bf16[32,32,256]{2,1,0:T(8,128)(2,1)S(1)} all-to-all(bf16[32,32,256]{2,1,0:T(8,128)(2,1)S(1)} %bitcast.122), channel_id=1, replica_groups=mesh['x'=4,'core'=2,'y'=4,'z'=8] {'y','z'}, dimensions={0} | all-to-all | bytes 1048576 | tf_op jit(solution)/shard_map/all_to_all | solution.py:87
  114.8 13.6 %all_to_all.109 = bf16[8,32,256]{2,1,0:T(8,128)(2,1)} all-to-all(bf16[8,32,256]{2,1,0:T(8,128)(2,1)S(1)} %broadcast_in_dim.16), channel_id=1, replica_groups=mesh['x'=4,'core'=2,'y'=4,'z'=8] {'x','core'}, dimensions={0} | all-to-all | bytes 262144 | tf_op jit(solution)/shard_map/all_to_all | solution.py:90
  133.9 6.5 %all-to-all-done.8 = bf16[8,32,256]{2,1,0:T(8,128)(2,1)S(1)} async-done(((bf16[8,32,256]{2,1,0:T(8,128)(2,1)}), bf16[8,32,256]{2,1,0:T(8,128)(2,1)S(1)}, u32[]{:S(2)}, u32[]{:S(2)}) %all-to-all-start.8) | async-done | bytes 131104 | tf_op jit(solution)/shard_map/all_to_all | solution.py:91
  141.7 15.5 %all_to_all.110 = bf16[32,32,256]{2,1,0:T(8,128)(2,1)S(1)} all-to-all(bf16[32,32,256]{2,1,0:T(8,128)(2,1)S(1)} %bitcast.105), channel_id=1, replica_groups=mesh['x'=4,'core'=2,'y'=4,'z'=8] {'y','z'}, dimensions={0} | all-to-all | bytes 1048576 | tf_op jit(solution)/shard_map/all_to_all | solution.py:87
  157.4 13.3 %all_to_all.111 = bf16[8,32,256]{2,1,0:T(8,128)(2,1)S(1)} all-to-all(bf16[8,32,256]{2,1,0:T(8,128)(2,1)S(1)} %broadcast_in_dim.17), channel_id=1, replica_groups=mesh['x'=4,'core'=2,'y'=4,'z'=8] {'x','core'}, dimensions={0} | all-to-all | bytes 262144 | tf_op jit(solution)/shard_map/all_to_all | solution.py:90
  170.6 11.4 %all_to_all.112 = bf16[8,32,256]{2,1,0:T(8,128)(2,1)S(1)} all-to-all(bf16[8,32,256]{2,1,0:T(8,128)(2,1)S(1)} %all_to_all.111), channel_id=1, replica_groups=mesh['x'=4,'core'=2,'y'=4,'z'=8] {'z'}, dimensions={0} | all-to-all | bytes 262144 | tf_op jit(solution)/shard_map/all_to_all | solution.py:91
  183.4 15.5 %all_to_all.113 = bf16[32,32,256]{2,1,0:T(8,128)(2,1)S(1)} all-to-all(bf16[32,32,256]{2,1,0:T(8,128)(2,1)S(1)} %bitcast.123), channel_id=1, replica_groups=mesh['x'=4,'core'=2,'y'=4,'z'=8] {'y','z'}, dimensions={0} | all-to-all | bytes 1048576 | tf_op jit(solution)/shard_map/all_to_all | solution.py:87
  199.7 9.1 %all-to-all-start.13 = ((bf16[8,32,256]{2,1,0:T(8,128)(2,1)}), bf16[8,32,256]{2,1,0:T(8,128)(2,1)}, u32[]{:S(2)}, u32[]{:S(2)}) async-start(bf16[8,32,256]{2,1,0:T(8,128)(2,1)} %broadcast_in_dim.18), calls=%async_computation.13 | async-start | bytes 262144 | tf_op jit(solution)/shard_map/all_to_all | solution.py:90
  219.7 6.5 %all-to-all-done.14 = bf16[8,32,256]{2,1,0:T(8,128)(2,1)S(1)} async-done(((bf16[8,32,256]{2,1,0:T(8,128)(2,1)}), bf16[8,32,256]{2,1,0:T(8,128)(2,1)S(1)}, u32[]{:S(2)}, u32[]{:S(2)}) %all-to-all-start.14) | async-done | bytes 131104 | tf_op jit(solution)/shard_map/all_to_all | solution.py:91
  227.6 15.5 %all_to_all.114 = bf16[32,32,256]{2,1,0:T(8,128)(2,1)S(1)} all-to-all(bf16[32,32,256]{2,1,0:T(8,128)(2,1)S(1)} %bitcast.106), channel_id=1, replica_groups=mesh['x'=4,'core'=2,'y'=4,'z'=8] {'y','z'}, dimensions={0} | all-to-all | bytes 1048576 | tf_op jit(solution)/shard_map/all_to_all | solution.py:87
  243.2 13.3 %all_to_all.115 = bf16[8,32,256]{2,1,0:T(8,128)(2,1)S(1)} all-to-all(bf16[8,32,256]{2,1,0:T(8,128)(2,1)S(1)} %broadcast_in_dim.19), channel_id=1, replica_groups=mesh['x'=4,'core'=2,'y'=4,'z'=8] {'x','core'}, dimensions={0} | all-to-all | bytes 262144 | tf_op jit(solution)/shard_map/all_to_all | solution.py:90
  256.5 11.4 %all_to_all.116 = bf16[8,32,256]{2,1,0:T(8,128)(2,1)S(1)} all-to-all(bf16[8,32,256]{2,1,0:T(8,128)(2,1)S(1)} %all_to_all.115), channel_id=1, replica_groups=mesh['x'=4,'core'=2,'y'=4,'z'=8] {'z'}, dimensions={0} | all-to-all | bytes 262144 | tf_op jit(solution)/shard_map/all_to_all | solution.py:91
  269.2 15.5 %all_to_all.117 = bf16[32,32,256]{2,1,0:T(8,128)(2,1)S(1)} all-to-all(bf16[32,32,256]{2,1,0:T(8,128)(2,1)S(1)} %bitcast.124), channel_id=1, replica_groups=mesh['x'=4,'core'=2,'y'=4,'z'=8] {'y','z'}, dimensions={0} | all-to-all | bytes 1048576 | tf_op jit(solution)/shard_map/all_to_all | solution.py:87
  285.5 9.1 %all-to-all-start.19 = ((bf16[8,32,256]{2,1,0:T(8,128)(2,1)}), bf16[8,32,256]{2,1,0:T(8,128)(2,1)}, u32[]{:S(2)}, u32[]{:S(2)}) async-start(bf16[8,32,256]{2,1,0:T(8,128)(2,1)} %broadcast_in_dim.20), calls=%async_computation.19 | async-start | bytes 262144 | tf_op jit(solution)/shard_map/all_to_all | solution.py:90
  294.7 5.4 %all-to-all-done.19 = bf16[8,32,256]{2,1,0:T(8,128)(2,1)} async-done(((bf16[8,32,256]{2,1,0:T(8,128)(2,1)}), bf16[8,32,256]{2,1,0:T(8,128)(2,1)}, u32[]{:S(2)}, u32[]{:S(2)}) %all-to-all-start.19) | async-done | bytes 131104 | tf_op jit(solution)/shard_map/all_to_all | solution.py:90
  304.2 7.8 %all-to-all-done.20 = bf16[8,32,256]{2,1,0:T(8,128)(2,1)S(1)} async-done(((bf16[8,32,256]{2,1,0:T(8,128)(2,1)}), bf16[8,32,256]{2,1,0:T(8,128)(2,1)S(1)}, u32[]{:S(2)}, u32[]{:S(2)}) %all-to-all-start.20) | async-done | bytes 131104 | tf_op jit(solution)/shard_map/all_to_all | solution.py:91
  (53 shorter events, 42.0 us)
Async XLA Ops:
  1.6 180.5 %copy-start.1 = (bf16[4,1,256,256]{3,2,1,0:T(8,128)(2,1)S(1)}, bf16[4,1,256,256]{3,2,1,0:T(8,128)(2,1)}, u32[]{:S(2)}) copy-start(bf16[4,1,256,256]{3,2,1,0:T(8,128)(2,1)} %param.15) | copy-start | bytes 1572868
  3.8 26.3 %all-to-all-start = ((bf16[32,32,256]{2,1,0:T(8,128)(2,1)}), bf16[32,32,256]{2,1,0:T(8,128)(2,1)S(1)}, u32[]{:S(2)}, u32[]{:S(2)}) async-start(bf16[32,32,256]{2,1,0:T(8,128)(2,1)} %bitcast.6), calls=%async_computation | async-start | bytes 1048576 | tf_op jit(solution)/shard_map/all_to_all | solution.py:87
  30.9 13.2 %all-to-all-start.1 = ((bf16[8,32,256]{2,1,0:T(8,128)(2,1)}), bf16[8,32,256]{2,1,0:T(8,128)(2,1)}, u32[]{:S(2)}, u32[]{:S(2)}) async-start(bf16[8,32,256]{2,1,0:T(8,128)(2,1)} %broadcast_in_dim.14), calls=%async_computation.1 | async-start | bytes 262144 | tf_op jit(solution)/shard_map/all_to_all | solution.py:90
  44.1 12.0 %all-to-all-start.2 = ((bf16[8,32,256]{2,1,0:T(8,128)(2,1)}), bf16[8,32,256]{2,1,0:T(8,128)(2,1)S(1)}, u32[]{:S(2)}, u32[]{:S(2)}) async-start(bf16[8,32,256]{2,1,0:T(8,128)(2,1)} %all-to-all-done.1), calls=%async_computation.2 | async-start | bytes 262144 | tf_op jit(solution)/shard_map/all_to_all | solution.py:91
  128.4 12.0 %all-to-all-start.8 = ((bf16[8,32,256]{2,1,0:T(8,128)(2,1)}), bf16[8,32,256]{2,1,0:T(8,128)(2,1)S(1)}, u32[]{:S(2)}, u32[]{:S(2)}) async-start(bf16[8,32,256]{2,1,0:T(8,128)(2,1)} %all_to_all.109), calls=%async_computation.8 | async-start | bytes 262144 | tf_op jit(solution)/shard_map/all_to_all | solution.py:91
  199.7 14.5 %all-to-all-start.13 = ((bf16[8,32,256]{2,1,0:T(8,128)(2,1)}), bf16[8,32,256]{2,1,0:T(8,128)(2,1)}, u32[]{:S(2)}, u32[]{:S(2)}) async-start(bf16[8,32,256]{2,1,0:T(8,128)(2,1)} %broadcast_in_dim.18), calls=%async_computation.13 | async-start | bytes 262144 | tf_op jit(solution)/shard_map/all_to_all | solution.py:90
  214.2 12.0 %all-to-all-start.14 = ((bf16[8,32,256]{2,1,0:T(8,128)(2,1)}), bf16[8,32,256]{2,1,0:T(8,128)(2,1)S(1)}, u32[]{:S(2)}, u32[]{:S(2)}) async-start(bf16[8,32,256]{2,1,0:T(8,128)(2,1)} %all-to-all-done.13), calls=%async_computation.14 | async-start | bytes 262144 | tf_op jit(solution)/shard_map/all_to_all | solution.py:91
  285.5 14.5 %all-to-all-start.19 = ((bf16[8,32,256]{2,1,0:T(8,128)(2,1)}), bf16[8,32,256]{2,1,0:T(8,128)(2,1)}, u32[]{:S(2)}, u32[]{:S(2)}) async-start(bf16[8,32,256]{2,1,0:T(8,128)(2,1)} %broadcast_in_dim.20), calls=%async_computation.19 | async-start | bytes 262144 | tf_op jit(solution)/shard_map/all_to_all | solution.py:90
  300.1 12.0 %all-to-all-start.20 = ((bf16[8,32,256]{2,1,0:T(8,128)(2,1)}), bf16[8,32,256]{2,1,0:T(8,128)(2,1)S(1)}, u32[]{:S(2)}, u32[]{:S(2)}) async-start(bf16[8,32,256]{2,1,0:T(8,128)(2,1)} %all-to-all-done.19), calls=%async_computation.20 | async-start | bytes 262144 | tf_op jit(solution)/shard_map/all_to_all | solution.py:91
  304.2 7.8 %copy-start = (bf16[4,1,256,256]{3,2,1,0:T(8,128)(2,1)}, bf16[4,1,256,256]{3,2,1,0:T(8,128)(2,1)S(1)}, u32[]{:S(2)}) copy-start(bf16[4,1,256,256]{3,2,1,0:T(8,128)(2,1)S(1)} %constant_dynamic-update-slice_fusion.1) | copy-start | bytes 1572868

commit v11 on v9

--- a/solution.py
+++ b/solution.py
@@ -79,8 +79,9 @@
 
     def reduce_route(level_terms):
         rhs_width = level_terms.shape[2]
-        pieces = level_terms.astype(jnp.bfloat16).reshape(pcol_count, chunk_rows, rhs_width)
-        got = lax.all_to_all(pieces, PCOL, 0, 0, tiled=True)
+        pieces = level_terms.astype(jnp.bfloat16).reshape(level_rows, ring, chunk_rows, rhs_width)
+        pieces = jnp.transpose(pieces, (1, 0, 2, 3)).reshape(pcol_count, chunk_rows, rhs_width)
+        got = lax.all_to_all(pieces, PCOL[::-1], 0, 0, tiled=True)
         summed = jnp.sum(got.astype(jnp.float32), axis=0).astype(jnp.bfloat16)
         spread = jnp.broadcast_to(summed[None], (prow_count,) + summed.shape)
         gathered = lax.all_to_all(spread, PROW, 0, 0, tiled=True)

time: 313 us -> 319 us (1.019)
  blocking collectives: 206 us -> 214 us
  starting transfers between devices: 41.3 us -> 36.3 us
    all_to_all x6, blocking collectives: 93.3 us -> 115 us  [reduce_route(): got = lax.all_to_all(pieces, PCOL[::-1], 0, 0, tiled=True)]
    all_to_all x5, blocking collectives: 66.6 us -> 57.2 us  [reduce_route(): gathered = lax.all_to_all(spread, PROW, 0, 0, tiled=True)]
    all_to_all x4, blocking collectives: 45.7 us -> 41.9 us  [reduce_route(): arrived = lax.all_to_all(gathered, RING, 0, 0, tiled=True)]
where the time goes in v11:
time: 319 us; the launch traced here: 317 us
  blocking collectives  214 us (67%)
  waiting for transfers between devices  44.9 us (14%)
  starting transfers between devices  36.3 us (11%)
  matrix products  13.5 us (4%)
  other arithmetic  5.02 us (2%)
    all_to_all x6, blocking collectives, reduce_route(): got = lax.all_to_all(pieces, PCOL[::-1], 0, 0, tiled=True)  115 us
    all_to_all x5, blocking collectives, reduce_route(): gathered = lax.all_to_all(spread, PROW, 0, 0, tiled=True)  57.2 us
    all_to_all x4, blocking collectives, reduce_route(): arrived = lax.all_to_all(gathered, RING, 0, 0, tiled=True)  41.9 us
    all_to_all x3, waiting for transfers between devices, reduce_route(): arrived = lax.all_to_all(gathered, RING, 0, 0, tiled=True)  20.1 us
    all_to_all x1, waiting for transfers between devices, reduce_route(): got = lax.all_to_all(pieces, PCOL[::-1], 0, 0, tiled=True)  16.2 us
    all_to_all x2, starting transfers between devices, reduce_route(): gathered = lax.all_to_all(spread, PROW, 0, 0, tiled=True)  14.2 us
    dot_general x10, matrix products, panel_products(): jnp.einsum('nxy,yw->nxw', tile_stack, vector, preferred_element_type=jnp....  13.5 us
    all_to_all x1, starting transfers between devices, reduce_route(): got = lax.all_to_all(pieces, PCOL[::-1], 0, 0, tiled=True)  12 us
  transfers between devices with their start and end apart: 6, of which 6 were waited for; matrix products, arithmetic and copies ran while one was open for 2% of the time, Pallas kernels for 0%

profile of v11, /device:TPU:1, one launch (start us, length us, event | category | flops | bytes accessed | tf_op | source)
XLA Modules:
  0.0 316.9 jit_solution(684277122608370385)
XLA Ops:
  4.7 12.0 %all-to-all-start = ((bf16[32,32,256]{2,1,0:T(8,128)(2,1)}), bf16[32,32,256]{2,1,0:T(8,128)(2,1)S(1)}, u32[]{:S(2)}, u32[]{:S(2)}) async-start(bf16[32,32,256]{2,1,0:T(8,128)(2,1)} %bitcast.8), calls=%async_computation | async-start | bytes 1048576 | tf_op jit(solution)/shard_map/all_to_all | solution.py:84
  16.8 16.2 %all-to-all-done = bf16[32,32,256]{2,1,0:T(8,128)(2,1)S(1)} async-done(((bf16[32,32,256]{2,1,0:T(8,128)(2,1)}), bf16[32,32,256]{2,1,0:T(8,128)(2,1)S(1)}, u32[]{:S(2)}, u32[]{:S(2)}) %all-to-all-start) | async-done | bytes 524320 | tf_op jit(solution)/shard_map/all_to_all | solution.py:84
  33.7 6.7 %all-to-all-start.1 = ((bf16[8,32,256]{2,1,0:T(8,128)(2,1)}), bf16[8,32,256]{2,1,0:T(8,128)(2,1)}, u32[]{:S(2)}, u32[]{:S(2)}) async-start(bf16[8,32,256]{2,1,0:T(8,128)(2,1)} %broadcast_in_dim.14), calls=%async_computation.1 | async-start | bytes 262144 | tf_op jit(solution)/shard_map/all_to_all | solution.py:87
  41.2 4.6 %all-to-all-done.1 = bf16[8,32,256]{2,1,0:T(8,128)(2,1)} async-done(((bf16[8,32,256]{2,1,0:T(8,128)(2,1)}), bf16[8,32,256]{2,1,0:T(8,128)(2,1)}, u32[]{:S(2)}, u32[]{:S(2)}) %all-to-all-start.1) | async-done | bytes 131104 | tf_op jit(solution)/shard_map/all_to_all | solution.py:87
  49.4 7.5 %all-to-all-done.2 = bf16[8,32,256]{2,1,0:T(8,128)(2,1)S(1)} async-done(((bf16[8,32,256]{2,1,0:T(8,128)(2,1)}), bf16[8,32,256]{2,1,0:T(8,128)(2,1)S(1)}, u32[]{:S(2)}, u32[]{:S(2)}) %all-to-all-start.2) | async-done | bytes 131104 | tf_op jit(solution)/shard_map/all_to_all | solution.py:88
  58.3 19.5 %all_to_all.105 = bf16[32,32,256]{2,1,0:T(8,128)(2,1)S(1)} all-to-all(bf16[32,32,256]{2,1,0:T(8,128)(2,1)S(1)} %bitcast.124), channel_id=1, replica_groups=mesh['x'=4,'core'=2,'y'=4,'z'=8] {'z','y'}, dimensions={0} | all-to-all | bytes 1048576 | tf_op jit(solution)/shard_map/all_to_all | solution.py:84
  77.8 11.3 %all_to_all.106 = bf16[8,32,256]{2,1,0:T(8,128)(2,1)S(1)} all-to-all(bf16[8,32,256]{2,1,0:T(8,128)(2,1)S(1)} %broadcast_in_dim.15), channel_id=1, replica_groups=mesh['x'=4,'core'=2,'y'=4,'z'=8] {'x','core'}, dimensions={0} | all-to-all | bytes 262144 | tf_op jit(solution)/shard_map/all_to_all | solution.py:87
  89.2 10.5 %all_to_all.107 = bf16[8,32,256]{2,1,0:T(8,128)(2,1)S(1)} all-to-all(bf16[8,32,256]{2,1,0:T(8,128)(2,1)S(1)} %all_to_all.106), channel_id=1, replica_groups=mesh['x'=4,'core'=2,'y'=4,'z'=8] {'z'}, dimensions={0} | all-to-all | bytes 262144 | tf_op jit(solution)/shard_map/all_to_all | solution.py:88
  101.1 19.1 %all_to_all.108 = bf16[32,32,256]{2,1,0:T(8,128)(2,1)S(1)} all-to-all(bf16[32,32,256]{2,1,0:T(8,128)(2,1)S(1)} %bitcast.125), channel_id=1, replica_groups=mesh['x'=4,'core'=2,'y'=4,'z'=8] {'z','y'}, dimensions={0} | all-to-all | bytes 1048576 | tf_op jit(solution)/shard_map/all_to_all | solution.py:84
  120.2 11.9 %all_to_all.109 = bf16[8,32,256]{2,1,0:T(8,128)(2,1)} all-to-all(bf16[8,32,256]{2,1,0:T(8,128)(2,1)S(1)} %broadcast_in_dim.16), channel_id=1, replica_groups=mesh['x'=4,'core'=2,'y'=4,'z'=8] {'x','core'}, dimensions={0} | all-to-all | bytes 262144 | tf_op jit(solution)/shard_map/all_to_all | solution.py:87
  136.9 6.3 %all-to-all-done.8 = bf16[8,32,256]{2,1,0:T(8,128)(2,1)S(1)} async-done(((bf16[8,32,256]{2,1,0:T(8,128)(2,1)}), bf16[8,32,256]{2,1,0:T(8,128)(2,1)S(1)}, u32[]{:S(2)}, u32[]{:S(2)}) %all-to-all-start.8) | async-done | bytes 131104 | tf_op jit(solution)/shard_map/all_to_all | solution.py:88
  144.6 19.3 %all_to_all.110 = bf16[32,32,256]{2,1,0:T(8,128)(2,1)S(1)} all-to-all(bf16[32,32,256]{2,1,0:T(8,128)(2,1)S(1)} %bitcast.126), channel_id=1, replica_groups=mesh['x'=4,'core'=2,'y'=4,'z'=8] {'z','y'}, dimensions={0} | all-to-all | bytes 1048576 | tf_op jit(solution)/shard_map/all_to_all | solution.py:84
  164.1 11.3 %all_to_all.111 = bf16[8,32,256]{2,1,0:T(8,128)(2,1)S(1)} all-to-all(bf16[8,32,256]{2,1,0:T(8,128)(2,1)S(1)} %broadcast_in_dim.17), channel_id=1, replica_groups=mesh['x'=4,'core'=2,'y'=4,'z'=8] {'x','core'}, dimensions={0} | all-to-all | bytes 262144 | tf_op jit(solution)/shard_map/all_to_all | solution.py:87
  175.4 10.5 %all_to_all.112 = bf16[8,32,256]{2,1,0:T(8,128)(2,1)S(1)} all-to-all(bf16[8,32,256]{2,1,0:T(8,128)(2,1)S(1)} %all_to_all.111), channel_id=1, replica_groups=mesh['x'=4,'core'=2,'y'=4,'z'=8] {'z'}, dimensions={0} | all-to-all | bytes 262144 | tf_op jit(solution)/shard_map/all_to_all | solution.py:88
  187.3 19.1 %all_to_all.113 = bf16[32,32,256]{2,1,0:T(8,128)(2,1)S(1)} all-to-all(bf16[32,32,256]{2,1,0:T(8,128)(2,1)S(1)} %bitcast.127), channel_id=1, replica_groups=mesh['x'=4,'core'=2,'y'=4,'z'=8] {'z','y'}, dimensions={0} | all-to-all | bytes 1048576 | tf_op jit(solution)/shard_map/all_to_all | solution.py:84
  207.1 7.5 %all-to-all-start.13 = ((bf16[8,32,256]{2,1,0:T(8,128)(2,1)}), bf16[8,32,256]{2,1,0:T(8,128)(2,1)}, u32[]{:S(2)}, u32[]{:S(2)}) async-start(bf16[8,32,256]{2,1,0:T(8,128)(2,1)} %broadcast_in_dim.18), calls=%async_computation.13 | async-start | bytes 262144 | tf_op jit(solution)/shard_map/all_to_all | solution.py:87
  216.0 4.1 %all-to-all-done.13 = bf16[8,32,256]{2,1,0:T(8,128)(2,1)} async-done(((bf16[8,32,256]{2,1,0:T(8,128)(2,1)}), bf16[8,32,256]{2,1,0:T(8,128)(2,1)}, u32[]{:S(2)}, u32[]{:S(2)}) %all-to-all-start.13) | async-done | bytes 131104 | tf_op jit(solution)/shard_map/all_to_all | solution.py:87
  224.7 6.3 %all-to-all-done.14 = bf16[8,32,256]{2,1,0:T(8,128)(2,1)S(1)} async-done(((bf16[8,32,256]{2,1,0:T(8,128)(2,1)}), bf16[8,32,256]{2,1,0:T(8,128)(2,1)S(1)}, u32[]{:S(2)}, u32[]{:S(2)}) %all-to-all-start.14) | async-done | bytes 131104 | tf_op jit(solution)/shard_map/all_to_all | solution.py:88
  232.5 19.3 %all_to_all.114 = bf16[32,32,256]{2,1,0:T(8,128)(2,1)S(1)} all-to-all(bf16[32,32,256]{2,1,0:T(8,128)(2,1)S(1)} %bitcast.128), channel_id=1, replica_groups=mesh['x'=4,'core'=2,'y'=4,'z'=8] {'z','y'}, dimensions={0} | all-to-all | bytes 1048576 | tf_op jit(solution)/shard_map/all_to_all | solution.py:84
  251.9 11.3 %all_to_all.115 = bf16[8,32,256]{2,1,0:T(8,128)(2,1)S(1)} all-to-all(bf16[8,32,256]{2,1,0:T(8,128)(2,1)S(1)} %broadcast_in_dim.19), channel_id=1, replica_groups=mesh['x'=4,'core'=2,'y'=4,'z'=8] {'x','core'}, dimensions={0} | all-to-all | bytes 262144 | tf_op jit(solution)/shard_map/all_to_all | solution.py:87
  263.2 10.5 %all_to_all.116 = bf16[8,32,256]{2,1,0:T(8,128)(2,1)S(1)} all-to-all(bf16[8,32,256]{2,1,0:T(8,128)(2,1)S(1)} %all_to_all.115), channel_id=1, replica_groups=mesh['x'=4,'core'=2,'y'=4,'z'=8] {'z'}, dimensions={0} | all-to-all | bytes 262144 | tf_op jit(solution)/shard_map/all_to_all | solution.py:88
  275.1 19.1 %all_to_all.117 = bf16[32,32,256]{2,1,0:T(8,128)(2,1)S(1)} all-to-all(bf16[32,32,256]{2,1,0:T(8,128)(2,1)S(1)} %bitcast.129), channel_id=1, replica_groups=mesh['x'=4,'core'=2,'y'=4,'z'=8] {'z','y'}, dimensions={0} | all-to-all | bytes 1048576 | tf_op jit(solution)/shard_map/all_to_all | solution.py:84
  294.3 11.3 %all_to_all.118 = bf16[8,32,256]{2,1,0:T(8,128)(2,1)S(1)} all-to-all(bf16[8,32,256]{2,1,0:T(8,128)(2,1)S(1)} %broadcast_in_dim.20), channel_id=1, replica_groups=mesh['x'=4,'core'=2,'y'=4,'z'=8] {'x','core'}, dimensions={0} | all-to-all | bytes 262144 | tf_op jit(solution)/shard_map/all_to_all | solution.py:87
  305.6 10.5 %all_to_all.119 = bf16[8,32,256]{2,1,0:T(8,128)(2,1)S(1)} all-to-all(bf16[8,32,256]{2,1,0:T(8,128)(2,1)S(1)} %all_to_all.118), channel_id=1, replica_groups=mesh['x'=4,'core'=2,'y'=4,'z'=8] {'z'}, dimensions={0} | all-to-all | bytes 262144 | tf_op jit(solution)/shard_map/all_to_all | solution.py:88
  (52 shorter events, 31.1 us)
Async XLA Ops:
  0.0 99.6 %copy-start = (bf16[4,1,256,256]{3,2,1,0:T(8,128)(2,1)S(1)}, bf16[4,1,256,256]{3,2,1,0:T(8,128)(2,1)}, u32[]{:S(2)}) copy-start(bf16[4,1,256,256]{3,2,1,0:T(8,128)(2,1)} %param.6) | copy-start | bytes 1572868
  4.7 28.3 %all-to-all-start = ((bf16[32,32,256]{2,1,0:T(8,128)(2,1)}), bf16[32,32,256]{2,1,0:T(8,128)(2,1)S(1)}, u32[]{:S(2)}, u32[]{:S(2)}) async-start(bf16[32,32,256]{2,1,0:T(8,128)(2,1)} %bitcast.8), calls=%async_computation | async-start | bytes 1048576 | tf_op jit(solution)/shard_map/all_to_all | solution.py:84
  33.7 12.1 %all-to-all-start.1 = ((bf16[8,32,256]{2,1,0:T(8,128)(2,1)}), bf16[8,32,256]{2,1,0:T(8,128)(2,1)}, u32[]{:S(2)}, u32[]{:S(2)}) async-start(bf16[8,32,256]{2,1,0:T(8,128)(2,1)} %broadcast_in_dim.14), calls=%async_computation.1 | async-start | bytes 262144 | tf_op jit(solution)/shard_map/all_to_all | solution.py:87
  45.8 11.1 %all-to-all-start.2 = ((bf16[8,32,256]{2,1,0:T(8,128)(2,1)}), bf16[8,32,256]{2,1,0:T(8,128)(2,1)S(1)}, u32[]{:S(2)}, u32[]{:S(2)}) async-start(bf16[8,32,256]{2,1,0:T(8,128)(2,1)} %all-to-all-done.1), calls=%async_computation.2 | async-start | bytes 262144 | tf_op jit(solution)/shard_map/all_to_all | solution.py:88
  132.2 11.1 %all-to-all-start.8 = ((bf16[8,32,256]{2,1,0:T(8,128)(2,1)}), bf16[8,32,256]{2,1,0:T(8,128)(2,1)S(1)}, u32[]{:S(2)}, u32[]{:S(2)}) async-start(bf16[8,32,256]{2,1,0:T(8,128)(2,1)} %all_to_all.109), calls=%async_computation.8 | async-start | bytes 262144 | tf_op jit(solution)/shard_map/all_to_all | solution.py:88
  207.1 12.9 %all-to-all-start.13 = ((bf16[8,32,256]{2,1,0:T(8,128)(2,1)}), bf16[8,32,256]{2,1,0:T(8,128)(2,1)}, u32[]{:S(2)}, u32[]{:S(2)}) async-start(bf16[8,32,256]{2,1,0:T(8,128)(2,1)} %broadcast_in_dim.18), calls=%async_computation.13 | async-start | bytes 262144 | tf_op jit(solution)/shard_map/all_to_all | solution.py:87
  220.0 11.1 %all-to-all-start.14 = ((bf16[8,32,256]{2,1,0:T(8,128)(2,1)}), bf16[8,32,256]{2,1,0:T(8,128)(2,1)S(1)}, u32[]{:S(2)}, u32[]{:S(2)}) async-start(bf16[8,32,256]{2,1,0:T(8,128)(2,1)} %all-to-all-done.13), calls=%async_computation.14 | async-start | bytes 262144 | tf_op jit(solution)/shard_map/all_to_all | solution.py:88

commit v12 on v9

--- a/solution.py
+++ b/solution.py
@@ -83,7 +83,11 @@
         got = lax.all_to_all(pieces, PCOL, 0, 0, tiled=True)
         summed = jnp.sum(got.astype(jnp.float32), axis=0).astype(jnp.bfloat16)
         spread = jnp.broadcast_to(summed[None], (prow_count,) + summed.shape)
-        gathered = lax.all_to_all(spread, PROW, 0, 0, tiled=True)
+        gathered = lax.all_to_all(spread, PROW[::-1], 0, 0, tiled=True)
+        core_count = lax.axis_size(PROW[1])
+        gathered = jnp.transpose(
+            gathered.reshape((core_count, prow_count // core_count) + summed.shape), (1, 0, 2, 3)
+        ).reshape((prow_count,) + summed.shape)
         arrived = lax.all_to_all(gathered, RING, 0, 0, tiled=True)
         return arrived.reshape(block_size, rhs_width)
 

time: 313 us -> 316 us (level)
    all_to_all x6, blocking collectives: 93.3 us -> 99.9 us  [reduce_route(): got = lax.all_to_all(pieces, PCOL, 0, 0, tiled=True)]
    all_to_all x5, blocking collectives: 66.6 us -> 62.7 us  [reduce_route(): gathered = lax.all_to_all(spread, PROW[::-1], 0, 0, tiled=True)]
where the time goes in v12:
time: 316 us; the launch traced here: 314 us
  blocking collectives  208 us (66%)
  waiting for transfers between devices  43 us (14%)
  starting transfers between devices  39.9 us (13%)
  matrix products  14.3 us (5%)
  other arithmetic  4.95 us (2%)
  local copies, waits for them, and re-layouts  3.43 us (1%)
    all_to_all x6, blocking collectives, reduce_route(): got = lax.all_to_all(pieces, PCOL, 0, 0, tiled=True)  99.9 us
    all_to_all x5, blocking collectives, reduce_route(): gathered = lax.all_to_all(spread, PROW[::-1], 0, 0, tiled=True)  62.7 us
    all_to_all x4, blocking collectives, reduce_route(): arrived = lax.all_to_all(gathered, RING, 0, 0, tiled=True)  45.5 us
    all_to_all x3, waiting for transfers between devices, reduce_route(): arrived = lax.all_to_all(gathered, RING, 0, 0, tiled=True)  20.6 us
    all_to_all x2, starting transfers between devices, reduce_route(): gathered = lax.all_to_all(spread, PROW[::-1], 0, 0, tiled=True)  16.1 us
    dot_general x10, matrix products, panel_products(): jnp.einsum('nxy,yw->nxw', tile_stack, vector, preferred_element_type=jnp....  14.3 us
    all_to_all x1, waiting for transfers between devices, reduce_route(): got = lax.all_to_all(pieces, PCOL, 0, 0, tiled=True)  14.2 us
    all_to_all x1, starting transfers between devices, reduce_route(): got = lax.all_to_all(pieces, PCOL, 0, 0, tiled=True)  12.2 us
  transfers between devices with their start and end apart: 6, of which 6 were waited for; matrix products, arithmetic and copies ran while one was open for 2% of the time, Pallas kernels for 0%

profile of v12, /device:TPU:1, one launch (start us, length us, event | category | flops | bytes accessed | tf_op | source)
XLA Modules:
  0.0 313.9 jit_solution(6431050172662675754)
XLA Ops:
  4.6 12.2 %all-to-all-start = ((bf16[32,32,256]{2,1,0:T(8,128)(2,1)}), bf16[32,32,256]{2,1,0:T(8,128)(2,1)S(1)}, u32[]{:S(2)}, u32[]{:S(2)}) async-start(bf16[32,32,256]{2,1,0:T(8,128)(2,1)} %bitcast.6), calls=%async_computation | async-start | bytes 1048576 | tf_op jit(solution)/shard_map/all_to_all | solution.py:83
  16.8 14.2 %all-to-all-done = bf16[32,32,256]{2,1,0:T(8,128)(2,1)S(1)} async-done(((bf16[32,32,256]{2,1,0:T(8,128)(2,1)}), bf16[32,32,256]{2,1,0:T(8,128)(2,1)S(1)}, u32[]{:S(2)}, u32[]{:S(2)}) %all-to-all-start) | async-done | bytes 524320 | tf_op jit(solution)/shard_map/all_to_all | solution.py:83
  31.8 7.8 %all-to-all-start.1 = ((bf16[8,32,256]{2,1,0:T(8,128)(2,1)}), bf16[8,32,256]{2,1,0:T(8,128)(2,1)S(1)}, u32[]{:S(2)}, u32[]{:S(2)}) async-start(bf16[8,32,256]{2,1,0:T(8,128)(2,1)} %broadcast_in_dim.14), calls=%async_computation.1 | async-start | bytes 262144 | tf_op jit(solution)/shard_map/all_to_all | solution.py:86
  40.4 4.4 %all-to-all-done.1 = bf16[8,32,256]{2,1,0:T(8,128)(2,1)S(1)} async-done(((bf16[8,32,256]{2,1,0:T(8,128)(2,1)}), bf16[8,32,256]{2,1,0:T(8,128)(2,1)S(1)}, u32[]{:S(2)}, u32[]{:S(2)}) %all-to-all-start.1) | async-done | bytes 131104 | tf_op jit(solution)/shard_map/all_to_all | solution.py:86
  45.4 4.1 %all-to-all-start.2 = ((bf16[8,32,256]{2,1,0:T(8,128)(2,1)}), bf16[8,32,256]{2,1,0:T(8,128)(2,1)S(1)}, u32[]{:S(2)}, u32[]{:S(2)}) async-start(bf16[8,32,256]{2,1,0:T(8,128)(2,1)} %bitcast.9), calls=%async_computation.2 | async-start | bytes 262144 | tf_op jit(solution)/shard_map/all_to_all | solution.py:91
  49.8 7.6 %all-to-all-done.2 = bf16[8,32,256]{2,1,0:T(8,128)(2,1)S(1)} async-done(((bf16[8,32,256]{2,1,0:T(8,128)(2,1)}), bf16[8,32,256]{2,1,0:T(8,128)(2,1)S(1)}, u32[]{:S(2)}, u32[]{:S(2)}) %all-to-all-start.2) | async-done | bytes 131104 | tf_op jit(solution)/shard_map/all_to_all | solution.py:91
  58.8 16.6 %all_to_all.105 = bf16[32,32,256]{2,1,0:T(8,128)(2,1)S(1)} all-to-all(bf16[32,32,256]{2,1,0:T(8,128)(2,1)S(1)} %bitcast.153), channel_id=1, replica_groups=mesh['x'=4,'core'=2,'y'=4,'z'=8] {'y','z'}, dimensions={0} | all-to-all | bytes 1048576 | tf_op jit(solution)/shard_map/all_to_all | solution.py:83
  75.5 12.6 %all_to_all.106 = bf16[8,32,256]{2,1,0:T(8,128)(2,1)S(1)} all-to-all(bf16[8,32,256]{2,1,0:T(8,128)(2,1)S(1)} %broadcast_in_dim.15), channel_id=1, replica_groups=mesh['x'=4,'core'=2,'y'=4,'z'=8] {'core','x'}, dimensions={0} | all-to-all | bytes 262144 | tf_op jit(solution)/shard_map/all_to_all | solution.py:86
  88.1 11.4 %all_to_all.107 = bf16[8,32,256]{2,1,0:T(8,128)(2,1)S(1)} all-to-all(bf16[8,32,256]{2,1,0:T(8,128)(2,1)S(1)} %bitcast.157), channel_id=1, replica_groups=mesh['x'=4,'core'=2,'y'=4,'z'=8] {'z'}, dimensions={0} | all-to-all | bytes 262144 | tf_op jit(solution)/shard_map/all_to_all | solution.py:91
  100.9 16.7 %all_to_all.108 = bf16[32,32,256]{2,1,0:T(8,128)(2,1)S(1)} all-to-all(bf16[32,32,256]{2,1,0:T(8,128)(2,1)S(1)} %bitcast.150), channel_id=1, replica_groups=mesh['x'=4,'core'=2,'y'=4,'z'=8] {'y','z'}, dimensions={0} | all-to-all | bytes 1048576 | tf_op jit(solution)/shard_map/all_to_all | solution.py:83
  117.7 12.5 %all_to_all.109 = bf16[8,32,256]{2,1,0:T(8,128)(2,1)S(1)} all-to-all(bf16[8,32,256]{2,1,0:T(8,128)(2,1)S(1)} %broadcast_in_dim.16), channel_id=1, replica_groups=mesh['x'=4,'core'=2,'y'=4,'z'=8] {'core','x'}, dimensions={0} | all-to-all | bytes 262144 | tf_op jit(solution)/shard_map/all_to_all | solution.py:86
  135.9 6.5 %all-to-all-done.8 = bf16[8,32,256]{2,1,0:T(8,128)(2,1)S(1)} async-done(((bf16[8,32,256]{2,1,0:T(8,128)(2,1)}), bf16[8,32,256]{2,1,0:T(8,128)(2,1)S(1)}, u32[]{:S(2)}, u32[]{:S(2)}) %all-to-all-start.8) | async-done | bytes 131104 | tf_op jit(solution)/shard_map/all_to_all | solution.py:91
  143.8 16.7 %all_to_all.110 = bf16[32,32,256]{2,1,0:T(8,128)(2,1)S(1)} all-to-all(bf16[32,32,256]{2,1,0:T(8,128)(2,1)S(1)} %bitcast.129), channel_id=1, replica_groups=mesh['x'=4,'core'=2,'y'=4,'z'=8] {'y','z'}, dimensions={0} | all-to-all | bytes 1048576 | tf_op jit(solution)/shard_map/all_to_all | solution.py:83
  160.6 12.5 %all_to_all.111 = bf16[8,32,256]{2,1,0:T(8,128)(2,1)S(1)} all-to-all(bf16[8,32,256]{2,1,0:T(8,128)(2,1)S(1)} %broadcast_in_dim.17), channel_id=1, replica_groups=mesh['x'=4,'core'=2,'y'=4,'z'=8] {'core','x'}, dimensions={0} | all-to-all | bytes 262144 | tf_op jit(solution)/shard_map/all_to_all | solution.py:86
  173.1 11.4 %all_to_all.112 = bf16[8,32,256]{2,1,0:T(8,128)(2,1)S(1)} all-to-all(bf16[8,32,256]{2,1,0:T(8,128)(2,1)S(1)} %bitcast.160), channel_id=1, replica_groups=mesh['x'=4,'core'=2,'y'=4,'z'=8] {'z'}, dimensions={0} | all-to-all | bytes 262144 | tf_op jit(solution)/shard_map/all_to_all | solution.py:91
  185.9 16.6 %all_to_all.113 = bf16[32,32,256]{2,1,0:T(8,128)(2,1)S(1)} all-to-all(bf16[32,32,256]{2,1,0:T(8,128)(2,1)S(1)} %bitcast.151), channel_id=1, replica_groups=mesh['x'=4,'core'=2,'y'=4,'z'=8] {'y','z'}, dimensions={0} | all-to-all | bytes 1048576 | tf_op jit(solution)/shard_map/all_to_all | solution.py:83
  203.2 8.3 %all-to-all-start.13 = ((bf16[8,32,256]{2,1,0:T(8,128)(2,1)}), bf16[8,32,256]{2,1,0:T(8,128)(2,1)S(1)}, u32[]{:S(2)}, u32[]{:S(2)}) async-start(bf16[8,32,256]{2,1,0:T(8,128)(2,1)} %broadcast_in_dim.18), calls=%async_computation.13 | async-start | bytes 262144 | tf_op jit(solution)/shard_map/all_to_all | solution.py:86
  222.5 6.5 %all-to-all-done.14 = bf16[8,32,256]{2,1,0:T(8,128)(2,1)S(1)} async-done(((bf16[8,32,256]{2,1,0:T(8,128)(2,1)}), bf16[8,32,256]{2,1,0:T(8,128)(2,1)S(1)}, u32[]{:S(2)}, u32[]{:S(2)}) %all-to-all-start.14) | async-done | bytes 131104 | tf_op jit(solution)/shard_map/all_to_all | solution.py:91
  230.3 16.7 %all_to_all.114 = bf16[32,32,256]{2,1,0:T(8,128)(2,1)S(1)} all-to-all(bf16[32,32,256]{2,1,0:T(8,128)(2,1)S(1)} %bitcast.130), channel_id=1, replica_groups=mesh['x'=4,'core'=2,'y'=4,'z'=8] {'y','z'}, dimensions={0} | all-to-all | bytes 1048576 | tf_op jit(solution)/shard_map/all_to_all | solution.py:83
  247.1 12.5 %all_to_all.115 = bf16[8,32,256]{2,1,0:T(8,128)(2,1)S(1)} all-to-all(bf16[8,32,256]{2,1,0:T(8,128)(2,1)S(1)} %broadcast_in_dim.19), channel_id=1, replica_groups=mesh['x'=4,'core'=2,'y'=4,'z'=8] {'core','x'}, dimensions={0} | all-to-all | bytes 262144 | tf_op jit(solution)/shard_map/all_to_all | solution.py:86
  259.6 11.4 %all_to_all.116 = bf16[8,32,256]{2,1,0:T(8,128)(2,1)S(1)} all-to-all(bf16[8,32,256]{2,1,0:T(8,128)(2,1)S(1)} %bitcast.162), channel_id=1, replica_groups=mesh['x'=4,'core'=2,'y'=4,'z'=8] {'z'}, dimensions={0} | all-to-all | bytes 262144 | tf_op jit(solution)/shard_map/all_to_all | solution.py:91
  272.4 16.7 %all_to_all.117 = bf16[32,32,256]{2,1,0:T(8,128)(2,1)S(1)} all-to-all(bf16[32,32,256]{2,1,0:T(8,128)(2,1)S(1)} %bitcast.152), channel_id=1, replica_groups=mesh['x'=4,'core'=2,'y'=4,'z'=8] {'y','z'}, dimensions={0} | all-to-all | bytes 1048576 | tf_op jit(solution)/shard_map/all_to_all | solution.py:83
  289.2 12.5 %all_to_all.118 = bf16[8,32,256]{2,1,0:T(8,128)(2,1)S(1)} all-to-all(bf16[8,32,256]{2,1,0:T(8,128)(2,1)S(1)} %broadcast_in_dim.20), channel_id=1, replica_groups=mesh['x'=4,'core'=2,'y'=4,'z'=8] {'core','x'}, dimensions={0} | all-to-all | bytes 262144 | tf_op jit(solution)/shard_map/all_to_all | solution.py:86
  301.7 11.4 %all_to_all.119 = bf16[8,32,256]{2,1,0:T(8,128)(2,1)S(1)} all-to-all(bf16[8,32,256]{2,1,0:T(8,128)(2,1)S(1)} %bitcast.164), channel_id=1, replica_groups=mesh['x'=4,'core'=2,'y'=4,'z'=8] {'z'}, dimensions={0} | all-to-all | bytes 262144 | tf_op jit(solution)/shard_map/all_to_all | solution.py:91
  (52 shorter events, 34.0 us)
Async XLA Ops:
  4.6 179.9 %copy-start = (bf16[4,1,256,256]{3,2,1,0:T(8,128)(2,1)S(1)}, bf16[4,1,256,256]{3,2,1,0:T(8,128)(2,1)}, u32[]{:S(2)}) copy-start(bf16[4,1,256,256]{3,2,1,0:T(8,128)(2,1)} %param.6) | copy-start | bytes 1572868
  4.6 26.5 %all-to-all-start = ((bf16[32,32,256]{2,1,0:T(8,128)(2,1)}), bf16[32,32,256]{2,1,0:T(8,128)(2,1)S(1)}, u32[]{:S(2)}, u32[]{:S(2)}) async-start(bf16[32,32,256]{2,1,0:T(8,128)(2,1)} %bitcast.6), calls=%async_computation | async-start | bytes 1048576 | tf_op jit(solution)/shard_map/all_to_all | solution.py:83
  31.8 13.0 %all-to-all-start.1 = ((bf16[8,32,256]{2,1,0:T(8,128)(2,1)}), bf16[8,32,256]{2,1,0:T(8,128)(2,1)S(1)}, u32[]{:S(2)}, u32[]{:S(2)}) async-start(bf16[8,32,256]{2,1,0:T(8,128)(2,1)} %broadcast_in_dim.14), calls=%async_computation.1 | async-start | bytes 262144 | tf_op jit(solution)/shard_map/all_to_all | solution.py:86
  45.4 12.0 %all-to-all-start.2 = ((bf16[8,32,256]{2,1,0:T(8,128)(2,1)}), bf16[8,32,256]{2,1,0:T(8,128)(2,1)S(1)}, u32[]{:S(2)}, u32[]{:S(2)}) async-start(bf16[8,32,256]{2,1,0:T(8,128)(2,1)} %bitcast.9), calls=%async_computation.2 | async-start | bytes 262144 | tf_op jit(solution)/shard_map/all_to_all | solution.py:91
  130.8 11.6 %all-to-all-start.8 = ((bf16[8,32,256]{2,1,0:T(8,128)(2,1)}), bf16[8,32,256]{2,1,0:T(8,128)(2,1)S(1)}, u32[]{:S(2)}, u32[]{:S(2)}) async-start(bf16[8,32,256]{2,1,0:T(8,128)(2,1)} %bitcast.27), calls=%async_computation.8 | async-start | bytes 262144 | tf_op jit(solution)/shard_map/all_to_all | solution.py:91
  203.2 13.5 %all-to-all-start.13 = ((bf16[8,32,256]{2,1,0:T(8,128)(2,1)}), bf16[8,32,256]{2,1,0:T(8,128)(2,1)S(1)}, u32[]{:S(2)}, u32[]{:S(2)}) async-start(bf16[8,32,256]{2,1,0:T(8,128)(2,1)} %broadcast_in_dim.18), calls=%async_computation.13 | async-start | bytes 262144 | tf_op jit(solution)/shard_map/all_to_all | solution.py:86
  217.4 11.6 %all-to-all-start.14 = ((bf16[8,32,256]{2,1,0:T(8,128)(2,1)}), bf16[8,32,256]{2,1,0:T(8,128)(2,1)S(1)}, u32[]{:S(2)}, u32[]{:S(2)}) async-start(bf16[8,32,256]{2,1,0:T(8,128)(2,1)} %bitcast.47), calls=%async_computation.14 | async-start | bytes 262144 | tf_op jit(solution)/shard_map/all_to_all | solution.py:91

commit v13 on v10

--- a/solution.py
+++ b/solution.py
@@ -92,6 +92,8 @@
         return arrived.reshape(block_size, rhs_width)
 
     rhs_width = columns_in.shape[2]
+    row_in_group = prow_index + prow_count * jnp.arange(level_rows, dtype=jnp.int32)
+    owns_row = (row_in_group == pcol_index).astype(jnp.float32)
     partial_levels = [None] * LEVELS
     solution = jnp.zeros((LEVELS, block_size, rhs_width), columns_in.dtype)
     for section_now in range(LEVELS):
@@ -100,8 +102,8 @@
         if section_now == 0:
             rhs_column = columns_in[0]
         else:
-            update = reduce_route(partial_levels[section_now]).astype(jnp.float32)
-            rhs_column = (columns_in[section_now].astype(jnp.float32) - update).astype(jnp.bfloat16)
+            own_b = columns_in[section_now].astype(jnp.float32)
+            rhs_column = reduce_route(owns_row[:, None, None] * own_b[None] - partial_levels[section_now])
         diag_terms = panel_products(
             column_tiles(first_row, section_now)[:level_rows],
             diag_bits[first_row:after_row, section_now],

time: 314 us -> 314 us (level)
  no operation moved by 1% of the time
where the time goes in v13:
time: 314 us; the launch traced here: 313 us
  blocking collectives  181 us (58%)
  starting transfers between devices  54.6 us (17%)
  waiting for transfers between devices  54.6 us (17%)
  matrix products  14.3 us (5%)
  other arithmetic  5.38 us (2%)
    all_to_all x6, blocking collectives, reduce_route(): got = lax.all_to_all(pieces, PCOL, 0, 0, tiled=True)  93.3 us
    all_to_all x4, blocking collectives, reduce_route(): gathered = lax.all_to_all(spread, PROW, 0, 0, tiled=True)  53.3 us
    all_to_all x3, blocking collectives, reduce_route(): arrived = lax.all_to_all(gathered, RING, 0, 0, tiled=True)  34.2 us
    all_to_all x4, waiting for transfers between devices, reduce_route(): arrived = lax.all_to_all(gathered, RING, 0, 0, tiled=True)  28.6 us
    all_to_all x3, starting transfers between devices, reduce_route(): gathered = lax.all_to_all(spread, PROW, 0, 0, tiled=True)  26.1 us
    all_to_all x4, starting transfers between devices, reduce_route(): arrived = lax.all_to_all(gathered, RING, 0, 0, tiled=True)  16.5 us
    dot_general x10, matrix products, panel_products(): jnp.einsum('nxy,yw->nxw', tile_stack, vector, preferred_element_type=jnp....  14.3 us
    all_to_all x3, waiting for transfers between devices, reduce_route(): gathered = lax.all_to_all(spread, PROW, 0, 0, tiled=True)  13.9 us
  transfers between devices with their start and end apart: 8, of which 8 were waited for; matrix products, arithmetic and copies ran while one was open for 2% of the time, Pallas kernels for 0%

profile of v13, /device:TPU:1, one launch (start us, length us, event | category | flops | bytes accessed | tf_op | source)
XLA Modules:
  0.0 312.6 jit_solution(5214910235986523786)
XLA Ops:
  3.7 12.0 %all-to-all-start = ((bf16[32,32,256]{2,1,0:T(8,128)(2,1)}), bf16[32,32,256]{2,1,0:T(8,128)(2,1)S(1)}, u32[]{:S(2)}, u32[]{:S(2)}) async-start(bf16[32,32,256]{2,1,0:T(8,128)(2,1)} %bitcast.6), calls=%async_computation | async-start | bytes 1048576 | tf_op jit(solution)/shard_map/all_to_all | solution.py:87
  18.0 12.1 %all-to-all-done = bf16[32,32,256]{2,1,0:T(8,128)(2,1)S(1)} async-done(((bf16[32,32,256]{2,1,0:T(8,128)(2,1)}), bf16[32,32,256]{2,1,0:T(8,128)(2,1)S(1)}, u32[]{:S(2)}, u32[]{:S(2)}) %all-to-all-start) | async-done | bytes 524320 | tf_op jit(solution)/shard_map/all_to_all | solution.py:87
  30.8 7.8 %all-to-all-start.1 = ((bf16[8,32,256]{2,1,0:T(8,128)(2,1)}), bf16[8,32,256]{2,1,0:T(8,128)(2,1)}, u32[]{:S(2)}, u32[]{:S(2)}) async-start(bf16[8,32,256]{2,1,0:T(8,128)(2,1)} %broadcast_in_dim.14), calls=%async_computation.1 | async-start | bytes 262144 | tf_op jit(solution)/shard_map/all_to_all | solution.py:90
  39.6 4.4 %all-to-all-done.1 = bf16[8,32,256]{2,1,0:T(8,128)(2,1)} async-done(((bf16[8,32,256]{2,1,0:T(8,128)(2,1)}), bf16[8,32,256]{2,1,0:T(8,128)(2,1)}, u32[]{:S(2)}, u32[]{:S(2)}) %all-to-all-start.1) | async-done | bytes 131104 | tf_op jit(solution)/shard_map/all_to_all | solution.py:90
  48.3 7.8 %all-to-all-done.2 = bf16[8,32,256]{2,1,0:T(8,128)(2,1)S(1)} async-done(((bf16[8,32,256]{2,1,0:T(8,128)(2,1)}), bf16[8,32,256]{2,1,0:T(8,128)(2,1)S(1)}, u32[]{:S(2)}, u32[]{:S(2)}) %all-to-all-start.2) | async-done | bytes 131104 | tf_op jit(solution)/shard_map/all_to_all | solution.py:91
  57.4 15.5 %all_to_all.105 = bf16[32,32,256]{2,1,0:T(8,128)(2,1)S(1)} all-to-all(bf16[32,32,256]{2,1,0:T(8,128)(2,1)S(1)} %bitcast.122), channel_id=1, replica_groups=mesh['x'=4,'core'=2,'y'=4,'z'=8] {'y','z'}, dimensions={0} | all-to-all | bytes 1048576 | tf_op jit(solution)/shard_map/all_to_all | solution.py:87
  73.0 13.2 %all_to_all.106 = bf16[8,32,256]{2,1,0:T(8,128)(2,1)S(1)} all-to-all(bf16[8,32,256]{2,1,0:T(8,128)(2,1)S(1)} %broadcast_in_dim.15), channel_id=1, replica_groups=mesh['x'=4,'core'=2,'y'=4,'z'=8] {'x','core'}, dimensions={0} | all-to-all | bytes 262144 | tf_op jit(solution)/shard_map/all_to_all | solution.py:90
  86.3 11.4 %all_to_all.107 = bf16[8,32,256]{2,1,0:T(8,128)(2,1)S(1)} all-to-all(bf16[8,32,256]{2,1,0:T(8,128)(2,1)S(1)} %all_to_all.106), channel_id=1, replica_groups=mesh['x'=4,'core'=2,'y'=4,'z'=8] {'z'}, dimensions={0} | all-to-all | bytes 262144 | tf_op jit(solution)/shard_map/all_to_all | solution.py:91
  99.0 15.5 %all_to_all.108 = bf16[32,32,256]{2,1,0:T(8,128)(2,1)S(1)} all-to-all(bf16[32,32,256]{2,1,0:T(8,128)(2,1)S(1)} %bitcast.123), channel_id=1, replica_groups=mesh['x'=4,'core'=2,'y'=4,'z'=8] {'y','z'}, dimensions={0} | all-to-all | bytes 1048576 | tf_op jit(solution)/shard_map/all_to_all | solution.py:87
  114.7 13.6 %all_to_all.109 = bf16[8,32,256]{2,1,0:T(8,128)(2,1)} all-to-all(bf16[8,32,256]{2,1,0:T(8,128)(2,1)S(1)} %broadcast_in_dim.16), channel_id=1, replica_groups=mesh['x'=4,'core'=2,'y'=4,'z'=8] {'x','core'}, dimensions={0} | all-to-all | bytes 262144 | tf_op jit(solution)/shard_map/all_to_all | solution.py:90
  133.7 6.5 %all-to-all-done.8 = bf16[8,32,256]{2,1,0:T(8,128)(2,1)S(1)} async-done(((bf16[8,32,256]{2,1,0:T(8,128)(2,1)}), bf16[8,32,256]{2,1,0:T(8,128)(2,1)S(1)}, u32[]{:S(2)}, u32[]{:S(2)}) %all-to-all-start.8) | async-done | bytes 131104 | tf_op jit(solution)/shard_map/all_to_all | solution.py:91
  141.6 15.6 %all_to_all.110 = bf16[32,32,256]{2,1,0:T(8,128)(2,1)S(1)} all-to-all(bf16[32,32,256]{2,1,0:T(8,128)(2,1)S(1)} %bitcast.109), channel_id=1, replica_groups=mesh['x'=4,'core'=2,'y'=4,'z'=8] {'y','z'}, dimensions={0} | all-to-all | bytes 1048576 | tf_op jit(solution)/shard_map/all_to_all | solution.py:87
  157.3 13.2 %all_to_all.111 = bf16[8,32,256]{2,1,0:T(8,128)(2,1)S(1)} all-to-all(bf16[8,32,256]{2,1,0:T(8,128)(2,1)S(1)} %broadcast_in_dim.17), channel_id=1, replica_groups=mesh['x'=4,'core'=2,'y'=4,'z'=8] {'x','core'}, dimensions={0} | all-to-all | bytes 262144 | tf_op jit(solution)/shard_map/all_to_all | solution.py:90
  170.5 11.4 %all_to_all.112 = bf16[8,32,256]{2,1,0:T(8,128)(2,1)S(1)} all-to-all(bf16[8,32,256]{2,1,0:T(8,128)(2,1)S(1)} %all_to_all.111), channel_id=1, replica_groups=mesh['x'=4,'core'=2,'y'=4,'z'=8] {'z'}, dimensions={0} | all-to-all | bytes 262144 | tf_op jit(solution)/shard_map/all_to_all | solution.py:91
  183.3 15.5 %all_to_all.113 = bf16[32,32,256]{2,1,0:T(8,128)(2,1)S(1)} all-to-all(bf16[32,32,256]{2,1,0:T(8,128)(2,1)S(1)} %bitcast.124), channel_id=1, replica_groups=mesh['x'=4,'core'=2,'y'=4,'z'=8] {'y','z'}, dimensions={0} | all-to-all | bytes 1048576 | tf_op jit(solution)/shard_map/all_to_all | solution.py:87
  199.6 9.1 %all-to-all-start.13 = ((bf16[8,32,256]{2,1,0:T(8,128)(2,1)}), bf16[8,32,256]{2,1,0:T(8,128)(2,1)}, u32[]{:S(2)}, u32[]{:S(2)}) async-start(bf16[8,32,256]{2,1,0:T(8,128)(2,1)} %broadcast_in_dim.18), calls=%async_computation.13 | async-start | bytes 262144 | tf_op jit(solution)/shard_map/all_to_all | solution.py:90
  219.6 6.5 %all-to-all-done.14 = bf16[8,32,256]{2,1,0:T(8,128)(2,1)S(1)} async-done(((bf16[8,32,256]{2,1,0:T(8,128)(2,1)}), bf16[8,32,256]{2,1,0:T(8,128)(2,1)S(1)}, u32[]{:S(2)}, u32[]{:S(2)}) %all-to-all-start.14) | async-done | bytes 131104 | tf_op jit(solution)/shard_map/all_to_all | solution.py:91
  227.5 15.5 %all_to_all.114 = bf16[32,32,256]{2,1,0:T(8,128)(2,1)S(1)} all-to-all(bf16[32,32,256]{2,1,0:T(8,128)(2,1)S(1)} %bitcast.108), channel_id=1, replica_groups=mesh['x'=4,'core'=2,'y'=4,'z'=8] {'y','z'}, dimensions={0} | all-to-all | bytes 1048576 | tf_op jit(solution)/shard_map/all_to_all | solution.py:87
  243.1 13.3 %all_to_all.115 = bf16[8,32,256]{2,1,0:T(8,128)(2,1)S(1)} all-to-all(bf16[8,32,256]{2,1,0:T(8,128)(2,1)S(1)} %broadcast_in_dim.19), channel_id=1, replica_groups=mesh['x'=4,'core'=2,'y'=4,'z'=8] {'x','core'}, dimensions={0} | all-to-all | bytes 262144 | tf_op jit(solution)/shard_map/all_to_all | solution.py:90
  256.4 11.4 %all_to_all.116 = bf16[8,32,256]{2,1,0:T(8,128)(2,1)S(1)} all-to-all(bf16[8,32,256]{2,1,0:T(8,128)(2,1)S(1)} %all_to_all.115), channel_id=1, replica_groups=mesh['x'=4,'core'=2,'y'=4,'z'=8] {'z'}, dimensions={0} | all-to-all | bytes 262144 | tf_op jit(solution)/shard_map/all_to_all | solution.py:91
  269.1 15.5 %all_to_all.117 = bf16[32,32,256]{2,1,0:T(8,128)(2,1)S(1)} all-to-all(bf16[32,32,256]{2,1,0:T(8,128)(2,1)S(1)} %bitcast.125), channel_id=1, replica_groups=mesh['x'=4,'core'=2,'y'=4,'z'=8] {'y','z'}, dimensions={0} | all-to-all | bytes 1048576 | tf_op jit(solution)/shard_map/all_to_all | solution.py:87
  285.4 9.1 %all-to-all-start.19 = ((bf16[8,32,256]{2,1,0:T(8,128)(2,1)}), bf16[8,32,256]{2,1,0:T(8,128)(2,1)}, u32[]{:S(2)}, u32[]{:S(2)}) async-start(bf16[8,32,256]{2,1,0:T(8,128)(2,1)} %broadcast_in_dim.20), calls=%async_computation.19 | async-start | bytes 262144 | tf_op jit(solution)/shard_map/all_to_all | solution.py:90
  294.6 5.4 %all-to-all-done.19 = bf16[8,32,256]{2,1,0:T(8,128)(2,1)} async-done(((bf16[8,32,256]{2,1,0:T(8,128)(2,1)}), bf16[8,32,256]{2,1,0:T(8,128)(2,1)}, u32[]{:S(2)}, u32[]{:S(2)}) %all-to-all-start.19) | async-done | bytes 131104 | tf_op jit(solution)/shard_map/all_to_all | solution.py:90
  304.1 7.8 %all-to-all-done.20 = bf16[8,32,256]{2,1,0:T(8,128)(2,1)S(1)} async-done(((bf16[8,32,256]{2,1,0:T(8,128)(2,1)}), bf16[8,32,256]{2,1,0:T(8,128)(2,1)S(1)}, u32[]{:S(2)}, u32[]{:S(2)}) %all-to-all-start.20) | async-done | bytes 131104 | tf_op jit(solution)/shard_map/all_to_all | solution.py:91
  (53 shorter events, 43.0 us)
Async XLA Ops:
  3.7 26.4 %all-to-all-start = ((bf16[32,32,256]{2,1,0:T(8,128)(2,1)}), bf16[32,32,256]{2,1,0:T(8,128)(2,1)S(1)}, u32[]{:S(2)}, u32[]{:S(2)}) async-start(bf16[32,32,256]{2,1,0:T(8,128)(2,1)} %bitcast.6), calls=%async_computation | async-start | bytes 1048576 | tf_op jit(solution)/shard_map/all_to_all | solution.py:87
  30.8 13.2 %all-to-all-start.1 = ((bf16[8,32,256]{2,1,0:T(8,128)(2,1)}), bf16[8,32,256]{2,1,0:T(8,128)(2,1)}, u32[]{:S(2)}, u32[]{:S(2)}) async-start(bf16[8,32,256]{2,1,0:T(8,128)(2,1)} %broadcast_in_dim.14), calls=%async_computation.1 | async-start | bytes 262144 | tf_op jit(solution)/shard_map/all_to_all | solution.py:90
  44.0 12.0 %all-to-all-start.2 = ((bf16[8,32,256]{2,1,0:T(8,128)(2,1)}), bf16[8,32,256]{2,1,0:T(8,128)(2,1)S(1)}, u32[]{:S(2)}, u32[]{:S(2)}) async-start(bf16[8,32,256]{2,1,0:T(8,128)(2,1)} %all-to-all-done.1), calls=%async_computation.2 | async-start | bytes 262144 | tf_op jit(solution)/shard_map/all_to_all | solution.py:91
  128.3 12.0 %all-to-all-start.8 = ((bf16[8,32,256]{2,1,0:T(8,128)(2,1)}), bf16[8,32,256]{2,1,0:T(8,128)(2,1)S(1)}, u32[]{:S(2)}, u32[]{:S(2)}) async-start(bf16[8,32,256]{2,1,0:T(8,128)(2,1)} %all_to_all.109), calls=%async_computation.8 | async-start | bytes 262144 | tf_op jit(solution)/shard_map/all_to_all | solution.py:91
  199.6 14.5 %all-to-all-start.13 = ((bf16[8,32,256]{2,1,0:T(8,128)(2,1)}), bf16[8,32,256]{2,1,0:T(8,128)(2,1)}, u32[]{:S(2)}, u32[]{:S(2)}) async-start(bf16[8,32,256]{2,1,0:T(8,128)(2,1)} %broadcast_in_dim.18), calls=%async_computation.13 | async-start | bytes 262144 | tf_op jit(solution)/shard_map/all_to_all | solution.py:90
  214.1 12.0 %all-to-all-start.14 = ((bf16[8,32,256]{2,1,0:T(8,128)(2,1)}), bf16[8,32,256]{2,1,0:T(8,128)(2,1)S(1)}, u32[]{:S(2)}, u32[]{:S(2)}) async-start(bf16[8,32,256]{2,1,0:T(8,128)(2,1)} %all-to-all-done.13), calls=%async_computation.14 | async-start | bytes 262144 | tf_op jit(solution)/shard_map/all_to_all | solution.py:91
  285.4 14.5 %all-to-all-start.19 = ((bf16[8,32,256]{2,1,0:T(8,128)(2,1)}), bf16[8,32,256]{2,1,0:T(8,128)(2,1)}, u32[]{:S(2)}, u32[]{:S(2)}) async-start(bf16[8,32,256]{2,1,0:T(8,128)(2,1)} %broadcast_in_dim.20), calls=%async_computation.19 | async-start | bytes 262144 | tf_op jit(solution)/shard_map/all_to_all | solution.py:90
  300.0 12.0 %all-to-all-start.20 = ((bf16[8,32,256]{2,1,0:T(8,128)(2,1)}), bf16[8,32,256]{2,1,0:T(8,128)(2,1)S(1)}, u32[]{:S(2)}, u32[]{:S(2)}) async-start(bf16[8,32,256]{2,1,0:T(8,128)(2,1)} %all-to-all-done.19), calls=%async_computation.20 | async-start | bytes 262144 | tf_op jit(solution)/shard_map/all_to_all | solution.py:91
  304.1 7.8 %copy-start = (bf16[4,1,256,256]{3,2,1,0:T(8,128)(2,1)}, bf16[4,1,256,256]{3,2,1,0:T(8,128)(2,1)S(1)}, u32[]{:S(2)}) copy-start(bf16[4,1,256,256]{3,2,1,0:T(8,128)(2,1)S(1)} %constant_dynamic-update-slice_fusion.1) | copy-start | bytes 1572868

commit v14 on v9

--- a/solution.py
+++ b/solution.py
@@ -77,11 +77,14 @@
         (row_nodes[:, None] == col_nodes[None, :]) & (row_ids[:, None] >= col_ids[None, :])
     ).astype(jnp.int32)
 
-    def reduce_route(level_terms):
+    def reduce_route(level_terms, source_bits=None):
         rhs_width = level_terms.shape[2]
         pieces = level_terms.astype(jnp.bfloat16).reshape(pcol_count, chunk_rows, rhs_width)
         got = lax.all_to_all(pieces, PCOL, 0, 0, tiled=True)
-        summed = jnp.sum(got.astype(jnp.float32), axis=0).astype(jnp.bfloat16)
+        got = got.astype(jnp.float32)
+        if source_bits is not None:
+            got = got * source_bits[:, None, None]
+        summed = jnp.sum(got, axis=0).astype(jnp.bfloat16)
         spread = jnp.broadcast_to(summed[None], (prow_count,) + summed.shape)
         gathered = lax.all_to_all(spread, PROW, 0, 0, tiled=True)
         arrived = lax.all_to_all(gathered, RING, 0, 0, tiled=True)
@@ -98,12 +101,23 @@
         else:
             update = reduce_route(partial_levels[section_now]).astype(jnp.float32)
             rhs_column = (columns_in[section_now].astype(jnp.float32) - update).astype(jnp.bfloat16)
-        diag_terms = panel_products(
-            column_tiles(first_row, section_now)[:level_rows],
-            diag_bits[first_row:after_row, section_now],
-            rhs_column,
-        )
-        solved = reduce_route(diag_terms)
+        if section_now == 0:
+            diag_terms = jnp.einsum(
+                "nxy,yw->nxw", column_tiles(0, 0)[:level_rows], rhs_column, preferred_element_type=jnp.float32
+            )
+            piece_row = prow_index + prow_count * (pcol_index // ring)
+            sender_cols = jnp.arange(pcol_count, dtype=jnp.int32)
+            piece_node = lookup(block_node, piece_row[None])
+            sender_nodes = lookup(block_node, sender_cols)
+            sender_bits = ((sender_nodes == piece_node) & (sender_cols <= piece_row)).astype(jnp.float32)
+            solved = reduce_route(diag_terms, sender_bits)
+        else:
+            diag_terms = panel_products(
+                column_tiles(first_row, section_now)[:level_rows],
+                diag_bits[first_row:after_row, section_now],
+                rhs_column,
+            )
+            solved = reduce_route(diag_terms)
         solved_list.append(solved)
         for later in range(section_now + 1, LEVELS):
             later_row = later * level_rows

time: 313 us -> 313 us (level)
  blocking collectives: 206 us -> 181 us
  starting transfers between devices: 41.3 us -> 54.6 us
  waiting for transfers between devices: 43.5 us -> 52.8 us
    all_to_all x5 -> x4, blocking collectives: 66.6 us -> 53.3 us  [reduce_route(): gathered = lax.all_to_all(spread, PROW, 0, 0, tiled=True)]
    all_to_all x4 -> x3, blocking collectives: 45.7 us -> 34.2 us  [reduce_route(): arrived = lax.all_to_all(gathered, RING, 0, 0, tiled=True)]
    all_to_all x2 -> x3, starting transfers between devices: 16.9 us -> 26 us  [reduce_route(): gathered = lax.all_to_all(spread, PROW, 0, 0, tiled=True)]
    all_to_all x3 -> x4, waiting for transfers between devices: 20.6 us -> 28.3 us  [reduce_route(): arrived = lax.all_to_all(gathered, RING, 0, 0, tiled=True)]
    all_to_all x2 -> x3, waiting for transfers between devices: 8.64 us -> 13.9 us  [reduce_route(): gathered = lax.all_to_all(spread, PROW, 0, 0, tiled=True)]
    all_to_all x3 -> x4, starting transfers between devices: 12.4 us -> 16.5 us  [reduce_route(): arrived = lax.all_to_all(gathered, RING, 0, 0, tiled=True)]
    all_to_all x1, waiting for transfers between devices: 14.2 us -> 10.6 us  [reduce_route(): got = lax.all_to_all(pieces, PCOL, 0, 0, tiled=True)]
    dot_general x10 -> x9, matrix products: 14.4 us -> 12.2 us  [panel_products(): jnp.einsum('nxy,yw->nxw', tile_stack, vector, preferred_element_type=jnp....]
  transfers between devices with their start and end apart: 6 -> 8, of which waited for: 6 -> 8; matrix products, arithmetic and copies ran while one was open for 2% -> 3% of each run, Pallas kernels for 0% -> 0%
where the time goes in v14:
time: 313 us; the launch traced here: 311 us
  blocking collectives  181 us (58%)
  starting transfers between devices  54.6 us (17%)
  waiting for transfers between devices  52.8 us (17%)
  matrix products  14.4 us (5%)
  other arithmetic  6.56 us (2%)
    all_to_all x6, blocking collectives, reduce_route(): got = lax.all_to_all(pieces, PCOL, 0, 0, tiled=True)  93.3 us
    all_to_all x4, blocking collectives, reduce_route(): gathered = lax.all_to_all(spread, PROW, 0, 0, tiled=True)  53.3 us
    all_to_all x3, blocking collectives, reduce_route(): arrived = lax.all_to_all(gathered, RING, 0, 0, tiled=True)  34.2 us
    all_to_all x4, waiting for transfers between devices, reduce_route(): arrived = lax.all_to_all(gathered, RING, 0, 0, tiled=True)  28.3 us
    all_to_all x3, starting transfers between devices, reduce_route(): gathered = lax.all_to_all(spread, PROW, 0, 0, tiled=True)  26 us
    all_to_all x4, starting transfers between devices, reduce_route(): arrived = lax.all_to_all(gathered, RING, 0, 0, tiled=True)  16.5 us
    all_to_all x3, waiting for transfers between devices, reduce_route(): gathered = lax.all_to_all(spread, PROW, 0, 0, tiled=True)  13.9 us
    dot_general x9, matrix products, panel_products(): jnp.einsum('nxy,yw->nxw', tile_stack, vector, preferred_element_type=jnp....  12.2 us
  transfers between devices with their start and end apart: 8, of which 8 were waited for; matrix products, arithmetic and copies ran while one was open for 3% of the time, Pallas kernels for 0%

profile of v14, /device:TPU:1, one launch (start us, length us, event | category | flops | bytes accessed | tf_op | source)
XLA Modules:
  0.0 311.4 jit_solution(537308293432025421)
XLA Ops:
  2.2 12.0 %all-to-all-start = ((bf16[32,32,256]{2,1,0:T(8,128)(2,1)}), bf16[32,32,256]{2,1,0:T(8,128)(2,1)S(1)}, u32[]{:S(2)}, u32[]{:S(2)}) async-start(bf16[32,32,256]{2,1,0:T(8,128)(2,1)} %bitcast.3), calls=%async_computation | async-start | bytes 1048576 | tf_op jit(solution)/shard_map/all_to_all | solution.py:83
  18.0 10.6 %all-to-all-done = bf16[32,32,256]{2,1,0:T(8,128)(2,1)S(1)} async-done(((bf16[32,32,256]{2,1,0:T(8,128)(2,1)}), bf16[32,32,256]{2,1,0:T(8,128)(2,1)S(1)}, u32[]{:S(2)}, u32[]{:S(2)}) %all-to-all-start) | async-done | bytes 524320 | tf_op jit(solution)/shard_map/all_to_all | solution.py:83
  29.4 7.8 %all-to-all-start.1 = ((bf16[8,32,256]{2,1,0:T(8,128)(2,1)}), bf16[8,32,256]{2,1,0:T(8,128)(2,1)}, u32[]{:S(2)}, u32[]{:S(2)}) async-start(bf16[8,32,256]{2,1,0:T(8,128)(2,1)} %broadcast_in_dim.14), calls=%async_computation.1 | async-start | bytes 262144 | tf_op jit(solution)/shard_map/all_to_all | solution.py:89
  38.0 4.6 %all-to-all-done.1 = bf16[8,32,256]{2,1,0:T(8,128)(2,1)} async-done(((bf16[8,32,256]{2,1,0:T(8,128)(2,1)}), bf16[8,32,256]{2,1,0:T(8,128)(2,1)}, u32[]{:S(2)}, u32[]{:S(2)}) %all-to-all-start.1) | async-done | bytes 131104 | tf_op jit(solution)/shard_map/all_to_all | solution.py:89
  46.9 7.6 %all-to-all-done.2 = bf16[8,32,256]{2,1,0:T(8,128)(2,1)S(1)} async-done(((bf16[8,32,256]{2,1,0:T(8,128)(2,1)}), bf16[8,32,256]{2,1,0:T(8,128)(2,1)S(1)}, u32[]{:S(2)}, u32[]{:S(2)}) %all-to-all-start.2) | async-done | bytes 131104 | tf_op jit(solution)/shard_map/all_to_all | solution.py:90
  55.9 15.6 %all_to_all.105 = bf16[32,32,256]{2,1,0:T(8,128)(2,1)S(1)} all-to-all(bf16[32,32,256]{2,1,0:T(8,128)(2,1)S(1)} %bitcast.123), channel_id=1, replica_groups=mesh['x'=4,'core'=2,'y'=4,'z'=8] {'y','z'}, dimensions={0} | all-to-all | bytes 1048576 | tf_op jit(solution)/shard_map/all_to_all | solution.py:83
  72.2 9.1 %all-to-all-start.4 = ((bf16[8,32,256]{2,1,0:T(8,128)(2,1)}), bf16[8,32,256]{2,1,0:T(8,128)(2,1)}, u32[]{:S(2)}, u32[]{:S(2)}) async-start(bf16[8,32,256]{2,1,0:T(8,128)(2,1)} %broadcast_in_dim.15), calls=%async_computation.4 | async-start | bytes 262144 | tf_op jit(solution)/shard_map/all_to_all | solution.py:89
  81.5 5.2 %all-to-all-done.4 = bf16[8,32,256]{2,1,0:T(8,128)(2,1)} async-done(((bf16[8,32,256]{2,1,0:T(8,128)(2,1)}), bf16[8,32,256]{2,1,0:T(8,128)(2,1)}, u32[]{:S(2)}, u32[]{:S(2)}) %all-to-all-start.4) | async-done | bytes 131104 | tf_op jit(solution)/shard_map/all_to_all | solution.py:89
  91.0 7.7 %all-to-all-done.5 = bf16[8,32,256]{2,1,0:T(8,128)(2,1)S(1)} async-done(((bf16[8,32,256]{2,1,0:T(8,128)(2,1)}), bf16[8,32,256]{2,1,0:T(8,128)(2,1)S(1)}, u32[]{:S(2)}, u32[]{:S(2)}) %all-to-all-start.5) | async-done | bytes 131104 | tf_op jit(solution)/shard_map/all_to_all | solution.py:90
  100.1 15.5 %all_to_all.106 = bf16[32,32,256]{2,1,0:T(8,128)(2,1)S(1)} all-to-all(bf16[32,32,256]{2,1,0:T(8,128)(2,1)S(1)} %bitcast.120), channel_id=1, replica_groups=mesh['x'=4,'core'=2,'y'=4,'z'=8] {'y','z'}, dimensions={0} | all-to-all | bytes 1048576 | tf_op jit(solution)/shard_map/all_to_all | solution.py:83
  115.8 13.6 %all_to_all.107 = bf16[8,32,256]{2,1,0:T(8,128)(2,1)} all-to-all(bf16[8,32,256]{2,1,0:T(8,128)(2,1)S(1)} %broadcast_in_dim.16), channel_id=1, replica_groups=mesh['x'=4,'core'=2,'y'=4,'z'=8] {'x','core'}, dimensions={0} | all-to-all | bytes 262144 | tf_op jit(solution)/shard_map/all_to_all | solution.py:89
  134.8 6.5 %all-to-all-done.8 = bf16[8,32,256]{2,1,0:T(8,128)(2,1)S(1)} async-done(((bf16[8,32,256]{2,1,0:T(8,128)(2,1)}), bf16[8,32,256]{2,1,0:T(8,128)(2,1)S(1)}, u32[]{:S(2)}, u32[]{:S(2)}) %all-to-all-start.8) | async-done | bytes 131104 | tf_op jit(solution)/shard_map/all_to_all | solution.py:90
  142.7 15.6 %all_to_all.108 = bf16[32,32,256]{2,1,0:T(8,128)(2,1)S(1)} all-to-all(bf16[32,32,256]{2,1,0:T(8,128)(2,1)S(1)} %bitcast.99), channel_id=1, replica_groups=mesh['x'=4,'core'=2,'y'=4,'z'=8] {'y','z'}, dimensions={0} | all-to-all | bytes 1048576 | tf_op jit(solution)/shard_map/all_to_all | solution.py:83
  158.4 13.2 %all_to_all.109 = bf16[8,32,256]{2,1,0:T(8,128)(2,1)S(1)} all-to-all(bf16[8,32,256]{2,1,0:T(8,128)(2,1)S(1)} %broadcast_in_dim.17), channel_id=1, replica_groups=mesh['x'=4,'core'=2,'y'=4,'z'=8] {'x','core'}, dimensions={0} | all-to-all | bytes 262144 | tf_op jit(solution)/shard_map/all_to_all | solution.py:89
  171.6 11.4 %all_to_all.110 = bf16[8,32,256]{2,1,0:T(8,128)(2,1)S(1)} all-to-all(bf16[8,32,256]{2,1,0:T(8,128)(2,1)S(1)} %all_to_all.109), channel_id=1, replica_groups=mesh['x'=4,'core'=2,'y'=4,'z'=8] {'z'}, dimensions={0} | all-to-all | bytes 262144 | tf_op jit(solution)/shard_map/all_to_all | solution.py:90
  184.4 15.5 %all_to_all.111 = bf16[32,32,256]{2,1,0:T(8,128)(2,1)S(1)} all-to-all(bf16[32,32,256]{2,1,0:T(8,128)(2,1)S(1)} %bitcast.121), channel_id=1, replica_groups=mesh['x'=4,'core'=2,'y'=4,'z'=8] {'y','z'}, dimensions={0} | all-to-all | bytes 1048576 | tf_op jit(solution)/shard_map/all_to_all | solution.py:83
  200.7 9.1 %all-to-all-start.13 = ((bf16[8,32,256]{2,1,0:T(8,128)(2,1)}), bf16[8,32,256]{2,1,0:T(8,128)(2,1)}, u32[]{:S(2)}, u32[]{:S(2)}) async-start(bf16[8,32,256]{2,1,0:T(8,128)(2,1)} %broadcast_in_dim.18), calls=%async_computation.13 | async-start | bytes 262144 | tf_op jit(solution)/shard_map/all_to_all | solution.py:89
  220.7 6.5 %all-to-all-done.14 = bf16[8,32,256]{2,1,0:T(8,128)(2,1)S(1)} async-done(((bf16[8,32,256]{2,1,0:T(8,128)(2,1)}), bf16[8,32,256]{2,1,0:T(8,128)(2,1)S(1)}, u32[]{:S(2)}, u32[]{:S(2)}) %all-to-all-start.14) | async-done | bytes 131104 | tf_op jit(solution)/shard_map/all_to_all | solution.py:90
  228.5 15.5 %all_to_all.112 = bf16[32,32,256]{2,1,0:T(8,128)(2,1)S(1)} all-to-all(bf16[32,32,256]{2,1,0:T(8,128)(2,1)S(1)} %bitcast.100), channel_id=1, replica_groups=mesh['x'=4,'core'=2,'y'=4,'z'=8] {'y','z'}, dimensions={0} | all-to-all | bytes 1048576 | tf_op jit(solution)/shard_map/all_to_all | solution.py:83
  244.2 13.3 %all_to_all.113 = bf16[8,32,256]{2,1,0:T(8,128)(2,1)S(1)} all-to-all(bf16[8,32,256]{2,1,0:T(8,128)(2,1)S(1)} %broadcast_in_dim.19), channel_id=1, replica_groups=mesh['x'=4,'core'=2,'y'=4,'z'=8] {'x','core'}, dimensions={0} | all-to-all | bytes 262144 | tf_op jit(solution)/shard_map/all_to_all | solution.py:89
  257.4 11.4 %all_to_all.114 = bf16[8,32,256]{2,1,0:T(8,128)(2,1)S(1)} all-to-all(bf16[8,32,256]{2,1,0:T(8,128)(2,1)S(1)} %all_to_all.113), channel_id=1, replica_groups=mesh['x'=4,'core'=2,'y'=4,'z'=8] {'z'}, dimensions={0} | all-to-all | bytes 262144 | tf_op jit(solution)/shard_map/all_to_all | solution.py:90
  270.2 15.5 %all_to_all.115 = bf16[32,32,256]{2,1,0:T(8,128)(2,1)S(1)} all-to-all(bf16[32,32,256]{2,1,0:T(8,128)(2,1)S(1)} %bitcast.122), channel_id=1, replica_groups=mesh['x'=4,'core'=2,'y'=4,'z'=8] {'y','z'}, dimensions={0} | all-to-all | bytes 1048576 | tf_op jit(solution)/shard_map/all_to_all | solution.py:83
  285.8 13.3 %all_to_all.116 = bf16[8,32,256]{2,1,0:T(8,128)(2,1)S(1)} all-to-all(bf16[8,32,256]{2,1,0:T(8,128)(2,1)S(1)} %broadcast_in_dim.20), channel_id=1, replica_groups=mesh['x'=4,'core'=2,'y'=4,'z'=8] {'x','core'}, dimensions={0} | all-to-all | bytes 262144 | tf_op jit(solution)/shard_map/all_to_all | solution.py:89
  299.1 11.4 %all_to_all.117 = bf16[8,32,256]{2,1,0:T(8,128)(2,1)S(1)} all-to-all(bf16[8,32,256]{2,1,0:T(8,128)(2,1)S(1)} %all_to_all.116), channel_id=1, replica_groups=mesh['x'=4,'core'=2,'y'=4,'z'=8] {'z'}, dimensions={0} | all-to-all | bytes 262144 | tf_op jit(solution)/shard_map/all_to_all | solution.py:90
  (50 shorter events, 43.5 us)
Async XLA Ops:
  0.0 183.0 %copy-start = (bf16[4,1,256,256]{3,2,1,0:T(8,128)(2,1)S(1)}, bf16[4,1,256,256]{3,2,1,0:T(8,128)(2,1)}, u32[]{:S(2)}) copy-start(bf16[4,1,256,256]{3,2,1,0:T(8,128)(2,1)} %param.6) | copy-start | bytes 1572868
  2.2 26.4 %all-to-all-start = ((bf16[32,32,256]{2,1,0:T(8,128)(2,1)}), bf16[32,32,256]{2,1,0:T(8,128)(2,1)S(1)}, u32[]{:S(2)}, u32[]{:S(2)}) async-start(bf16[32,32,256]{2,1,0:T(8,128)(2,1)} %bitcast.3), calls=%async_computation | async-start | bytes 1048576 | tf_op jit(solution)/shard_map/all_to_all | solution.py:83
  29.4 13.2 %all-to-all-start.1 = ((bf16[8,32,256]{2,1,0:T(8,128)(2,1)}), bf16[8,32,256]{2,1,0:T(8,128)(2,1)}, u32[]{:S(2)}, u32[]{:S(2)}) async-start(bf16[8,32,256]{2,1,0:T(8,128)(2,1)} %broadcast_in_dim.14), calls=%async_computation.1 | async-start | bytes 262144 | tf_op jit(solution)/shard_map/all_to_all | solution.py:89
  42.6 12.0 %all-to-all-start.2 = ((bf16[8,32,256]{2,1,0:T(8,128)(2,1)}), bf16[8,32,256]{2,1,0:T(8,128)(2,1)S(1)}, u32[]{:S(2)}, u32[]{:S(2)}) async-start(bf16[8,32,256]{2,1,0:T(8,128)(2,1)} %all-to-all-done.1), calls=%async_computation.2 | async-start | bytes 262144 | tf_op jit(solution)/shard_map/all_to_all | solution.py:90
  72.2 14.5 %all-to-all-start.4 = ((bf16[8,32,256]{2,1,0:T(8,128)(2,1)}), bf16[8,32,256]{2,1,0:T(8,128)(2,1)}, u32[]{:S(2)}, u32[]{:S(2)}) async-start(bf16[8,32,256]{2,1,0:T(8,128)(2,1)} %broadcast_in_dim.15), calls=%async_computation.4 | async-start | bytes 262144 | tf_op jit(solution)/shard_map/all_to_all | solution.py:89
  86.7 12.0 %all-to-all-start.5 = ((bf16[8,32,256]{2,1,0:T(8,128)(2,1)}), bf16[8,32,256]{2,1,0:T(8,128)(2,1)S(1)}, u32[]{:S(2)}, u32[]{:S(2)}) async-start(bf16[8,32,256]{2,1,0:T(8,128)(2,1)} %all-to-all-done.4), calls=%async_computation.5 | async-start | bytes 262144 | tf_op jit(solution)/shard_map/all_to_all | solution.py:90
  129.4 12.0 %all-to-all-start.8 = ((bf16[8,32,256]{2,1,0:T(8,128)(2,1)}), bf16[8,32,256]{2,1,0:T(8,128)(2,1)S(1)}, u32[]{:S(2)}, u32[]{:S(2)}) async-start(bf16[8,32,256]{2,1,0:T(8,128)(2,1)} %all_to_all.107), calls=%async_computation.8 | async-start | bytes 262144 | tf_op jit(solution)/shard_map/all_to_all | solution.py:90
  200.7 14.5 %all-to-all-start.13 = ((bf16[8,32,256]{2,1,0:T(8,128)(2,1)}), bf16[8,32,256]{2,1,0:T(8,128)(2,1)}, u32[]{:S(2)}, u32[]{:S(2)}) async-start(bf16[8,32,256]{2,1,0:T(8,128)(2,1)} %broadcast_in_dim.18), calls=%async_computation.13 | async-start | bytes 262144 | tf_op jit(solution)/shard_map/all_to_all | solution.py:89
  215.2 12.0 %all-to-all-start.14 = ((bf16[8,32,256]{2,1,0:T(8,128)(2,1)}), bf16[8,32,256]{2,1,0:T(8,128)(2,1)S(1)}, u32[]{:S(2)}, u32[]{:S(2)}) async-start(bf16[8,32,256]{2,1,0:T(8,128)(2,1)} %all-to-all-done.13), calls=%async_computation.14 | async-start | bytes 262144 | tf_op jit(solution)/shard_map/all_to_all | solution.py:90
